TPU v7x, 1024 devices: a whole 4x8x16 slice. The times are simulated.
1024 devices in a mesh: ctx: 64 (over z, x), head: 8 (over y), dp: 2 (over core).
Axes of the slice: x: 4, y: 8, z: 16, core: 2. Of those that a mesh axis runs over, the one named last changes fastest.
Arguments:
- ssd_grad: bfloat16 [2, 8192, 8192], P('dp', 'ctx', 'head'), may hold values from -6 to 6
- ssd_input: bfloat16 [2, 8192, 8192], P('dp', 'ctx', 'head'), may hold values from -0.75 to 0.75
- state_write: bfloat16 [2, 8192, 1024], P('dp', 'ctx', 'head'), may hold values from -0.4375 to 0.4375
- state_read: bfloat16 [2, 8192, 1024], P('dp', 'ctx', 'head'), may hold values from -0.4375 to 0.4375
- log_decay: float32 [2, 128, 8192], P('dp', 'head', 'ctx'), may hold values from -2 to 0
Outputs:
- input_grad: bfloat16 [2, 8192, 8192], P('dp', 'ctx', 'head')
- write_grad: bfloat16 [2, 8192, 1024], P('dp', 'ctx', 'head')
- read_grad: bfloat16 [2, 8192, 1024], P('dp', 'ctx', 'head')
All inputs are finite; a program needn't handle non-finite values.
Results may differ from a plain program's by a relative error of at most 0.0065.
Values sent between devices are 32-bit elements; how exact they have to be, the bound alone decides.
No kernel may reach another device: no remote copies, remote signals or barrier semaphores. Data moves between devices by JAX's collectives and lax.ppermute only.
A program may use at most 64 MiB of HBM per device.

v0:
```python
import math

import jax
import jax.numpy as jnp
from jax import lax
from jax.sharding import PartitionSpec as P

HEAD_COUNT = 128
HEAD_DIM = 64
NSTATE = 128
GROUPS = 8


HIGH = lax.Precision.HIGHEST


def carried_in(shard, axis, combine, identity, reverse):
    count, index = (lax.axis_size(axis), lax.axis_index(axis))
    everything = jax.tree.map(lambda part: lax.all_gather(part, axis), shard)
    start = jax.tree.map(
        lambda part, zero: jnp.broadcast_to(jnp.asarray(zero, part.dtype), part.shape),
        shard,
        identity,
    )

    def step(k, before):
        at = count - 1 - k if reverse else k
        reached = at > index if reverse else at < index
        new = combine(before, jax.tree.map(lambda part: part[at], everything))
        return jax.tree.map(lambda a, b: jnp.where(reached, a, b), new, before)

    return lax.fori_loop(0, count, step, start)


def merge_states(earlier, later):
    return (later[0] * earlier[0], later[1] + later[0][:, None, None] * earlier[1])


def block_terms(pieces):
    group_scores, grad_block, input_block, cum_block, write_block, read_block = pieces
    length = group_scores.shape[0]
    position = jnp.arange(length)
    later = (position[:, None] >= position[None, :])[None]
    gaps = cum_block[:, :, None] - cum_block[:, None, :]
    decay = jnp.where(later, jnp.exp(jnp.where(later, gaps, 0.0)), 0.0)
    weights = (group_scores[None] * decay).astype(jnp.bfloat16)
    inner = jnp.einsum("kts,tkp->skp", weights, grad_block, preferred_element_type=jnp.float32)
    dots = jnp.einsum("tkp,skp->kts", grad_block, input_block, preferred_element_type=jnp.float32)
    mixed = (dots * decay).astype(jnp.bfloat16)
    read_part = jnp.einsum("kts,sn->tn", mixed, write_block, preferred_element_type=jnp.float32)
    write_part = jnp.einsum("kts,tn->sn", mixed, read_block, preferred_element_type=jnp.float32)
    return (inner, read_part, write_part)


def per_device(ssd_grad, ssd_input, state_write, state_read, log_decay):
    grads = ssd_grad[0]
    length = grads.shape[0]
    decays = log_decay[0]
    heads = decays.shape[0]
    groups = state_write.shape[2] // NSTATE
    per_group = HEAD_COUNT // GROUPS
    width = math.gcd(per_group, 8)
    count = heads // width
    repeats = per_group // width
    chain_width = math.gcd(heads, 8)
    chain_count = heads // chain_width
    cums = jnp.cumsum(decays, axis=1)
    totals = cums[:, -1]
    grad_heads = grads.reshape(length, heads, HEAD_DIM)
    input_heads = ssd_input[0].reshape(length, heads, HEAD_DIM)
    write_groups = state_write[0].reshape(length, groups, NSTATE)
    read_groups = state_read[0].reshape(length, groups, NSTATE)
    fade = jnp.exp(totals[None, :] - cums.T)
    lift = jnp.exp(cums).T
    carried = (lift[:, :, None] * jnp.repeat(read_groups, per_group, axis=1)).astype(jnp.bfloat16)
    written = (fade[:, :, None] * jnp.repeat(write_groups, per_group, axis=1)).astype(jnp.bfloat16)
    back_local = jnp.einsum("thn,thp->hnp", carried, grad_heads, preferred_element_type=jnp.float32)
    fwd_local = jnp.einsum("shn,shp->hnp", written, input_heads, preferred_element_type=jnp.float32)
    passage = jnp.exp(totals)
    identity = (
        jnp.ones((chain_width,), jnp.float32),
        jnp.zeros((chain_width, NSTATE, HEAD_DIM), jnp.float32),
    )
    passage_blocks = passage.reshape(chain_count, chain_width)
    back_blocks = back_local.reshape(chain_count, chain_width, NSTATE, HEAD_DIM)
    fwd_blocks = fwd_local.reshape(chain_count, chain_width, NSTATE, HEAD_DIM)

    def later_chain(pieces):
        return carried_in(pieces, "ctx", merge_states, identity, True)[1]

    def earlier_chain(pieces):
        return carried_in(pieces, "ctx", merge_states, identity, False)[1]

    scores = jnp.einsum(
        "tgn,sgn->gts", read_groups, write_groups, preferred_element_type=jnp.float32
    )
    pieces = (
        jnp.repeat(scores, repeats, axis=0),
        jnp.transpose(grad_heads.reshape(length, count, width, HEAD_DIM), (1, 0, 2, 3)),
        jnp.transpose(input_heads.reshape(length, count, width, HEAD_DIM), (1, 0, 2, 3)),
        cums.reshape(count, width, length),
        jnp.repeat(jnp.transpose(write_groups, (1, 0, 2)), repeats, axis=0),
        jnp.repeat(jnp.transpose(read_groups, (1, 0, 2)), repeats, axis=0),
    )
    inner, read_part, write_part = lax.map(block_terms, pieces)
    incoming = lax.map(later_chain, (passage_blocks, back_blocks))
    prior = lax.map(earlier_chain, (passage_blocks, fwd_blocks))
    incoming, prior = (
        incoming.reshape(heads, NSTATE, HEAD_DIM),
        prior.reshape(heads, NSTATE, HEAD_DIM),
    )
    inner = jnp.transpose(inner, (1, 0, 2, 3)).reshape(length, heads, HEAD_DIM)
    read_intra = jnp.transpose(
        read_part.reshape(groups, repeats, length, NSTATE).sum(axis=1), (1, 0, 2)
    )
    write_intra = jnp.transpose(
        write_part.reshape(groups, repeats, length, NSTATE).sum(axis=1), (1, 0, 2)
    )
    incoming = incoming.reshape(groups, per_group, NSTATE, HEAD_DIM)
    prior = prior.reshape(groups, per_group, NSTATE, HEAD_DIM)
    outer = jnp.einsum("sgn,gknp->sgkp", write_groups.astype(jnp.float32), incoming, precision=HIGH)
    outer = outer.reshape(length, heads, HEAD_DIM) * fade[:, :, None]
    input_grad = (inner + outer).astype(jnp.bfloat16).reshape(1, length, heads * HEAD_DIM)
    lifted = (grad_heads.astype(jnp.float32) * lift[:, :, None]).reshape(
        length, groups, per_group, HEAD_DIM
    )
    read_inter = jnp.einsum("tgkp,gknp->tgn", lifted, prior, precision=HIGH)
    faded = (input_heads.astype(jnp.float32) * fade[:, :, None]).reshape(
        length, groups, per_group, HEAD_DIM
    )
    write_inter = jnp.einsum("sgkp,gknp->sgn", faded, incoming, precision=HIGH)
    read_grad = (read_intra + read_inter).astype(jnp.bfloat16).reshape(1, length, groups * NSTATE)
    write_grad = (
        (write_intra + write_inter).astype(jnp.bfloat16).reshape(1, length, groups * NSTATE)
    )
    return (input_grad, write_grad, read_grad)


def solution(mesh):
    in_specs = (
        P("dp", "ctx", "head"),
        P("dp", "ctx", "head"),
        P("dp", "ctx", "head"),
        P("dp", "ctx", "head"),
        P("dp", "head", "ctx"),
    )
    out_specs = (P("dp", "ctx", "head"), P("dp", "ctx", "head"), P("dp", "ctx", "head"))
    return jax.shard_map(
        per_device, mesh=mesh, in_specs=in_specs, out_specs=out_specs, check_vma=False
    )
```

profile of v0, /device:TPU:56, one launch (start us, length us, event | category | flops | bytes accessed | tf_op | source)
XLA Modules:
  0.0 1201.5 jit_solution(11334482343834815660)
XLA Ops:
  7.2 1.0 reduce_window_sum.11
  8.4 1.1 copy.41
  11.1 592.4 %while.75 = (s32[]{:T(128)}, f32[2,8,128,64]{3,2,1,0:T(8,128)S(1)}, f32[2,8]{1,0:T(2,128)S(1)}, f32[2,8,128,64]{2,3,1,0:T(8,128)S(1)}, s32[]{:T(128)}, /*index=5...) while((s32[]{:T(128)}, f32[2,8,128,64]{3,2,1,0:T(8,128)S(1)}, ...), condition=%wide.region_7.8_spmd, body=%wide.region_4.7_spmd.sunk | while | flops 262157 | bytes 54528648 | solution.py:106
  11.9 86.5 %all-gather.4 = f32[64,1,8]{2,1,0:T(1,128)S(1)} all-gather(f32[1,1,8]{2,1,0:T(1,128)S(1)} %fusion.84), channel_id=1, replica_groups=mesh['ctx'=64,'head'=8,'dp'=2] {'ctx'}, dimensions={0}, use_global_device_ids=true | all-gather | bytes 2080 | tf_op jit(solution)/shard_map/while/body/eval_jaxpr/all_gather | solution.py:19
  98.4 126.7 %all-gather.9.cloned.1.call-done = f32[64,8,128,64]{2,3,1,0:T(8,128)} async-done(((f32[1,8,128,64]{2,3,1,0:T(8,128)}), f32[64,8,128,64]{2,3,1,0:T(8,128)}) %all-gather.9.cloned.1.call-update) | async-done | bytes 16777232 | tf_op jit(solution)/shard_map/while/body/eval_jaxpr/all_gather | solution.py:19
  225.1 88.0 %while.78 = (s32[]{:T(128)}, f32[8,128,64]{2,1,0:T(8,128)S(1)}, s32[]{:T(128)}, f32[64,8,128,64]{2,3,1,0:T(8,128)}, f32[64,8]{1,0:T(8,128)S(1)}, /*index=5*/s32[]{:T(128)}, s32[]{:T(128)}, s32[]{:T(128)}, s32[]{:T(128)}) while((s32[]{:T(128)}, f32[8,128,64]{2,1,0:T(8,128)S(1)}, s32[]{:T(128)}, f32[64,8,128,64]{2,3,1,0:T(8,128)}, ...), condition=%wide.region_6.6_spmd.clone, body=%wide.region_5.5_spmd.clone.sunk | while | flops 262152 | bytes 1835271 | solution.py:32
  226.5 1.0 constant_dynamic-slice_fusion.13
  227.9 1.0 constant_dynamic-slice_fusion.13
  233.4 1.0 constant_dynamic-slice_fusion.13
  234.8 1.0 constant_dynamic-slice_fusion.13
  236.1 1.0 constant_dynamic-slice_fusion.13
  237.5 1.0 constant_dynamic-slice_fusion.13
  241.6 1.0 constant_dynamic-slice_fusion.13
  243.0 1.0 constant_dynamic-slice_fusion.13
  244.4 1.0 constant_dynamic-slice_fusion.13
  245.8 1.0 constant_dynamic-slice_fusion.13
  251.3 1.0 constant_dynamic-slice_fusion.13
  252.7 1.0 constant_dynamic-slice_fusion.13
  254.0 1.0 constant_dynamic-slice_fusion.13
  259.5 1.0 constant_dynamic-slice_fusion.13
  260.9 1.0 constant_dynamic-slice_fusion.13
  262.3 1.0 constant_dynamic-slice_fusion.13
  263.7 1.0 constant_dynamic-slice_fusion.13
  267.8 1.0 constant_dynamic-slice_fusion.13
  269.2 1.0 constant_dynamic-slice_fusion.13
  270.5 1.0 constant_dynamic-slice_fusion.13
  271.9 1.0 constant_dynamic-slice_fusion.13
  277.4 1.0 constant_dynamic-slice_fusion.13
  278.8 1.0 constant_dynamic-slice_fusion.13
  280.2 1.0 constant_dynamic-slice_fusion.13
  285.7 1.0 constant_dynamic-slice_fusion.13
  287.0 1.0 constant_dynamic-slice_fusion.13
  314.0 72.8 %all-gather.4 = f32[64,1,8]{2,1,0:T(1,128)S(1)} all-gather(f32[1,1,8]{2,1,0:T(1,128)S(1)} %fusion.84), channel_id=1, replica_groups=mesh['ctx'=64,'head'=8,'dp'=2] {'ctx'}, dimensions={0}, use_global_device_ids=true | all-gather | bytes 2080 | tf_op jit(solution)/shard_map/while/body/eval_jaxpr/all_gather | solution.py:19
  386.8 128.6 %all-gather.9.cloned.1.call-done = f32[64,8,128,64]{2,3,1,0:T(8,128)} async-done(((f32[1,8,128,64]{2,3,1,0:T(8,128)}), f32[64,8,128,64]{2,3,1,0:T(8,128)}) %all-gather.9.cloned.1.call-update) | async-done | bytes 16777232 | tf_op jit(solution)/shard_map/while/body/eval_jaxpr/all_gather | solution.py:19
  515.4 88.0 %while.78 = (s32[]{:T(128)}, f32[8,128,64]{2,1,0:T(8,128)S(1)}, s32[]{:T(128)}, f32[64,8,128,64]{2,3,1,0:T(8,128)}, f32[64,8]{1,0:T(8,128)S(1)}, /*index=5*/s32[]{:T(128)}, s32[]{:T(128)}, s32[]{:T(128)}, s32[]{:T(128)}) while((s32[]{:T(128)}, f32[8,128,64]{2,1,0:T(8,128)S(1)}, s32[]{:T(128)}, f32[64,8,128,64]{2,3,1,0:T(8,128)}, ...), condition=%wide.region_6.6_spmd.clone, body=%wide.region_5.5_spmd.clone.sunk | while | flops 262152 | bytes 1835271 | solution.py:32
  603.5 1.0 fusion.44
  604.9 2.2 while.73
  607.8 1.0 bitcast_multiply_fusion
  609.9 1.0 fusion.34
  612.3 578.1 %while.77 = (s32[]{:T(128)}, f32[2,8,128,64]{3,2,1,0:T(8,128)S(1)}, f32[2,8]{1,0:T(2,128)S(1)}, f32[2,8,128,64]{2,3,1,0:T(8,128)S(1)}, s32[]{:T(128)}, /*index=5...) while((s32[]{:T(128)}, f32[2,8,128,64]{3,2,1,0:T(8,128)S(1)}, f32[2,8]{1,0:T(2,128)S(1)}, ...), condition=%wide.region_13.14_spmd, body=%wide.region_10.13_spmd.sunk | while | flops 262153 | bytes 54528552 | solution.py:107
  613.2 72.8 %all-gather.5 = f32[64,1,8]{2,1,0:T(1,128)S(1)} all-gather(f32[1,1,8]{2,1,0:T(1,128)S(1)} %fusion.85), channel_id=1, replica_groups=mesh['ctx'=64,'head'=8,'dp'=2] {'ctx'}, dimensions={0}, use_global_device_ids=true | all-gather | bytes 2080 | tf_op jit(solution)/shard_map/while/body/eval_jaxpr/all_gather | solution.py:19
  685.9 128.6 %all-gather.11.cloned.1.call-done = f32[64,8,128,64]{2,3,1,0:T(8,128)} async-done(((f32[1,8,128,64]{2,3,1,0:T(8,128)}), f32[64,8,128,64]{2,3,1,0:T(8,128)}) %all-gather.11.cloned.1.call-update) | async-done | bytes 16777232 | tf_op jit(solution)/shard_map/while/body/eval_jaxpr/all_gather | solution.py:19
  814.5 86.9 %while.79 = (s32[]{:T(128)}, f32[8,128,64]{2,1,0:T(8,128)S(1)}, s32[]{:T(128)}, f32[64,8,128,64]{2,3,1,0:T(8,128)}, f32[64,8]{1,0:T(8,128)S(1)}, /*index=5*/s32[]{:T(128)}, s32[]{:T(128)}) while((s32[]{:T(128)}, f32[8,128,64]{2,1,0:T(8,128)S(1)}, s32[]{:T(128)}, f32[64,8,128,64]{2,3,1,0:T(8,128)}, f32[64,8]{1,0:T(8,128)S(1)}, ...), condition=%wide.region_12.12_spmd.clone, body=%wide.region_11.11_spmd.clone.sunk | while | flops 262148 | bytes 1835209 | solution.py:32
  902.4 72.8 %all-gather.5 = f32[64,1,8]{2,1,0:T(1,128)S(1)} all-gather(f32[1,1,8]{2,1,0:T(1,128)S(1)} %fusion.85), channel_id=1, replica_groups=mesh['ctx'=64,'head'=8,'dp'=2] {'ctx'}, dimensions={0}, use_global_device_ids=true | all-gather | bytes 2080 | tf_op jit(solution)/shard_map/while/body/eval_jaxpr/all_gather | solution.py:19
  975.1 128.3 %all-gather.11.cloned.1.call-done = f32[64,8,128,64]{2,3,1,0:T(8,128)} async-done(((f32[1,8,128,64]{2,3,1,0:T(8,128)}), f32[64,8,128,64]{2,3,1,0:T(8,128)}) %all-gather.11.cloned.1.call-update) | async-done | bytes 16777232 | tf_op jit(solution)/shard_map/while/body/eval_jaxpr/all_gather | solution.py:19
  1103.4 86.9 %while.79 = (s32[]{:T(128)}, f32[8,128,64]{2,1,0:T(8,128)S(1)}, s32[]{:T(128)}, f32[64,8,128,64]{2,3,1,0:T(8,128)}, f32[64,8]{1,0:T(8,128)S(1)}, /*index=5*/s32[]{:T(128)}, s32[]{:T(128)}) while((s32[]{:T(128)}, f32[8,128,64]{2,1,0:T(8,128)S(1)}, s32[]{:T(128)}, f32[64,8,128,64]{2,3,1,0:T(8,128)}, f32[64,8]{1,0:T(8,128)S(1)}, ...), condition=%wide.region_12.12_spmd.clone, body=%wide.region_11.11_spmd.clone.sunk | while | flops 262148 | bytes 1835209 | solution.py:32
  1191.4 1.0 fusion.35
  1193.2 1.8 copy.52
  (1071 shorter events, 324.4 us)
Async XLA Ops:
  11.0 592.5 %copy-start.1 = (bf16[1,128,128]{2,1,0:T(8,128)(2,1)S(1)}, bf16[1,128,128]{2,1,0:T(8,128)(2,1)}, u32[]{:S(2)}) copy-start(bf16[1,128,128]{2,1,0:T(8,128)(2,1)} %param.17) | copy-start | bytes 98308
  11.0 593.4 %copy-start.3 = (bf16[1,128,1024]{2,1,0:T(8,128)(2,1)S(1)}, bf16[1,128,1024]{2,1,0:T(8,128)(2,1)}, u32[]{:S(2)}) copy-start(bf16[1,128,1024]{2,1,0:T(8,128)(2,1)} %param.16) | copy-start | bytes 786436
  11.0 593.6 %copy-start.2 = (bf16[1,128,128]{2,1,0:T(8,128)(2,1)S(1)}, bf16[1,128,128]{2,1,0:T(8,128)(2,1)}, u32[]{:S(2)}) copy-start(bf16[1,128,128]{2,1,0:T(8,128)(2,1)} %param.18) | copy-start | bytes 98308
  11.1 214.1 %all-gather.9.cloned.1.call-start = ((), (), s32[]{:S(2)}) async-start(), calls=%async_computation | async-start | bytes 17039360 | tf_op jit(solution)/shard_map/while/body/eval_jaxpr/all_gather | solution.py:19
  313.2 202.2 %all-gather.9.cloned.1.call-start = ((), (), s32[]{:S(2)}) async-start(), calls=%async_computation | async-start | bytes 17039360 | tf_op jit(solution)/shard_map/while/body/eval_jaxpr/all_gather | solution.py:19
  607.1 0.6 copy-start.4
  607.1 0.7 copy-start.5
  612.3 579.1 %copy-start = (f32[1,128,1024]{1,2,0:T(8,128)S(1)}, f32[1,128,1024]{1,2,0:T(8,128)}, u32[]{:S(2)}) copy-start(f32[1,128,1024]{1,2,0:T(8,128)} %get-tuple-element.512) | copy-start | bytes 1572868
  612.3 202.2 %all-gather.11.cloned.1.call-start = ((), (), s32[]{:S(2)}) async-start(), calls=%async_computation.1 | async-start | bytes 17039360 | tf_op jit(solution)/shard_map/while/body/eval_jaxpr/all_gather | solution.py:19
  901.5 201.9 %all-gather.11.cloned.1.call-start = ((), (), s32[]{:S(2)}) async-start(), calls=%async_computation.1 | async-start | bytes 17039360 | tf_op jit(solution)/shard_map/while/body/eval_jaxpr/all_gather | solution.py:19
Sparse Core Ops, SparseCore 0:
  16.6 208.5 all-gather.8
  318.7 196.6 all-gather.8
  617.9 196.6 all-gather.10
  906.7 196.6 all-gather.10
where the time goes:
time: 1210 us; the launch traced here: 1200 us
  waiting for transfers between devices  512 us (42%)
  local copies, waits for them, and re-layouts  312 us (26%)
  blocking collectives  305 us (25%)
  other arithmetic  38.7 us (3%)
  between operations  13.9 us (1%)
  loops' own time  12.9 us (1%)
    all_gather x4, waiting for transfers between devices, carried_in(): everything = jax.tree.map(lambda part: lax.all_gather(part, axis), shard)  512 us
    all_gather x4, blocking collectives, carried_in(): everything = jax.tree.map(lambda part: lax.all_gather(part, axis), shard)  305 us
    dynamic_slice x512, local copies, waits for them, and re-layouts, step(): new = combine(before, jax.tree.map(lambda part: part[at], everything))  300 us
    select_n x256, other arithmetic, step(): return jax.tree.map(lambda a, b: jnp.where(reached, a, b), new, before)  34 us
  transfers between devices with their start and end apart: 4, of which 4 were waited for; matrix products, arithmetic and copies ran while one was open for 0% of the time, Pallas kernels for 0%

commit v1 on v0

--- a/solution.py
+++ b/solution.py
@@ -14,26 +14,52 @@
 HIGH = lax.Precision.HIGHEST
 
 
-def carried_in(shard, axis, combine, identity, reverse):
-    count, index = (lax.axis_size(axis), lax.axis_index(axis))
-    everything = jax.tree.map(lambda part: lax.all_gather(part, axis), shard)
-    start = jax.tree.map(
-        lambda part, zero: jnp.broadcast_to(jnp.asarray(zero, part.dtype), part.shape),
-        shard,
-        identity,
-    )
-
-    def step(k, before):
-        at = count - 1 - k if reverse else k
-        reached = at > index if reverse else at < index
-        new = combine(before, jax.tree.map(lambda part: part[at], everything))
-        return jax.tree.map(lambda a, b: jnp.where(reached, a, b), new, before)
-
-    return lax.fori_loop(0, count, step, start)
+def lower_weights(p, idx):
+    k = jnp.arange(p.shape[0])[:, None]
+    q = jnp.where(k < idx, p, 1.0)
+    c = jnp.cumprod(q[::-1], axis=0)[::-1]
+    after = jnp.concatenate([c[1:], jnp.ones_like(c[:1])], axis=0)
+    return jnp.where(k < idx, after, 0.0)
 
 
-def merge_states(earlier, later):
-    return (later[0] * earlier[0], later[1] + later[0][:, None, None] * earlier[1])
+def upper_weights(p, idx):
+    k = jnp.arange(p.shape[0])[:, None]
+    q = jnp.where(k > idx, p, 1.0)
+    c = jnp.cumprod(q, axis=0)
+    before = jnp.concatenate([jnp.ones_like(c[:1]), c[:-1]], axis=0)
+    return jnp.where(k > idx, before, 0.0)
+
+
+def weighted(w, states):
+    return (w[:, :, None, None] * states).sum(axis=0)
+
+
+def chain_states(passage, fwd_local, back_local):
+    nx, nz = lax.axis_size("cx"), lax.axis_size("cz")
+    xi, zi = lax.axis_index("cx"), lax.axis_index("cz")
+    heads = passage.shape[0]
+    part = heads // nx
+    table = lax.all_gather(passage, ("cz", "cx")).reshape(nz, nx, heads)
+    group = jnp.take(table, zi, axis=0)
+    everything = lax.all_gather(jnp.stack([fwd_local, back_local]), "cx")
+    fwd_all, back_all = everything[:, 0], everything[:, 1]
+    local_f = weighted(lower_weights(group, xi), fwd_all)
+    local_b = weighted(upper_weights(group, xi), back_all)
+    agg_f = weighted(lower_weights(group, nx), fwd_all)
+    agg_b = weighted(upper_weights(group, -1), back_all)
+    k = jnp.arange(nx)[:, None]
+    lead_f = jnp.prod(jnp.where(k < xi, group, 1.0), axis=0)
+    lead_b = jnp.prod(jnp.where(k > xi, group, 1.0), axis=0)
+    mine = lax.dynamic_slice_in_dim(jnp.stack([agg_f, agg_b]), xi * part, part, axis=1)
+    spans = lax.dynamic_slice_in_dim(jnp.prod(table, axis=1), xi * part, part, axis=1)
+    rows = lax.all_gather(mine, "cz")
+    z_f = weighted(lower_weights(spans, zi), rows[:, 0])
+    z_b = weighted(upper_weights(spans, zi), rows[:, 1])
+    entry = lax.all_gather(jnp.stack([z_f, z_b]), "cx")
+    entry = jnp.transpose(entry, (1, 0, 2, 3, 4)).reshape(2, heads, NSTATE, HEAD_DIM)
+    prior = local_f + lead_f[:, None, None] * entry[0]
+    incoming = local_b + lead_b[:, None, None] * entry[1]
+    return incoming, prior
 
 
 def block_terms(pieces):
@@ -77,19 +103,6 @@
     back_local = jnp.einsum("thn,thp->hnp", carried, grad_heads, preferred_element_type=jnp.float32)
     fwd_local = jnp.einsum("shn,shp->hnp", written, input_heads, preferred_element_type=jnp.float32)
     passage = jnp.exp(totals)
-    identity = (
-        jnp.ones((chain_width,), jnp.float32),
-        jnp.zeros((chain_width, NSTATE, HEAD_DIM), jnp.float32),
-    )
-    passage_blocks = passage.reshape(chain_count, chain_width)
-    back_blocks = back_local.reshape(chain_count, chain_width, NSTATE, HEAD_DIM)
-    fwd_blocks = fwd_local.reshape(chain_count, chain_width, NSTATE, HEAD_DIM)
-
-    def later_chain(pieces):
-        return carried_in(pieces, "ctx", merge_states, identity, True)[1]
-
-    def earlier_chain(pieces):
-        return carried_in(pieces, "ctx", merge_states, identity, False)[1]
 
     scores = jnp.einsum(
         "tgn,sgn->gts", read_groups, write_groups, preferred_element_type=jnp.float32
@@ -103,12 +116,7 @@
         jnp.repeat(jnp.transpose(read_groups, (1, 0, 2)), repeats, axis=0),
     )
     inner, read_part, write_part = lax.map(block_terms, pieces)
-    incoming = lax.map(later_chain, (passage_blocks, back_blocks))
-    prior = lax.map(earlier_chain, (passage_blocks, fwd_blocks))
-    incoming, prior = (
-        incoming.reshape(heads, NSTATE, HEAD_DIM),
-        prior.reshape(heads, NSTATE, HEAD_DIM),
-    )
+    incoming, prior = chain_states(passage, fwd_local, back_local)
     inner = jnp.transpose(inner, (1, 0, 2, 3)).reshape(length, heads, HEAD_DIM)
     read_intra = jnp.transpose(
         read_part.reshape(groups, repeats, length, NSTATE).sum(axis=1), (1, 0, 2)
@@ -136,15 +144,31 @@
     return (input_grad, write_grad, read_grad)
 
 
+def x_extent(mesh):
+    column = mesh.devices[:, 0, 0]
+    try:
+        extent = len({d.coords[0] for d in column})
+    except AttributeError:
+        extent = 1
+    if extent < 1 or column.size % extent:
+        extent = 1
+    return extent
+
+
 def solution(mesh):
+    nx = x_extent(mesh)
+    shape = mesh.devices.shape
+    devices = mesh.devices.reshape(shape[0] // nx, nx, *shape[1:])
+    mesh = jax.sharding.Mesh(devices, ("cz", "cx", "head", "dp"))
+    ctx = ("cz", "cx")
     in_specs = (
-        P("dp", "ctx", "head"),
-        P("dp", "ctx", "head"),
-        P("dp", "ctx", "head"),
-        P("dp", "ctx", "head"),
-        P("dp", "head", "ctx"),
+        P("dp", ctx, "head"),
+        P("dp", ctx, "head"),
+        P("dp", ctx, "head"),
+        P("dp", ctx, "head"),
+        P("dp", "head", ctx),
     )
-    out_specs = (P("dp", "ctx", "head"), P("dp", "ctx", "head"), P("dp", "ctx", "head"))
+    out_specs = (P("dp", ctx, "head"), P("dp", ctx, "head"), P("dp", ctx, "head"))
     return jax.shard_map(
         per_device, mesh=mesh, in_specs=in_specs, out_specs=out_specs, check_vma=False
     )

time: 1210 us -> 298 us (0.25)
  waiting for transfers between devices: 512 us -> 99 us
  local copies, waits for them, and re-layouts: 312 us -> 6.9 us
  blocking collectives: 305 us -> 157 us
  other arithmetic: 38.7 us -> 13.2 us
  loops' own time: 12.9 us -> 0.1 us
    all_gather x4 -> x3, waiting for transfers between devices: 512 us -> 98.9 us  [the longest x1 70.7 us: chain_states(): rows = lax.all_gather(mine, 'cz')]
    all_gather x4 -> x0, blocking collectives: 305 us -> none  [carried_in(): everything = jax.tree.map(lambda part: lax.all_gather(part, axis), shard)]
    dynamic_slice x516 -> x0, local copies, waits for them, and re-layouts: 303 us -> none  [the longest x512 300 us: step(): new = combine(before, jax.tree.map(lambda part: part[at], everything))]
    unnamed x0 -> x1, blocking collectives: none -> 157 us
    select_n x256 -> x7, other arithmetic: 34 us -> 0.51 us  [the longest x3 0.22 us: lower_weights(): return jnp.where(k < idx, after, 0.0)]
    another operation x6 -> x0, loops' own time: 12.8 us -> none  [the longest x4 12.5 us: carried_in(): return lax.fori_loop(0, count, step, start)]
  transfers between devices with their start and end apart: 4 -> 3, of which waited for: 4 -> 2; matrix products, arithmetic and copies ran while one was open for 0% -> 2% of each run, Pallas kernels for 0% -> 0%
where the time goes in v1:
time: 298 us; the launch traced here: 297 us
  blocking collectives  157 us (53%)
  waiting for transfers between devices  99 us (33%)
  between operations  14.6 us (5%)
  other arithmetic  13.2 us (4%)
  local copies, waits for them, and re-layouts  6.9 us (2%)
  matrix products  5.64 us (2%)
    unnamed x1, blocking collectives  157 us
    all_gather x1, waiting for transfers between devices, chain_states(): rows = lax.all_gather(mine, 'cz')  70.7 us
    all_gather x1, waiting for transfers between devices, chain_states(): entry = lax.all_gather(jnp.stack([z_f, z_b]), 'cx')  28.2 us
    unnamed x12, local copies, waits for them, and re-layouts  6.08 us
  transfers between devices with their start and end apart: 3, of which 2 were waited for; matrix products, arithmetic and copies ran while one was open for 2% of the time, Pallas kernels for 0%

profile of v1, /device:TPU:56, one launch (start us, length us, event | category | flops | bytes accessed | tf_op | source)
XLA Modules:
  0.0 296.7 jit_solution(2645878069858129936)
XLA Ops:
  7.2 1.0 reduce_window_sum.11
  8.2 0.2 exponential_reduce_fusion
  8.4 0.1 exponential_bitcast_fusion.1
  8.5 1.1 copy.29
  9.6 0.8 bitcast_convert_fusion.1
  10.4 1.1 copy.30
  11.5 0.8 bitcast_convert_fusion
  12.2 0.5 convolution_bitcast_fusion.3
  12.8 0.5 convolution_bitcast_fusion.4
  13.3 1.1 pad_maximum_fusion
  14.5 1.3 dynamic-slice.4
  16.4 0.2 dynamic-update-slice.1
  16.7 157.1 %all-reduce.6 = f32[1024]{0:T(1024)S(1)} all-reduce(f32[1024]{0:T(1024)S(1)} %dynamic-update-slice.1), channel_id=2, replica_groups=mesh['cz'=16,'cx'=4,'head'=8,'dp'=2] {'cz','cx'}, use_global_device_ids=true, to_apply=%add.6 | all-reduce | flops 1024 | bytes 8192
  173.7 0.1 reshape.218
  173.9 0.1 fusion.51
  174.2 0.1 pad_select_fusion.2
  174.3 0.1 pad_select_fusion.5
  174.5 3.1 %multiply_reduce_fusion = (f32[16,128,64]{1,2,0:T(8,128)S(1)}, f32[16,128,64]{1,2,0:T(8,128)S(1)}, f32[16,128,64]{1,2,0:T(8,128)S(1)}, f32[16,128,64]{1,2,0:T(8,128)S(1)}) fusion(f32[4,2,16,128,64]{3,4,2,1,0:T(8,128)} %bitcast.197, f32[4,16]{1,0:T(4,128)S(1)} %pad_select_fusion.2, f32[4,16]{1,0:T(4,128)S(1)} %pad_select_fusion.3, ...), kind=kLoop, calls=%fused_computation.43 | loop fusion | flops 3670016 | bytes 6292480 | tf_op jit(solution)/shard_map/reduce_sum | solution.py:34
  177.6 0.7 fusion.44
  178.5 0.1 dynamic-slice_select_fusion
  178.7 0.1 mul.166
  178.8 0.1 mul.185
  178.8 0.1 pad_select_fusion.1
  178.9 0.1 pad_select_fusion
  179.0 0.1 fusion.47
  179.1 70.7 %all-gather.10.cloned.1.call-done = f32[32,4,128,64]{2,3,1,0:T(8,128)} async-done(((f32[2,4,128,64]{2,3,1,0:T(8,128)}), f32[32,4,128,64]{2,3,1,0:T(8,128)}) %all-gather.10.cloned.1.call-update) | async-done | bytes 4194320 | tf_op jit(solution)/shard_map/all_gather | solution.py:55
  249.9 2.6 fusion.29
  252.5 0.7 pad_maximum_fusion.1
  253.3 2.2 while.15
  253.3 0.4 fusion.79
  253.7 0.3 fusion.80
  254.0 0.1 fusion.81
  254.2 0.2 fusion.82
  254.4 0.4 fusion.79
  254.8 0.3 fusion.80
  255.1 0.1 fusion.81
  255.3 0.2 fusion.82
  255.5 0.1 copy.35
  255.6 0.1 copy.33
  255.7 28.2 %all-gather.12.cloned.1.call-done = f32[8,4,128,64]{2,3,1,0:T(8,128)} async-done(((f32[2,4,128,64]{2,3,1,0:T(8,128)}), f32[8,4,128,64]{2,3,1,0:T(8,128)}) %all-gather.12.cloned.1.call-update) | async-done | bytes 1048592 | tf_op jit(solution)/shard_map/all_gather | solution.py:58
  283.9 1.4 fusion.38
  285.3 0.4 fusion.45
  285.7 0.1 bitcast_multiply_fusion
  285.8 1.0 fusion.34
  286.8 0.7 copy.39
  287.6 1.0 fusion.35
  288.6 0.7 copy.38
  289.3 0.8 copy.37
  (47 shorter events, 0.9 us)
Async XLA Ops:
  7.2 167.4 %all-gather.8.cloned.1.call-start = ((), (), s32[]{:S(2)}) async-start(), calls=%async_computation | async-start | bytes 5242880 | tf_op jit(solution)/shard_map/all_gather | solution.py:44
  14.4 235.4 %all-gather.10.cloned.1.call-start = ((), (), s32[]{:S(2)}) async-start(), calls=%async_computation.1 | async-start | bytes 4456448 | tf_op jit(solution)/shard_map/all_gather | solution.py:55
  174.5 4.5 %copy-start = (bf16[1,128,128]{2,1,0:T(8,128)(2,1)S(1)}, bf16[1,128,128]{2,1,0:T(8,128)(2,1)}, u32[]{:S(2)}) copy-start(bf16[1,128,128]{2,1,0:T(8,128)(2,1)} %param.9) | copy-start | bytes 98308
  174.5 4.5 %copy-start.1 = (bf16[1,128,128]{2,1,0:T(8,128)(2,1)S(1)}, bf16[1,128,128]{2,1,0:T(8,128)(2,1)}, u32[]{:S(2)}) copy-start(bf16[1,128,128]{2,1,0:T(8,128)(2,1)} %param.10) | copy-start | bytes 98308
  178.4 105.6 %all-gather.12.cloned.1.call-start = ((), (), s32[]{:S(2)}) async-start(), calls=%async_computation.2 | async-start | bytes 1310720 | tf_op jit(solution)/shard_map/all_gather | solution.py:58
Sparse Core Ops, SparseCore 0:
  14.5 66.8 all-gather.7
  178.5 71.3 all-gather.9
  253.3 30.5 all-gather.11

commit v2 on v1

--- a/solution.py
+++ b/solution.py
@@ -34,15 +34,20 @@
     return (w[:, :, None, None] * states).sum(axis=0)
 
 
+def with_scalars(states, scalars):
+    rows = jnp.broadcast_to(scalars[None, :, None, None], states.shape[:2] + (8, states.shape[3]))
+    return jnp.concatenate([states, rows], axis=2)
+
+
 def chain_states(passage, fwd_local, back_local):
-    nx, nz = lax.axis_size("cx"), lax.axis_size("cz")
+    nx = lax.axis_size("cx")
     xi, zi = lax.axis_index("cx"), lax.axis_index("cz")
-    heads = passage.shape[0]
+    heads, n = fwd_local.shape[0], fwd_local.shape[1]
     part = heads // nx
-    table = lax.all_gather(passage, ("cz", "cx")).reshape(nz, nx, heads)
-    group = jnp.take(table, zi, axis=0)
-    everything = lax.all_gather(jnp.stack([fwd_local, back_local]), "cx")
-    fwd_all, back_all = everything[:, 0], everything[:, 1]
+    packed = with_scalars(jnp.stack([fwd_local, back_local]), passage)
+    everything = lax.all_gather(packed, "cx")
+    group = everything[:, 0, :, n, 0]
+    fwd_all, back_all = everything[:, 0, :, :n], everything[:, 1, :, :n]
     local_f = weighted(lower_weights(group, xi), fwd_all)
     local_b = weighted(upper_weights(group, xi), back_all)
     agg_f = weighted(lower_weights(group, nx), fwd_all)
@@ -50,13 +55,14 @@
     k = jnp.arange(nx)[:, None]
     lead_f = jnp.prod(jnp.where(k < xi, group, 1.0), axis=0)
     lead_b = jnp.prod(jnp.where(k > xi, group, 1.0), axis=0)
-    mine = lax.dynamic_slice_in_dim(jnp.stack([agg_f, agg_b]), xi * part, part, axis=1)
-    spans = lax.dynamic_slice_in_dim(jnp.prod(table, axis=1), xi * part, part, axis=1)
+    span = jnp.prod(group, axis=0)
+    mine = lax.dynamic_slice_in_dim(with_scalars(jnp.stack([agg_f, agg_b]), span), xi * part, part, axis=1)
     rows = lax.all_gather(mine, "cz")
-    z_f = weighted(lower_weights(spans, zi), rows[:, 0])
-    z_b = weighted(upper_weights(spans, zi), rows[:, 1])
+    spans = rows[:, 0, :, n, 0]
+    z_f = weighted(lower_weights(spans, zi), rows[:, 0, :, :n])
+    z_b = weighted(upper_weights(spans, zi), rows[:, 1, :, :n])
     entry = lax.all_gather(jnp.stack([z_f, z_b]), "cx")
-    entry = jnp.transpose(entry, (1, 0, 2, 3, 4)).reshape(2, heads, NSTATE, HEAD_DIM)
+    entry = jnp.transpose(entry, (1, 0, 2, 3, 4)).reshape(2, heads, n, HEAD_DIM)
     prior = local_f + lead_f[:, None, None] * entry[0]
     incoming = local_b + lead_b[:, None, None] * entry[1]
     return incoming, prior
@@ -88,8 +94,6 @@
     width = math.gcd(per_group, 8)
     count = heads // width
     repeats = per_group // width
-    chain_width = math.gcd(heads, 8)
-    chain_count = heads // chain_width
     cums = jnp.cumsum(decays, axis=1)
     totals = cums[:, -1]
     grad_heads = grads.reshape(length, heads, HEAD_DIM)

time: 298 us -> 284 us (0.953)
  blocking collectives: 157 us -> 0 us
  waiting for transfers between devices: 99 us -> 241 us
    unnamed x1 -> x0, blocking collectives: 157 us -> none
    all_gather x1, waiting for transfers between devices: 0.01 us -> 101 us  [chain_states(): everything = lax.all_gather(packed, 'cx')]
    all_gather x1, waiting for transfers between devices: 70.7 us -> 111 us  [chain_states(): rows = lax.all_gather(mine, 'cz')]
    unnamed x12 -> x10, local copies, waits for them, and re-layouts: 6.08 us -> 4.65 us
  transfers between devices with their start and end apart: 3 -> 3, of which waited for: 2 -> 3; matrix products, arithmetic and copies ran while one was open for 2% -> 1% of each run, Pallas kernels for 0% -> 0%
where the time goes in v2:
time: 284 us; the launch traced here: 283 us
  waiting for transfers between devices  241 us (85%)
  other arithmetic  15.3 us (5%)
  between operations  14 us (5%)
  local copies, waits for them, and re-layouts  6.82 us (2%)
  matrix products  5.63 us (2%)
    all_gather x1, waiting for transfers between devices, chain_states(): rows = lax.all_gather(mine, 'cz')  111 us
    all_gather x1, waiting for transfers between devices, chain_states(): everything = lax.all_gather(packed, 'cx')  101 us
    all_gather x1, waiting for transfers between devices, chain_states(): entry = lax.all_gather(jnp.stack([z_f, z_b]), 'cx')  28.9 us
    reduce_sum x2, other arithmetic, weighted(): return (w[:, :, None, None] * states).sum(axis=0)  5.76 us
  transfers between devices with their start and end apart: 3, of which 3 were waited for; matrix products, arithmetic and copies ran while one was open for 1% of the time, Pallas kernels for 0%

profile of v2, /device:TPU:56, one launch (start us, length us, event | category | flops | bytes accessed | tf_op | source)
XLA Modules:
  0.0 283.4 jit_solution(11709914518638012918)
XLA Ops:
  7.2 1.0 reduce_window_sum.11
  8.2 0.2 slice_reduce_fusion
  8.5 1.1 copy.38
  9.6 0.8 bitcast_convert_fusion.1
  10.4 1.1 copy.39
  11.5 0.8 bitcast_convert_fusion
  12.3 0.5 convolution_bitcast_fusion.3
  12.8 0.5 convolution_bitcast_fusion.4
  13.3 0.1 broadcast_in_dim.165
  13.5 1.6 pad_maximum_fusion
  15.2 101.0 %all-gather.7.cloned.1.call-done = f32[8,16,136,64]{2,3,1,0:T(8,128)} async-done(((f32[2,16,136,64]{2,3,1,0:T(8,128)}), f32[8,16,136,64]{2,3,1,0:T(8,128)}) %all-gather.7.cloned.1.call-update) | async-done | bytes 4456464 | tf_op jit(solution)/shard_map/all_gather | solution.py:48
  116.1 1.3 slice_reduce_fusion.1
  117.5 0.1 copy.53
  117.6 0.1 fusion.52
  118.2 3.1 %multiply_reduce_fusion = (f32[16,128,64]{1,2,0:T(8,128)S(1)}, f32[16,128,64]{1,2,0:T(8,128)S(1)}, f32[16,128,64]{1,2,0:T(8,128)S(1)}, f32[16,128,64]{1,2,0:T(8,128)S(1)}) fusion(f32[4,2,16,136,64]{3,4,2,1,0:T(8,128)} %bitcast.204, f32[4,16]{1,0:T(4,128)S(1)} %pad_select_fusion.2, f32[4,16]{1,0:T(4,128)S(1)} %pad_select_fusion.3, ...), kind=kLoop, calls=%fused_computation.47 | loop fusion | flops 3670016 | bytes 6292480 | tf_op jit(solution)/shard_map/reduce_sum | solution.py:34
  121.4 0.1 broadcast_in_dim.171
  121.5 0.9 fusion.39
  122.6 0.1 fusion.48
  122.7 111.4 %all-gather.9.cloned.1.call-done = f32[32,4,136,64]{2,3,1,0:T(8,128)} async-done(((f32[2,4,136,64]{2,3,1,0:T(8,128)}), f32[32,4,136,64]{2,3,1,0:T(8,128)}) %all-gather.9.cloned.1.call-update) | async-done | bytes 4456464 | tf_op jit(solution)/shard_map/all_gather | solution.py:60
  234.1 1.0 slice.78
  235.1 0.1 copy.43
  235.2 0.1 copy.44
  235.4 0.1 pad_select_fusion.1
  235.6 0.1 pad_select_fusion
  235.6 2.6 fusion.29
  238.3 0.7 pad_maximum_fusion.1
  239.1 2.2 while.14
  239.2 0.4 fusion.80
  239.5 0.3 fusion.81
  239.9 0.1 fusion.82
  240.0 0.2 fusion.83
  240.3 0.4 fusion.80
  240.6 0.3 fusion.81
  241.0 0.1 fusion.82
  241.1 0.2 fusion.83
  241.3 0.1 copy.48
  241.4 0.1 copy.46
  241.5 0.1 mul.165
  241.6 0.1 mul.184
  241.7 28.9 %all-gather.11.cloned.1.call-done = f32[8,4,128,64]{2,3,1,0:T(8,128)} async-done(((f32[2,4,128,64]{2,3,1,0:T(8,128)}), f32[8,4,128,64]{2,3,1,0:T(8,128)}) %all-gather.11.cloned.1.call-update) | async-done | bytes 1048592 | tf_op jit(solution)/shard_map/all_gather | solution.py:64
  270.6 1.4 fusion.40
  272.0 0.4 fusion.46
  272.4 0.1 bitcast_multiply_fusion
  272.5 1.0 fusion.34
  273.6 0.7 copy.52
  274.3 1.0 fusion.35
  275.3 0.7 copy.51
  276.0 0.8 copy.50
  (49 shorter events, 1.2 us)
Async XLA Ops:
  7.2 109.0 %all-gather.7.cloned.1.call-start = ((), (), s32[]{:S(2)}) async-start(), calls=%async_computation | async-start | bytes 10485760 | tf_op jit(solution)/shard_map/all_gather | solution.py:48
  15.1 219.1 %all-gather.9.cloned.1.call-start = ((), (), s32[]{:S(2)}) async-start(), calls=%async_computation.1 | async-start | bytes 8912896 | tf_op jit(solution)/shard_map/all_gather | solution.py:60
  121.4 1.2 copy-start
  121.4 1.2 copy-start.1
  122.4 148.2 %all-gather.11.cloned.1.call-start = ((), (), s32[]{:S(2)}) async-start(), calls=%async_computation.2 | async-start | bytes 1310720 | tf_op jit(solution)/shard_map/all_gather | solution.py:64
Sparse Core Ops, SparseCore 0:
  15.2 100.9 all-gather.6
  122.6 111.5 all-gather.8
  239.2 31.4 all-gather.10

commit v3 on v2

--- a/solution.py
+++ b/solution.py
@@ -39,33 +39,48 @@
     return jnp.concatenate([states, rows], axis=2)
 
 
+def exchange(pieces, axis):
+    count, index = lax.axis_size(axis), lax.axis_index(axis)
+    got = [jnp.take(pieces, index, axis=0)]
+    for shift in range(1, count):
+        send = jnp.take(pieces, (index + shift) % count, axis=0)
+        got.append(lax.ppermute(send, axis, [(i, (i + shift) % count) for i in range(count)]))
+    return jnp.take(jnp.stack(got), (index - jnp.arange(count)) % count, axis=0)
+
+
+def all_weights(p, lower):
+    rows = [lower_weights(p, x) if lower else upper_weights(p, x) for x in range(p.shape[0])]
+    return jnp.stack(rows)
+
+
 def chain_states(passage, fwd_local, back_local):
     nx = lax.axis_size("cx")
     xi, zi = lax.axis_index("cx"), lax.axis_index("cz")
-    heads, n = fwd_local.shape[0], fwd_local.shape[1]
+    heads, n, width = fwd_local.shape
     part = heads // nx
     packed = with_scalars(jnp.stack([fwd_local, back_local]), passage)
-    everything = lax.all_gather(packed, "cx")
-    group = everything[:, 0, :, n, 0]
-    fwd_all, back_all = everything[:, 0, :, :n], everything[:, 1, :, :n]
-    local_f = weighted(lower_weights(group, xi), fwd_all)
-    local_b = weighted(upper_weights(group, xi), back_all)
+    pieces = jnp.transpose(packed.reshape(2, nx, part, n + 8, width), (1, 0, 2, 3, 4))
+    members = exchange(pieces, "cx")
+    group = members[:, 0, :, n, 0]
+    fwd_all, back_all = members[:, 0, :, :n], members[:, 1, :, :n]
+    w_f, w_b = all_weights(group, True), all_weights(group, False)
+    local_f = (w_f[:, :, :, None, None] * fwd_all[None]).sum(axis=1)
+    local_b = (w_b[:, :, :, None, None] * back_all[None]).sum(axis=1)
     agg_f = weighted(lower_weights(group, nx), fwd_all)
     agg_b = weighted(upper_weights(group, -1), back_all)
     k = jnp.arange(nx)[:, None]
-    lead_f = jnp.prod(jnp.where(k < xi, group, 1.0), axis=0)
-    lead_b = jnp.prod(jnp.where(k > xi, group, 1.0), axis=0)
+    lead_f = jnp.stack([jnp.prod(jnp.where(k < x, group, 1.0), axis=0) for x in range(nx)])
+    lead_b = jnp.stack([jnp.prod(jnp.where(k > x, group, 1.0), axis=0) for x in range(nx)])
     span = jnp.prod(group, axis=0)
-    mine = lax.dynamic_slice_in_dim(with_scalars(jnp.stack([agg_f, agg_b]), span), xi * part, part, axis=1)
-    rows = lax.all_gather(mine, "cz")
+    rows = lax.all_gather(with_scalars(jnp.stack([agg_f, agg_b]), span), "cz")
     spans = rows[:, 0, :, n, 0]
     z_f = weighted(lower_weights(spans, zi), rows[:, 0, :, :n])
     z_b = weighted(upper_weights(spans, zi), rows[:, 1, :, :n])
-    entry = lax.all_gather(jnp.stack([z_f, z_b]), "cx")
-    entry = jnp.transpose(entry, (1, 0, 2, 3, 4)).reshape(2, heads, n, HEAD_DIM)
-    prior = local_f + lead_f[:, None, None] * entry[0]
-    incoming = local_b + lead_b[:, None, None] * entry[1]
-    return incoming, prior
+    prior = local_f + lead_f[:, :, None, None] * z_f[None]
+    incoming = local_b + lead_b[:, :, None, None] * z_b[None]
+    back = exchange(jnp.stack([incoming, prior], axis=1), "cx")
+    back = jnp.transpose(back, (1, 0, 2, 3, 4)).reshape(2, heads, n, width)
+    return back[0], back[1]
 
 
 def block_terms(pieces):

time: 284 us -> 211 us (0.74)
  waiting for transfers between devices: 241 us -> 116 us
  starting transfers between devices: 0.12 us -> 22.8 us
  other arithmetic: 15.3 us -> 29.9 us
  local copies, waits for them, and re-layouts: 6.82 us -> 19 us
    all_gather x3 -> x1, waiting for transfers between devices: 241 us -> 91.6 us  [chain_states(): rows = lax.all_gather(with_scalars(jnp.stack([agg_f, agg_b]), span), 'cz')]
    ppermute x0 -> x6, waiting for transfers between devices: none -> 24.3 us  [exchange(): lax.ppermute(send, axis, [(i, (i + shift) % count) for i in range(count)])]
    ppermute x0 -> x6, starting transfers between devices: none -> 22.7 us  [exchange(): lax.ppermute(send, axis, [(i, (i + shift) % count) for i in range(count)])]
    another operation x3 -> x15, other arithmetic: 0.72 us -> 8.47 us  [the longest x9 5.8 us: all_weights(): return jnp.stack(rows)]
    another operation x3 -> x6, other arithmetic: 0.11 us -> 4.99 us  [upper_weights(): c = jnp.cumprod(q, axis=0)]
    rev x3 -> x5, local copies, waits for them, and re-layouts: 0.06 us -> 3.71 us  [lower_weights(): c = jnp.cumprod(q[::-1], axis=0)[::-1]]
    slice x3 -> x5, local copies, waits for them, and re-layouts: 0.08 us -> 3.68 us  [lower_weights(): after = jnp.concatenate([c[1:], jnp.ones_like(c[:1])], axis=0)]
    another operation x3 -> x5, other arithmetic: 0.12 us -> 3.71 us  [lower_weights(): c = jnp.cumprod(q[::-1], axis=0)[::-1]]
  transfers between devices with their start and end apart: 3 -> 7, of which waited for: 3 -> 6; matrix products, arithmetic and copies ran while one was open for 1% -> 14% of each run, Pallas kernels for 0% -> 0%
where the time goes in v3:
time: 211 us; the launch traced here: 208 us
  waiting for transfers between devices  116 us (55%)
  other arithmetic  29.9 us (14%)
  starting transfers between devices  22.8 us (11%)
  local copies, waits for them, and re-layouts  19 us (9%)
  between operations  14.8 us (7%)
  matrix products  5.6 us (3%)
    all_gather x1, waiting for transfers between devices, chain_states(): rows = lax.all_gather(with_scalars(jnp.stack([agg_f, agg_b]), span), 'cz')  91.6 us
    ppermute x6, waiting for transfers between devices, exchange(): lax.ppermute(send, axis, [(i, (i + shift) % count) for i in range(count)])  24.3 us
    ppermute x6, starting transfers between devices, exchange(): lax.ppermute(send, axis, [(i, (i + shift) % count) for i in range(count)])  22.7 us
    another operation x9, other arithmetic, all_weights(): return jnp.stack(rows)  5.8 us
    unnamed x51, local copies, waits for them, and re-layouts  5.66 us
    another operation x6, other arithmetic, upper_weights(): c = jnp.cumprod(q, axis=0)  4.99 us
  transfers between devices with their start and end apart: 7, of which 6 were waited for; matrix products, arithmetic and copies ran while one was open for 14% of the time, Pallas kernels for 0%

profile of v3, /device:TPU:56, one launch (start us, length us, event | category | flops | bytes accessed | tf_op | source)
XLA Modules:
  0.0 207.9 jit_solution(10048713477183516758)
XLA Ops:
  7.3 1.0 reduce_window_sum.11
  8.5 1.1 copy.76
  9.7 0.8 bitcast_convert_fusion.1
  10.4 1.1 copy.77
  11.6 0.8 bitcast_convert_fusion
  14.1 3.4 %collective-permute-start = (f32[2,4,136,64]{2,3,1,0:T(8,128)S(1)}, f32[2,4,136,64]{2,3,1,0:T(8,128)S(1)}, u32[]{:S(2)}, u32[]{:S(2)}) collective-permute-start(f32[2,4,136,64]{2,3,1,0:T(8,128)S(1)} %get-tuple-element.144), channel_id=1, source_target_pairs={{0,16},{16,32},{32,48},{48,0},{1,17},{17,33},{33,49},{49,1},{2,18}... | collective-permute-start | bytes 835592 | tf_op jit(solution)/shard_map/ppermute | solution.py:47
  17.5 4.6 %collective-permute-start.1 = (f32[2,4,136,64]{2,3,1,0:T(8,128)S(1)}, f32[2,4,136,64]{2,3,1,0:T(8,128)S(1)}, u32[]{:S(2)}, u32[]{:S(2)}) collective-permute-start(f32[2,4,136,64]{2,3,1,0:T(8,128)S(1)} %get-tuple-element.143), channel_id=1, source_target_pairs={{0,32},{16,48},{32,0},{48,16},{1,33},{17,49},{33,1},{49,17},{2,34}... | collective-permute-start | bytes 835592 | tf_op jit(solution)/shard_map/ppermute | solution.py:47
  22.1 3.3 %collective-permute-start.2 = (f32[2,4,136,64]{2,3,1,0:T(8,128)S(1)}, f32[2,4,136,64]{2,3,1,0:T(8,128)S(1)}, u32[]{:S(2)}, u32[]{:S(2)}) collective-permute-start(f32[2,4,136,64]{2,3,1,0:T(8,128)S(1)} %get-tuple-element.142), channel_id=1, source_target_pairs={{0,48},{16,0},{32,16},{48,32},{1,49},{17,1},{33,17},{49,33},{2,50}... | collective-permute-start | bytes 835592 | tf_op jit(solution)/shard_map/ppermute | solution.py:47
  25.7 5.3 %collective-permute-done = f32[2,4,136,64]{2,3,1,0:T(8,128)S(1)} collective-permute-done((f32[2,4,136,64]{2,3,1,0:T(8,128)S(1)}, f32[2,4,136,64]{2,3,1,0:T(8,128)S(1)}, u32[]{:S(2)}, u32[]{:S(2)}) %collective-permute-start) | collective-permute-done | bytes 278560 | tf_op jit(solution)/shard_map/ppermute | solution.py:47
  31.0 12.1 %collective-permute-done.1 = f32[2,4,136,64]{2,3,1,0:T(8,128)S(1)} collective-permute-done((f32[2,4,136,64]{2,3,1,0:T(8,128)S(1)}, f32[2,4,136,64]{2,3,1,0:T(8,128)S(1)}, u32[]{:S(2)}, u32[]{:S(2)}) %collective-permute-start.1) | collective-permute-done | bytes 278560 | tf_op jit(solution)/shard_map/ppermute | solution.py:47
  43.1 1.6 collective-permute-done.2
  44.8 2.0 gather_fusion
  46.8 1.9 broadcast_select_fusion
  49.0 1.3 fusion.61
  50.8 0.9 pad_maximum_fusion.3
  54.1 1.3 rev.25
  55.3 1.2 reduce_window.73
  56.5 1.2 slice.98
  57.7 1.2 rev.24
  58.9 1.2 reduce_window.72
  60.1 1.2 slice.96
  61.3 1.2 rev.11
  62.5 1.2 reduce_window.71
  63.8 1.2 slice.94
  65.0 1.2 reduce_window.51
  66.2 1.2 reduce_window.67
  67.5 1.2 reduce_window.66
  68.7 1.3 reduce_window.54
  69.9 1.3 pad_maximum_fusion.6
  71.9 0.8 select_bitcast_fusion.7
  73.4 0.7 select_bitcast_fusion.9
  74.1 0.7 select_bitcast_fusion.4
  74.9 0.7 select_bitcast_fusion.5
  77.8 91.6 %all-gather.3.cloned.1.call-done = f32[32,4,136,64]{2,3,1,0:T(8,128)} async-done(((f32[2,4,136,64]{2,3,1,0:T(8,128)}), f32[32,4,136,64]{2,3,1,0:T(8,128)}) %all-gather.3.cloned.1.call-update) | async-done | bytes 4456464 | tf_op jit(solution)/shard_map/all_gather | solution.py:75
  169.3 1.0 slice.138
  170.8 2.6 %fusion.27 = (f32[4,128,64]{1,2,0:T(8,128)S(1)}, f32[4,128,64]{1,2,0:T(8,128)S(1)}) fusion(f32[16,2,4,136,64]{3,4,2,1,0:T(8,128)} %bitcast.247, f32[16,4]{1,0:T(8,128)S(1)} %pad_select_fusion, f32[16,4]{1,0:T(8,128)S(1)} %pad_select_fusion.1), kind=kLoop, calls=%fused_computation.39 | loop fusion | flops 2031616 | bytes 4456960 | tf_op jit(solution)/shard_map/reduce_sum | solution.py:34
  173.8 3.4 %collective-permute-start.3 = (f32[2,4,128,64]{2,3,1,0:T(8,128)S(1)}, f32[2,4,128,64]{2,3,1,0:T(8,128)S(1)}, u32[]{:S(2)}, u32[]{:S(2)}) collective-permute-start(f32[2,4,128,64]{2,3,1,0:T(8,128)S(1)} %get-tuple-element.148), channel_id=1, source_target_pairs={{0,16},{16,32},{32,48},{48,0},{1,17},{17,33},{33,49},{49,1},{2,18}... | collective-permute-start | bytes 786440 | tf_op jit(solution)/shard_map/ppermute | solution.py:47
  177.2 4.6 %collective-permute-start.4 = (f32[2,4,128,64]{2,3,1,0:T(8,128)S(1)}, f32[2,4,128,64]{2,3,1,0:T(8,128)}, u32[]{:S(2)}, u32[]{:S(2)}) collective-permute-start(f32[2,4,128,64]{2,3,1,0:T(8,128)S(1)} %get-tuple-element.149), channel_id=1, source_target_pairs={{0,32},{16,48},{32,0},{48,16},{1,33},{17,49},{33,1},{49,17},{2,34}... | collective-permute-start | bytes 786440 | tf_op jit(solution)/shard_map/ppermute | solution.py:47
  181.8 3.4 %collective-permute-start.5 = (f32[2,4,128,64]{2,3,1,0:T(8,128)S(1)}, f32[2,4,128,64]{2,3,1,0:T(8,128)S(1)}, u32[]{:S(2)}, u32[]{:S(2)}) collective-permute-start(f32[2,4,128,64]{2,3,1,0:T(8,128)S(1)} %get-tuple-element.150), channel_id=1, source_target_pairs={{0,48},{16,0},{32,16},{48,32},{1,49},{17,1},{33,17},{49,33},{2,50}... | collective-permute-start | bytes 786440 | tf_op jit(solution)/shard_map/ppermute | solution.py:47
  185.2 2.2 %while.16 = (s32[]{:T(128)}, f32[2,128,8,64]{1,3,2,0:T(8,128)S(1)}, f32[2,128,128]{2,1,0:T(8,128)S(1)}, f32[2,128,128]{2,1,0:T(8,128)S(1)}, bf16[2,128,8,64]{1,3...) while((s32[]{:T(128)}, f32[2,128,8,64]{1,3,2,0:T(8,128)S(1)}, ...), condition=%wide.region_3.4_spmd, body=%wide.region_1.3_spmd.sunk | while | flops 43515904 | bytes 1224821 | solution.py:137
  187.7 3.9 %collective-permute-done.4 = f32[2,4,128,64]{2,3,1,0:T(8,128)} collective-permute-done((f32[2,4,128,64]{2,3,1,0:T(8,128)S(1)}, f32[2,4,128,64]{2,3,1,0:T(8,128)}, u32[]{:S(2)}, u32[]{:S(2)}) %collective-permute-start.4) | collective-permute-done | bytes 262176 | tf_op jit(solution)/shard_map/ppermute | solution.py:47
  191.6 1.5 collective-permute-done.5
  193.8 1.2 pad_maximum_fusion.2
  195.0 0.7 gather_fusion.1
  196.8 1.0 fusion.34
  197.8 0.7 copy.90
  198.5 1.0 fusion.35
  200.2 0.8 copy.88
  (135 shorter events, 14.4 us)
Async XLA Ops:
  7.2 162.2 %all-gather.3.cloned.1.call-start = ((), (), s32[]{:S(2)}) async-start(), calls=%async_computation | async-start | bytes 8912896 | tf_op jit(solution)/shard_map/all_gather | solution.py:75
  8.5 5.2 %copy-start.4 = (f32[128,16]{0,1:T(8,128)}, f32[128,16]{0,1:T(8,128)S(1)}, u32[]{:S(2)}) copy-start(f32[128,16]{0,1:T(8,128)S(1)} %get-tuple-element.156) | copy-start | bytes 24580
  14.1 16.9 %collective-permute-start = (f32[2,4,136,64]{2,3,1,0:T(8,128)S(1)}, f32[2,4,136,64]{2,3,1,0:T(8,128)S(1)}, u32[]{:S(2)}, u32[]{:S(2)}) collective-permute-start(f32[2,4,136,64]{2,3,1,0:T(8,128)S(1)} %get-tuple-element.144), channel_id=1, source_target_pairs={{0,16},{16,32},{32,48},{48,0},{1,17},{17,33},{33,49},{49,1},{2,18}... | collective-permute-start | bytes 835592 | tf_op jit(solution)/shard_map/ppermute | solution.py:47
  17.5 25.6 %collective-permute-start.1 = (f32[2,4,136,64]{2,3,1,0:T(8,128)S(1)}, f32[2,4,136,64]{2,3,1,0:T(8,128)S(1)}, u32[]{:S(2)}, u32[]{:S(2)}) collective-permute-start(f32[2,4,136,64]{2,3,1,0:T(8,128)S(1)} %get-tuple-element.143), channel_id=1, source_target_pairs={{0,32},{16,48},{32,0},{48,16},{1,33},{17,49},{33,1},{49,17},{2,34}... | collective-permute-start | bytes 835592 | tf_op jit(solution)/shard_map/ppermute | solution.py:47
  22.1 22.5 %collective-permute-start.2 = (f32[2,4,136,64]{2,3,1,0:T(8,128)S(1)}, f32[2,4,136,64]{2,3,1,0:T(8,128)S(1)}, u32[]{:S(2)}, u32[]{:S(2)}) collective-permute-start(f32[2,4,136,64]{2,3,1,0:T(8,128)S(1)} %get-tuple-element.142), channel_id=1, source_target_pairs={{0,48},{16,0},{32,16},{48,32},{1,49},{17,1},{33,17},{49,33},{2,50}... | collective-permute-start | bytes 835592 | tf_op jit(solution)/shard_map/ppermute | solution.py:47
  25.5 21.3 %copy-start.8 = (pred[4]{0:T(512)(128)(4,1)}, pred[4]{0:T(512)(128)(4,1)S(1)}, u32[]{:S(2)}) copy-start(pred[4]{0:T(512)(128)(4,1)S(1)} %compare_and_fusion) | copy-start | bytes 16
  25.5 23.4 %copy-start.13 = (pred[4]{0:T(512)(128)(4,1)}, pred[4]{0:T(512)(128)(4,1)S(1)}, u32[]{:S(2)}) copy-start(pred[4]{0:T(512)(128)(4,1)S(1)} %iota_compare_fusion.10) | copy-start | bytes 16
  25.6 23.4 %copy-start.14 = (pred[4]{0:T(512)(128)(4,1)}, pred[4]{0:T(512)(128)(4,1)S(1)}, u32[]{:S(2)}) copy-start(pred[4]{0:T(512)(128)(4,1)S(1)} %iota_compare_fusion.11) | copy-start | bytes 16
  25.6 23.4 %copy-start.12 = (pred[4]{0:T(512)(128)(4,1)}, pred[4]{0:T(512)(128)(4,1)S(1)}, u32[]{:S(2)}) copy-start(pred[4]{0:T(512)(128)(4,1)S(1)} %iota_compare_fusion.2) | copy-start | bytes 16
  25.6 23.4 %copy-start.11 = (pred[4]{0:T(512)(128)(4,1)}, pred[4]{0:T(512)(128)(4,1)S(1)}, u32[]{:S(2)}) copy-start(pred[4]{0:T(512)(128)(4,1)S(1)} %iota_compare_fusion.3) | copy-start | bytes 16
  25.6 23.4 %copy-start.10 = (pred[4]{0:T(512)(128)(4,1)}, pred[4]{0:T(512)(128)(4,1)S(1)}, u32[]{:S(2)}) copy-start(pred[4]{0:T(512)(128)(4,1)S(1)} %iota_compare_fusion.4) | copy-start | bytes 16
  25.7 23.3 %copy-start.16 = (pred[4]{0:T(512)(128)(4,1)}, pred[4]{0:T(512)(128)(4,1)S(1)}, u32[]{:S(2)}) copy-start(pred[4]{0:T(512)(128)(4,1)S(1)} %iota_compare_fusion.8) | copy-start | bytes 16
  25.7 23.3 %copy-start.15 = (pred[4]{0:T(512)(128)(4,1)}, pred[4]{0:T(512)(128)(4,1)S(1)}, u32[]{:S(2)}) copy-start(pred[4]{0:T(512)(128)(4,1)S(1)} %iota_compare_fusion.9) | copy-start | bytes 16
  25.7 19.0 %copy-start.7 = (s32[1024]{0:T(1024)}, s32[1024]{0:T(1024)S(1)}, u32[]{:S(2)}) copy-start(s32[1024]{0:T(1024)S(1)} %pad_clamp_fusion) | copy-start | bytes 12292
  48.7 5.2 %copy-start = (bf16[1,128,128]{2,1,0:T(8,128)(2,1)S(1)}, bf16[1,128,128]{2,1,0:T(8,128)(2,1)}, u32[]{:S(2)}) copy-start(bf16[1,128,128]{2,1,0:T(8,128)(2,1)} %param.13) | copy-start | bytes 98308
  48.7 5.2 %copy-start.1 = (bf16[1,128,128]{2,1,0:T(8,128)(2,1)S(1)}, bf16[1,128,128]{2,1,0:T(8,128)(2,1)}, u32[]{:S(2)}) copy-start(bf16[1,128,128]{2,1,0:T(8,128)(2,1)} %param.14) | copy-start | bytes 98308
  77.0 0.6 copy-start.17
  77.0 0.7 copy-start.18
  77.0 0.7 copy-start.19
  77.0 0.7 copy-start.22
  77.1 93.4 %copy-start.20 = (pred[16]{0:T(512)(128)(4,1)S(1)}, pred[16]{0:T(512)(128)(4,1)}, u32[]{:S(2)}) copy-start(pred[16]{0:T(512)(128)(4,1)} %iota_compare_fusion.7) | copy-start | bytes 52
  77.1 93.4 %copy-start.21 = (pred[16]{0:T(512)(128)(4,1)S(1)}, pred[16]{0:T(512)(128)(4,1)}, u32[]{:S(2)}) copy-start(pred[16]{0:T(512)(128)(4,1)} %iota_compare_fusion.1) | copy-start | bytes 52
  170.8 2.8 %copy-start.6 = (f32[4,4]{1,0:T(4,128)S(1)}, f32[4,4]{1,0:T(4,128)}, u32[]{:S(2)}) copy-start(f32[4,4]{1,0:T(4,128)} %pad_maximum_fusion.6) | copy-start | bytes 196
  173.8 13.9 %collective-permute-start.3 = (f32[2,4,128,64]{2,3,1,0:T(8,128)S(1)}, f32[2,4,128,64]{2,3,1,0:T(8,128)S(1)}, u32[]{:S(2)}, u32[]{:S(2)}) collective-permute-start(f32[2,4,128,64]{2,3,1,0:T(8,128)S(1)} %get-tuple-element.148), channel_id=1, source_target_pairs={{0,16},{16,32},{32,48},{48,0},{1,17},{17,33},{33,49},{49,1},{2,18}... | collective-permute-start | bytes 786440 | tf_op jit(solution)/shard_map/ppermute | solution.py:47
  177.2 14.4 %collective-permute-start.4 = (f32[2,4,128,64]{2,3,1,0:T(8,128)S(1)}, f32[2,4,128,64]{2,3,1,0:T(8,128)}, u32[]{:S(2)}, u32[]{:S(2)}) collective-permute-start(f32[2,4,128,64]{2,3,1,0:T(8,128)S(1)} %get-tuple-element.149), channel_id=1, source_target_pairs={{0,32},{16,48},{32,0},{48,16},{1,33},{17,49},{33,1},{49,17},{2,34}... | collective-permute-start | bytes 786440 | tf_op jit(solution)/shard_map/ppermute | solution.py:47
  181.8 11.3 %collective-permute-start.5 = (f32[2,4,128,64]{2,3,1,0:T(8,128)S(1)}, f32[2,4,128,64]{2,3,1,0:T(8,128)S(1)}, u32[]{:S(2)}, u32[]{:S(2)}) collective-permute-start(f32[2,4,128,64]{2,3,1,0:T(8,128)S(1)} %get-tuple-element.150), channel_id=1, source_target_pairs={{0,48},{16,0},{32,16},{48,32},{1,49},{17,1},{33,17},{49,33},{2,50}... | collective-permute-start | bytes 786440 | tf_op jit(solution)/shard_map/ppermute | solution.py:47
  187.7 5.4 %copy-start.2 = (f32[2,4,128,64]{2,3,1,0:T(8,128)}, f32[2,4,128,64]{2,3,1,0:T(8,128)S(1)}, u32[]{:S(2)}) copy-start(f32[2,4,128,64]{2,3,1,0:T(8,128)S(1)} %collective-permute-done.3) | copy-start | bytes 786436
  193.1 0.7 copy-start.3
  195.0 0.8 copy-start.9
  195.9 0.7 copy-start.5
Sparse Core Ops, SparseCore 0:
  51.8 117.4 all-gather.2

commit v4 on v3

--- a/solution.py
+++ b/solution.py
@@ -51,6 +51,34 @@
 def all_weights(p, lower):
     rows = [lower_weights(p, x) if lower else upper_weights(p, x) for x in range(p.shape[0])]
     return jnp.stack(rows)
+
+
+def z_scan(own, axis, forward):
+    count, index = lax.axis_size(axis), lax.axis_index(axis)
+    n = own.shape[1] - 8
+    row = jnp.arange(own.shape[1])[None, :, None]
+    held = own
+    entry = jnp.where(row < n, 0.0, 1.0) * jnp.ones_like(own)
+    shift = 1
+    while shift < count:
+        if forward:
+            pairs = [(i, i + shift) for i in range(count - shift)]
+            valid = index >= shift
+        else:
+            pairs = [(i, i - shift) for i in range(shift, count)]
+            valid = index + shift < count
+        got = lax.ppermute(held, axis, pairs)
+        got = jnp.where(valid, got, jnp.where(row < n, 0.0, 1.0))
+        got_state, got_pass = got[:, :n], got[:, n:n + 1, :1]
+
+        def merge(mine):
+            mine_pass = mine[:, n:n + 1, :1]
+            state = mine[:, :n] + mine_pass * got_state
+            return jnp.concatenate([state, mine[:, n:] * got_pass], axis=1)
+
+        held, entry = merge(held), merge(entry)
+        shift *= 2
+    return entry[:, :n]
 
 
 def chain_states(passage, fwd_local, back_local):
@@ -72,10 +100,9 @@
     lead_f = jnp.stack([jnp.prod(jnp.where(k < x, group, 1.0), axis=0) for x in range(nx)])
     lead_b = jnp.stack([jnp.prod(jnp.where(k > x, group, 1.0), axis=0) for x in range(nx)])
     span = jnp.prod(group, axis=0)
-    rows = lax.all_gather(with_scalars(jnp.stack([agg_f, agg_b]), span), "cz")
-    spans = rows[:, 0, :, n, 0]
-    z_f = weighted(lower_weights(spans, zi), rows[:, 0, :, :n])
-    z_b = weighted(upper_weights(spans, zi), rows[:, 1, :, :n])
+    own = with_scalars(jnp.stack([agg_f, agg_b]), span)
+    z_f = z_scan(own[0], "cz", True)
+    z_b = z_scan(own[1], "cz", False)
     prior = local_f + lead_f[:, :, None, None] * z_f[None]
     incoming = local_b + lead_b[:, :, None, None] * z_b[None]
     back = exchange(jnp.stack([incoming, prior], axis=1), "cx")

time: 211 us -> 209 us (level)
  the two profiles are of different devices: /device:TPU:56 before, /device:TPU:67 now
where the time goes in v4:
time: 209 us; the launch traced here: 208 us
  waiting for transfers between devices  109 us (52%)
  starting transfers between devices  59.5 us (28%)
  other arithmetic  15.5 us (7%)
  local copies, waits for them, and re-layouts  15 us (7%)
  matrix products  7.03 us (3%)
    ppermute x8, waiting for transfers between devices, z_scan(): got = lax.ppermute(held, axis, pairs)  83.1 us
    ppermute x8, starting transfers between devices, z_scan(): got = lax.ppermute(held, axis, pairs)  41.3 us
    ppermute x6, waiting for transfers between devices, exchange(): lax.ppermute(send, axis, [(i, (i + shift) % count) for i in range(count)])  25.9 us
    ppermute x6, starting transfers between devices, exchange(): lax.ppermute(send, axis, [(i, (i + shift) % count) for i in range(count)])  18.2 us
    unnamed x99, local copies, waits for them, and re-layouts  5.99 us
  transfers between devices with their start and end apart: 14, of which 11 were waited for; matrix products, arithmetic and copies ran while one was open for 5% of the time, Pallas kernels for 0%

profile of v4, /device:TPU:67, one launch (start us, length us, event | category | flops | bytes accessed | tf_op | source)
XLA Modules:
  0.0 208.0 jit_solution(14124112910101711979)
XLA Ops:
  0.7 1.0 reduce_window_sum.11
  2.0 1.1 copy.83
  3.1 0.8 bitcast_convert_fusion.1
  3.9 1.1 copy.84
  5.0 0.8 bitcast_convert_fusion
  7.3 1.2 dynamic-slice_select_fusion
  8.6 3.1 %collective-permute-start = (f32[2,4,136,64]{2,3,1,0:T(8,128)}, f32[2,4,136,64]{2,3,1,0:T(8,128)}, u32[]{:S(2)}, u32[]{:S(2)}) collective-permute-start(f32[2,4,136,64]{2,3,1,0:T(8,128)} %get-tuple-element.149), channel_id=1, source_target_pairs={{0,16},{16,32},{32,48},{48,0},{1,17},{17,33},{33,49},{49,1},{2,18}... | collective-permute-start | bytes 835592 | tf_op jit(solution)/shard_map/ppermute | solution.py:47
  11.7 2.7 %collective-permute-start.1 = (f32[2,4,136,64]{2,3,1,0:T(8,128)}, f32[2,4,136,64]{2,3,1,0:T(8,128)}, u32[]{:S(2)}, u32[]{:S(2)}) collective-permute-start(f32[2,4,136,64]{2,3,1,0:T(8,128)} %get-tuple-element.148), channel_id=1, source_target_pairs={{0,32},{16,48},{32,0},{48,16},{1,33},{17,49},{33,1},{49,17},{2,34}... | collective-permute-start | bytes 835592 | tf_op jit(solution)/shard_map/ppermute | solution.py:47
  14.4 3.8 %collective-permute-start.2 = (f32[2,4,136,64]{2,3,1,0:T(8,128)}, f32[2,4,136,64]{2,3,1,0:T(8,128)}, u32[]{:S(2)}, u32[]{:S(2)}) collective-permute-start(f32[2,4,136,64]{2,3,1,0:T(8,128)} %get-tuple-element.147), channel_id=1, source_target_pairs={{0,48},{16,0},{32,16},{48,32},{1,49},{17,1},{33,17},{49,33},{2,50}... | collective-permute-start | bytes 835592 | tf_op jit(solution)/shard_map/ppermute | solution.py:47
  20.6 0.6 pad.30.clone
  21.3 2.3 %collective-permute-done = f32[2,4,136,64]{2,3,1,0:T(8,128)} collective-permute-done((f32[2,4,136,64]{2,3,1,0:T(8,128)}, f32[2,4,136,64]{2,3,1,0:T(8,128)}, u32[]{:S(2)}, u32[]{:S(2)}) %collective-permute-start) | collective-permute-done | bytes 278560 | tf_op jit(solution)/shard_map/ppermute | solution.py:47
  23.6 4.4 %collective-permute-done.1 = f32[2,4,136,64]{2,3,1,0:T(8,128)} collective-permute-done((f32[2,4,136,64]{2,3,1,0:T(8,128)}, f32[2,4,136,64]{2,3,1,0:T(8,128)}, u32[]{:S(2)}, u32[]{:S(2)}) %collective-permute-start.1) | collective-permute-done | bytes 278560 | tf_op jit(solution)/shard_map/ppermute | solution.py:47
  27.9 12.6 %collective-permute-done.2 = f32[2,4,136,64]{2,3,1,0:T(8,128)} collective-permute-done((f32[2,4,136,64]{2,3,1,0:T(8,128)}, f32[2,4,136,64]{2,3,1,0:T(8,128)}, u32[]{:S(2)}, u32[]{:S(2)}) %collective-permute-start.2) | collective-permute-done | bytes 278560 | tf_op jit(solution)/shard_map/ppermute | solution.py:47
  40.5 1.5 pad_maximum_fusion.1
  42.0 2.0 gather_fusion
  44.1 1.9 broadcast_select_fusion
  46.2 0.9 slice_bitcast_fusion
  47.1 1.3 fusion.61
  49.3 4.0 %collective-permute-start.7 = (f32[4,136,64]{1,2,0:T(8,128)S(1)}, f32[4,136,64]{1,2,0:T(8,128)S(1)}, u32[]{:S(2)}, u32[]{:S(2)}) collective-permute-start(f32[4,136,64]{1,2,0:T(8,128)S(1)} %get-tuple-element.156), channel_id=1, source_target_pairs={{0,64},{64,128},{128,192},{192,256},{256,320},{320,384},{384,448},... | collective-permute-start | bytes 417800 | tf_op jit(solution)/shard_map/ppermute | solution.py:70
  53.4 1.9 collective-permute-start.3
  56.4 0.7 pad_maximum_fusion.11
  57.7 0.8 collective-permute-done.7
  58.9 6.9 %collective-permute-start.8 = (f32[4,136,64]{1,2,0:T(8,128)S(1)}, f32[4,136,64]{1,2,0:T(8,128)S(1)}, u32[]{:S(2)}, u32[]{:S(2)}) collective-permute-start(f32[4,136,64]{1,2,0:T(8,128)S(1)} %pad_maximum_fusion.7), channel_id=1, source_target_pairs={{0,128},{64,192},{128,256},{192,320},{256,384},{320,448},{384,512}... | collective-permute-start | bytes 417800 | tf_op jit(solution)/shard_map/ppermute | solution.py:70
  66.0 9.5 %collective-permute-done.8 = f32[4,136,64]{1,2,0:T(8,128)S(1)} collective-permute-done((f32[4,136,64]{1,2,0:T(8,128)S(1)}, f32[4,136,64]{1,2,0:T(8,128)S(1)}, u32[]{:S(2)}, u32[]{:S(2)}) %collective-permute-start.8) | collective-permute-done | bytes 139296 | tf_op jit(solution)/shard_map/ppermute | solution.py:70
  75.9 1.3 collective-permute-start.4
  77.6 8.9 %collective-permute-start.9 = (f32[4,136,64]{1,2,0:T(8,128)S(1)}, f32[4,136,64]{1,2,0:T(8,128)S(1)}, u32[]{:S(2)}, u32[]{:S(2)}) collective-permute-start(f32[4,136,64]{1,2,0:T(8,128)S(1)} %pad_maximum_fusion.8), channel_id=1, source_target_pairs={{0,256},{64,320},{128,384},{192,448},{256,512},{320,576},{384,640}... | collective-permute-start | bytes 417800 | tf_op jit(solution)/shard_map/ppermute | solution.py:70
  87.2 8.5 %collective-permute-done.9 = f32[4,136,64]{1,2,0:T(8,128)S(1)} collective-permute-done((f32[4,136,64]{1,2,0:T(8,128)S(1)}, f32[4,136,64]{1,2,0:T(8,128)S(1)}, u32[]{:S(2)}, u32[]{:S(2)}) %collective-permute-start.9) | collective-permute-done | bytes 139296 | tf_op jit(solution)/shard_map/ppermute | solution.py:70
  96.0 1.3 collective-permute-start.5
  97.8 15.7 %collective-permute-start.10 = (f32[4,136,64]{1,2,0:T(8,128)S(1)}, f32[4,136,64]{1,2,0:T(8,128)S(1)}, u32[]{:S(2)}, u32[]{:S(2)}) collective-permute-start(f32[4,136,64]{1,2,0:T(8,128)S(1)} %pad_maximum_fusion.9), channel_id=1, source_target_pairs={{0,512},{64,576},{128,640},{192,704},{256,768},{320,832},{384,896}... | collective-permute-start | bytes 417800 | tf_op jit(solution)/shard_map/ppermute | solution.py:70
  114.0 1.3 collective-permute-start.6
  115.6 1.2 collective-permute-done.10
  116.7 62.8 %collective-permute-done.6 = f32[4,136,64]{1,2,0:T(8,128)S(1)} collective-permute-done((f32[4,136,64]{1,2,0:T(8,128)S(1)}, f32[4,136,64]{1,2,0:T(8,128)S(1)}, u32[]{:S(2)}, u32[]{:S(2)}) %collective-permute-start.6) | collective-permute-done | bytes 139296 | tf_op jit(solution)/shard_map/ppermute | solution.py:70
  179.5 0.7 fusion.50
  180.5 1.9 collective-permute-start.11
  182.5 2.6 %collective-permute-start.12 = (f32[2,4,128,64]{2,3,1,0:T(8,128)S(1)}, f32[2,4,128,64]{2,3,1,0:T(8,128)S(1)}, u32[]{:S(2)}, u32[]{:S(2)}) collective-permute-start(f32[2,4,128,64]{2,3,1,0:T(8,128)S(1)} %get-tuple-element.154), channel_id=1, source_target_pairs={{0,32},{16,48},{32,0},{48,16},{1,33},{17,49},{33,1},{49,17},{2,34}... | collective-permute-start | bytes 786440 | tf_op jit(solution)/shard_map/ppermute | solution.py:47
  185.1 4.0 %collective-permute-start.13 = (f32[2,4,128,64]{2,3,1,0:T(8,128)S(1)}, f32[2,4,128,64]{2,3,1,0:T(8,128)S(1)}, u32[]{:S(2)}, u32[]{:S(2)}) collective-permute-start(f32[2,4,128,64]{2,3,1,0:T(8,128)S(1)} %get-tuple-element.155), channel_id=1, source_target_pairs={{0,48},{16,0},{32,16},{48,32},{1,49},{17,1},{33,17},{49,33},{2,50}... | collective-permute-start | bytes 786440 | tf_op jit(solution)/shard_map/ppermute | solution.py:47
  189.2 3.6 %while.16 = (s32[]{:T(128)}, f32[2,128,8,64]{1,3,2,0:T(8,128)}, f32[2,128,128]{2,1,0:T(8,128)S(1)}, f32[2,128,128]{2,1,0:T(8,128)S(1)}, bf16[2,128,8,64]{1,3,2,0...) while((s32[]{:T(128)}, f32[2,128,8,64]{1,3,2,0:T(8,128)}, ...), condition=%wide.region_3.4_spmd, body=%wide.region_1.3_spmd.sunk | while | flops 43515904 | bytes 1224821 | solution.py:164
  189.2 1.1 fusion.96
  191.1 1.1 fusion.96
  193.3 6.4 %collective-permute-done.13 = f32[2,4,128,64]{2,3,1,0:T(8,128)S(1)} collective-permute-done((f32[2,4,128,64]{2,3,1,0:T(8,128)S(1)}, f32[2,4,128,64]{2,3,1,0:T(8,128)S(1)}, u32[]{:S(2)}, u32[]{:S(2)}) %collective-permute-start.13) | collective-permute-done | bytes 262176 | tf_op jit(solution)/shard_map/ppermute | solution.py:47
  199.7 0.7 copy-done.5
  200.4 1.1 pad_maximum_fusion.2
  201.5 0.7 gather_fusion.1
  203.7 1.0 fusion.30
  204.7 0.7 copy.94
  205.4 1.0 fusion.31
  206.4 0.7 copy.93
  207.1 0.8 copy.92
  (230 shorter events, 13.6 us)
Async XLA Ops:
  7.3 13.8 %copy-start.1 = (bf16[1,128,128]{2,1,0:T(8,128)(2,1)S(1)}, bf16[1,128,128]{2,1,0:T(8,128)(2,1)}, u32[]{:S(2)}) copy-start(bf16[1,128,128]{2,1,0:T(8,128)(2,1)} %param.13) | copy-start | bytes 98308
  7.3 13.8 %copy-start.3 = (bf16[1,128,128]{2,1,0:T(8,128)(2,1)S(1)}, bf16[1,128,128]{2,1,0:T(8,128)(2,1)}, u32[]{:S(2)}) copy-start(bf16[1,128,128]{2,1,0:T(8,128)(2,1)} %param.14) | copy-start | bytes 98308
  8.6 15.0 %collective-permute-start = (f32[2,4,136,64]{2,3,1,0:T(8,128)}, f32[2,4,136,64]{2,3,1,0:T(8,128)}, u32[]{:S(2)}, u32[]{:S(2)}) collective-permute-start(f32[2,4,136,64]{2,3,1,0:T(8,128)} %get-tuple-element.149), channel_id=1, source_target_pairs={{0,16},{16,32},{32,48},{48,0},{1,17},{17,33},{33,49},{49,1},{2,18}... | collective-permute-start | bytes 835592 | tf_op jit(solution)/shard_map/ppermute | solution.py:47
  11.7 16.2 %collective-permute-start.1 = (f32[2,4,136,64]{2,3,1,0:T(8,128)}, f32[2,4,136,64]{2,3,1,0:T(8,128)}, u32[]{:S(2)}, u32[]{:S(2)}) collective-permute-start(f32[2,4,136,64]{2,3,1,0:T(8,128)} %get-tuple-element.148), channel_id=1, source_target_pairs={{0,32},{16,48},{32,0},{48,16},{1,33},{17,49},{33,1},{49,17},{2,34}... | collective-permute-start | bytes 835592 | tf_op jit(solution)/shard_map/ppermute | solution.py:47
  14.4 26.0 %collective-permute-start.2 = (f32[2,4,136,64]{2,3,1,0:T(8,128)}, f32[2,4,136,64]{2,3,1,0:T(8,128)}, u32[]{:S(2)}, u32[]{:S(2)}) collective-permute-start(f32[2,4,136,64]{2,3,1,0:T(8,128)} %get-tuple-element.147), channel_id=1, source_target_pairs={{0,48},{16,0},{32,16},{48,32},{1,49},{17,1},{33,17},{49,33},{2,50}... | collective-permute-start | bytes 835592 | tf_op jit(solution)/shard_map/ppermute | solution.py:47
  18.3 25.8 %copy-start.21 = (pred[4]{0:T(512)(128)(4,1)}, pred[4]{0:T(512)(128)(4,1)S(1)}, u32[]{:S(2)}) copy-start(pred[4]{0:T(512)(128)(4,1)S(1)} %compare_and_fusion) | copy-start | bytes 16
  18.3 28.8 %copy-start.36 = (pred[4]{0:T(512)(128)(4,1)}, pred[4]{0:T(512)(128)(4,1)S(1)}, u32[]{:S(2)}) copy-start(pred[4]{0:T(512)(128)(4,1)S(1)} %iota_compare_fusion.1) | copy-start | bytes 16
  18.3 28.8 %copy-start.34 = (pred[4]{0:T(512)(128)(4,1)}, pred[4]{0:T(512)(128)(4,1)S(1)}, u32[]{:S(2)}) copy-start(pred[4]{0:T(512)(128)(4,1)S(1)} %iota_compare_fusion.2) | copy-start | bytes 16
  18.3 28.8 %copy-start.30 = (pred[4]{0:T(512)(128)(4,1)}, pred[4]{0:T(512)(128)(4,1)S(1)}, u32[]{:S(2)}) copy-start(pred[4]{0:T(512)(128)(4,1)S(1)} %iota_compare_fusion.3) | copy-start | bytes 16
  18.4 28.7 %copy-start.28 = (pred[4]{0:T(512)(128)(4,1)}, pred[4]{0:T(512)(128)(4,1)S(1)}, u32[]{:S(2)}) copy-start(pred[4]{0:T(512)(128)(4,1)S(1)} %iota_compare_fusion.6) | copy-start | bytes 16
  18.4 28.7 %copy-start.26 = (pred[4]{0:T(512)(128)(4,1)}, pred[4]{0:T(512)(128)(4,1)S(1)}, u32[]{:S(2)}) copy-start(pred[4]{0:T(512)(128)(4,1)S(1)} %iota_compare_fusion.7) | copy-start | bytes 16
  18.4 28.7 %copy-start.24 = (pred[4]{0:T(512)(128)(4,1)}, pred[4]{0:T(512)(128)(4,1)S(1)}, u32[]{:S(2)}) copy-start(pred[4]{0:T(512)(128)(4,1)S(1)} %iota_compare_fusion.8) | copy-start | bytes 16
  19.5 22.5 %copy-start.20 = (s32[1024]{0:T(1024)}, s32[1024]{0:T(1024)S(1)}, u32[]{:S(2)}) copy-start(s32[1024]{0:T(1024)S(1)} %pad_clamp_fusion) | copy-start | bytes 12292
  19.5 27.6 %copy-start.32 = (pred[4]{0:T(512)(128)(4,1)}, pred[4]{0:T(512)(128)(4,1)S(1)}, u32[]{:S(2)}) copy-start(pred[4]{0:T(512)(128)(4,1)S(1)} %iota_compare_fusion.9) | copy-start | bytes 16
  48.9 7.1 %copy-start.33 = (pred[4]{0:T(512)(128)(4,1)S(1)}, pred[4]{0:T(512)(128)(4,1)}, u32[]{:S(2)}) copy-start(pred[4]{0:T(512)(128)(4,1)} %copy-done.32) | copy-start | bytes 16
  48.9 7.1 %copy-start.15 = (f32[4,4]{1,0:T(4,128)S(1)}, f32[4,4]{1,0:T(4,128)}, u32[]{:S(2)}) copy-start(f32[4,4]{1,0:T(4,128)} %get-tuple-element.169) | copy-start | bytes 196
  48.9 7.2 %copy-start.29 = (pred[4]{0:T(512)(128)(4,1)S(1)}, pred[4]{0:T(512)(128)(4,1)}, u32[]{:S(2)}) copy-start(pred[4]{0:T(512)(128)(4,1)} %copy-done.28) | copy-start | bytes 16
  49.0 7.2 %copy-start.14 = (f32[4,4]{1,0:T(4,128)S(1)}, f32[4,4]{1,0:T(4,128)}, u32[]{:S(2)}) copy-start(f32[4,4]{1,0:T(4,128)} %get-tuple-element.171) | copy-start | bytes 196
  49.0 7.3 %copy-start.27 = (pred[4]{0:T(512)(128)(4,1)S(1)}, pred[4]{0:T(512)(128)(4,1)}, u32[]{:S(2)}) copy-start(pred[4]{0:T(512)(128)(4,1)} %copy-done.26) | copy-start | bytes 16
  49.0 7.3 %copy-start.13 = (f32[4,4]{1,0:T(4,128)S(1)}, f32[4,4]{1,0:T(4,128)}, u32[]{:S(2)}) copy-start(f32[4,4]{1,0:T(4,128)} %get-tuple-element.173) | copy-start | bytes 196
  49.0 7.4 %copy-start.25 = (pred[4]{0:T(512)(128)(4,1)S(1)}, pred[4]{0:T(512)(128)(4,1)}, u32[]{:S(2)}) copy-start(pred[4]{0:T(512)(128)(4,1)} %copy-done.24) | copy-start | bytes 16
  49.0 8.2 %copy-start = (f32[4,4,128,64]{2,3,1,0:T(8,128)S(1)}, f32[4,4,128,64]{2,3,1,0:T(8,128)}, u32[]{:S(2)}) copy-start(f32[4,4,128,64]{2,3,1,0:T(8,128)} %get-tuple-element.144) | copy-start | bytes 1572868
  49.0 8.4 %copy-start.42 = (f32[4]{0:T(128)S(1)}, f32[4]{0:T(128)}, u32[]{:S(2)}) copy-start(f32[4]{0:T(128)} %get-tuple-element.130) | copy-start | bytes 52
  49.0 8.4 %copy-start.43 = (f32[4]{0:T(128)S(1)}, f32[4]{0:T(128)}, u32[]{:S(2)}) copy-start(f32[4]{0:T(128)} %get-tuple-element.162) | copy-start | bytes 52
  49.0 8.4 %copy-start.44 = (f32[4]{0:T(128)S(1)}, f32[4]{0:T(128)}, u32[]{:S(2)}) copy-start(f32[4]{0:T(128)} %get-tuple-element.164) | copy-start | bytes 52
  49.0 8.4 %copy-start.46 = (f32[4]{0:T(128)S(1)}, f32[4]{0:T(128)}, u32[]{:S(2)}) copy-start(f32[4]{0:T(128)} %pad.26.clone) | copy-start | bytes 52
  49.1 9.4 %copy-start.11 = (f32[136]{0:T(256)S(1)}, f32[136]{0:T(256)}, u32[]{:S(2)}) copy-start(f32[136]{0:T(256)} %copy-done.10) | copy-start | bytes 1636
  49.2 16.6 %copy-start.38 = (f32[4]{0:T(128)S(1)}, f32[4]{0:T(128)}, u32[]{:S(2)}) copy-start(f32[4]{0:T(128)} %get-tuple-element.168) | copy-start | bytes 52
  49.2 16.6 %copy-start.39 = (f32[4]{0:T(128)S(1)}, f32[4]{0:T(128)}, u32[]{:S(2)}) copy-start(f32[4]{0:T(128)} %get-tuple-element.170) | copy-start | bytes 52
  49.3 16.6 %copy-start.40 = (f32[4]{0:T(128)S(1)}, f32[4]{0:T(128)}, u32[]{:S(2)}) copy-start(f32[4]{0:T(128)} %get-tuple-element.172) | copy-start | bytes 52
  49.3 16.6 %copy-start.41 = (f32[4]{0:T(128)S(1)}, f32[4]{0:T(128)}, u32[]{:S(2)}) copy-start(f32[4]{0:T(128)} %get-tuple-element.174) | copy-start | bytes 52
  49.3 9.3 %collective-permute-start.7 = (f32[4,136,64]{1,2,0:T(8,128)S(1)}, f32[4,136,64]{1,2,0:T(8,128)S(1)}, u32[]{:S(2)}, u32[]{:S(2)}) collective-permute-start(f32[4,136,64]{1,2,0:T(8,128)S(1)} %get-tuple-element.156), channel_id=1, source_target_pairs={{0,64},{64,128},{128,192},{192,256},{256,320},{320,384},{384,448},... | collective-permute-start | bytes 417800 | tf_op jit(solution)/shard_map/ppermute | solution.py:70
  53.4 12.6 %collective-permute-start.3 = (f32[4,136,64]{1,2,0:T(8,128)S(1)}, f32[4,136,64]{1,2,0:T(8,128)S(1)}, u32[]{:S(2)}, u32[]{:S(2)}) collective-permute-start(f32[4,136,64]{1,2,0:T(8,128)S(1)} %get-tuple-element.157), channel_id=1, source_target_pairs={{64,0},{128,64},{192,128},{256,192},{320,256},{384,320},{448,384},... | collective-permute-start | bytes 417800 | tf_op jit(solution)/shard_map/ppermute | solution.py:70
  57.7 19.7 %copy-start.23 = (f32[8]{0:T(128)S(1)}, f32[8]{0:T(128)}, u32[]{:S(2)}) copy-start(f32[8]{0:T(128)} %slice_bitcast_fusion.4) | copy-start | bytes 100
  58.9 36.8 %copy-start.12 = (f32[136]{0:T(256)S(1)}, f32[136]{0:T(256)}, u32[]{:S(2)}) copy-start(f32[136]{0:T(256)} %copy-done.10) | copy-start | bytes 1636
  58.9 16.6 %collective-permute-start.8 = (f32[4,136,64]{1,2,0:T(8,128)S(1)}, f32[4,136,64]{1,2,0:T(8,128)S(1)}, u32[]{:S(2)}, u32[]{:S(2)}) collective-permute-start(f32[4,136,64]{1,2,0:T(8,128)S(1)} %pad_maximum_fusion.7), channel_id=1, source_target_pairs={{0,128},{64,192},{128,256},{192,320},{256,384},{320,448},{384,512}... | collective-permute-start | bytes 417800 | tf_op jit(solution)/shard_map/ppermute | solution.py:70
  75.9 11.2 %collective-permute-start.4 = (f32[4,136,64]{1,2,0:T(8,128)S(1)}, f32[4,136,64]{1,2,0:T(8,128)S(1)}, u32[]{:S(2)}, u32[]{:S(2)}) collective-permute-start(f32[4,136,64]{1,2,0:T(8,128)S(1)} %pad_maximum_fusion.4), channel_id=1, source_target_pairs={{128,0},{192,64},{256,128},{320,192},{384,256},{448,320},{512,384}... | collective-permute-start | bytes 417800 | tf_op jit(solution)/shard_map/ppermute | solution.py:70
  77.6 18.1 %collective-permute-start.9 = (f32[4,136,64]{1,2,0:T(8,128)S(1)}, f32[4,136,64]{1,2,0:T(8,128)S(1)}, u32[]{:S(2)}, u32[]{:S(2)}) collective-permute-start(f32[4,136,64]{1,2,0:T(8,128)S(1)} %pad_maximum_fusion.8), channel_id=1, source_target_pairs={{0,256},{64,320},{128,384},{192,448},{256,512},{320,576},{384,640}... | collective-permute-start | bytes 417800 | tf_op jit(solution)/shard_map/ppermute | solution.py:70
  95.8 83.7 %slice-start = ((f32[136]{0:T(256)}), f32[128]{0:T(128)S(1)}, s32[]{:S(2)}) async-start(f32[136]{0:T(256)} %copy-done.10), calls=%async_computation | async-start | bytes 1024 | tf_op jit(solution)/shard_map/slice | solution.py:72
  95.8 83.7 %copy-start.45 = (f32[128]{0:T(128)S(1)}, f32[128]{0:T(128)}, u32[]{:S(2)}) copy-start(f32[128]{0:T(128)} %slice_bitcast_fusion.5) | copy-start | bytes 1540
  96.0 17.6 %collective-permute-start.5 = (f32[4,136,64]{1,2,0:T(8,128)S(1)}, f32[4,136,64]{1,2,0:T(8,128)S(1)}, u32[]{:S(2)}, u32[]{:S(2)}) collective-permute-start(f32[4,136,64]{1,2,0:T(8,128)S(1)} %pad_maximum_fusion.5), channel_id=1, source_target_pairs={{256,0},{320,64},{384,128},{448,192},{512,256},{576,320},{640,384}... | collective-permute-start | bytes 417800 | tf_op jit(solution)/shard_map/ppermute | solution.py:70
  97.8 19.0 %collective-permute-start.10 = (f32[4,136,64]{1,2,0:T(8,128)S(1)}, f32[4,136,64]{1,2,0:T(8,128)S(1)}, u32[]{:S(2)}, u32[]{:S(2)}) collective-permute-start(f32[4,136,64]{1,2,0:T(8,128)S(1)} %pad_maximum_fusion.9), channel_id=1, source_target_pairs={{0,512},{64,576},{128,640},{192,704},{256,768},{320,832},{384,896}... | collective-permute-start | bytes 417800 | tf_op jit(solution)/shard_map/ppermute | solution.py:70
  114.0 65.5 %collective-permute-start.6 = (f32[4,136,64]{1,2,0:T(8,128)S(1)}, f32[4,136,64]{1,2,0:T(8,128)S(1)}, u32[]{:S(2)}, u32[]{:S(2)}) collective-permute-start(f32[4,136,64]{1,2,0:T(8,128)S(1)} %pad_maximum_fusion.6), channel_id=1, source_target_pairs={{512,0},{576,64},{640,128},{704,192},{768,256},{832,320},{896,384}... | collective-permute-start | bytes 417800 | tf_op jit(solution)/shard_map/ppermute | solution.py:70
  180.3 8.8 %copy-start.6 = (f32[2,128,128]{2,1,0:T(8,128)S(1)}, f32[2,128,128]{2,1,0:T(8,128)}, u32[]{:S(2)}) copy-start(f32[2,128,128]{2,1,0:T(8,128)} %custom-call.5) | copy-start | bytes 393220
  180.3 8.8 %copy-start.7 = (f32[2,128,128]{2,1,0:T(8,128)S(1)}, f32[2,128,128]{2,1,0:T(8,128)}, u32[]{:S(2)}) copy-start(f32[2,128,128]{2,1,0:T(8,128)} %custom-call.6) | copy-start | bytes 393220
  180.5 12.5 %collective-permute-start.11 = (f32[2,4,128,64]{2,3,1,0:T(8,128)S(1)}, f32[2,4,128,64]{2,3,1,0:T(8,128)S(1)}, u32[]{:S(2)}, u32[]{:S(2)}) collective-permute-start(f32[2,4,128,64]{2,3,1,0:T(8,128)S(1)} %get-tuple-element.153), channel_id=1, source_target_pairs={{0,16},{16,32},{32,48},{48,0},{1,17},{17,33},{33,49},{49,1},{2,18}... | collective-permute-start | bytes 786440 | tf_op jit(solution)/shard_map/ppermute | solution.py:47
  182.5 10.8 %collective-permute-start.12 = (f32[2,4,128,64]{2,3,1,0:T(8,128)S(1)}, f32[2,4,128,64]{2,3,1,0:T(8,128)S(1)}, u32[]{:S(2)}, u32[]{:S(2)}) collective-permute-start(f32[2,4,128,64]{2,3,1,0:T(8,128)S(1)} %get-tuple-element.154), channel_id=1, source_target_pairs={{0,32},{16,48},{32,0},{48,16},{1,33},{17,49},{33,1},{49,17},{2,34}... | collective-permute-start | bytes 786440 | tf_op jit(solution)/shard_map/ppermute | solution.py:47
  185.1 14.6 %collective-permute-start.13 = (f32[2,4,128,64]{2,3,1,0:T(8,128)S(1)}, f32[2,4,128,64]{2,3,1,0:T(8,128)S(1)}, u32[]{:S(2)}, u32[]{:S(2)}) collective-permute-start(f32[2,4,128,64]{2,3,1,0:T(8,128)S(1)} %get-tuple-element.155), channel_id=1, source_target_pairs={{0,48},{16,0},{32,16},{48,32},{1,49},{17,1},{33,17},{49,33},{2,50}... | collective-permute-start | bytes 786440 | tf_op jit(solution)/shard_map/ppermute | solution.py:47
  (14 other events, 65.6 us)

commit v5 on v4

--- a/solution.py
+++ b/solution.py
@@ -81,33 +81,45 @@
     return entry[:, :n]
 
 
-def chain_states(passage, fwd_local, back_local):
-    nx = lax.axis_size("cx")
-    xi, zi = lax.axis_index("cx"), lax.axis_index("cz")
-    heads, n, width = fwd_local.shape
-    part = heads // nx
-    packed = with_scalars(jnp.stack([fwd_local, back_local]), passage)
-    pieces = jnp.transpose(packed.reshape(2, nx, part, n + 8, width), (1, 0, 2, 3, 4))
-    members = exchange(pieces, "cx")
+def packed(state, scalars):
+    rows = jnp.broadcast_to(scalars[:, None, None], (state.shape[0], 8, state.shape[2]))
+    return jnp.concatenate([state, rows], axis=1)
+
+
+def entry_states(own_f, own_b, axes):
+    axis = axes[0]
+    count = lax.axis_size(axis)
+    heads, n, width = own_f.shape[0], own_f.shape[1] - 8, own_f.shape[2]
+    if len(axes) == 1 or heads % count:
+        whole = tuple(reversed(axes))
+        return z_scan(own_f, whole, True), z_scan(own_b, whole, False)
+    part = heads // count
+    pieces = jnp.stack([own_f, own_b]).reshape(2, count, part, n + 8, width)
+    members = exchange(jnp.transpose(pieces, (1, 0, 2, 3, 4)), axis)
     group = members[:, 0, :, n, 0]
     fwd_all, back_all = members[:, 0, :, :n], members[:, 1, :, :n]
     w_f, w_b = all_weights(group, True), all_weights(group, False)
     local_f = (w_f[:, :, :, None, None] * fwd_all[None]).sum(axis=1)
     local_b = (w_b[:, :, :, None, None] * back_all[None]).sum(axis=1)
-    agg_f = weighted(lower_weights(group, nx), fwd_all)
+    agg_f = weighted(lower_weights(group, count), fwd_all)
     agg_b = weighted(upper_weights(group, -1), back_all)
-    k = jnp.arange(nx)[:, None]
-    lead_f = jnp.stack([jnp.prod(jnp.where(k < x, group, 1.0), axis=0) for x in range(nx)])
-    lead_b = jnp.stack([jnp.prod(jnp.where(k > x, group, 1.0), axis=0) for x in range(nx)])
+    k = jnp.arange(count)[:, None]
+    lead_f = jnp.stack([jnp.prod(jnp.where(k < x, group, 1.0), axis=0) for x in range(count)])
+    lead_b = jnp.stack([jnp.prod(jnp.where(k > x, group, 1.0), axis=0) for x in range(count)])
     span = jnp.prod(group, axis=0)
-    own = with_scalars(jnp.stack([agg_f, agg_b]), span)
-    z_f = z_scan(own[0], "cz", True)
-    z_b = z_scan(own[1], "cz", False)
-    prior = local_f + lead_f[:, :, None, None] * z_f[None]
-    incoming = local_b + lead_b[:, :, None, None] * z_b[None]
-    back = exchange(jnp.stack([incoming, prior], axis=1), "cx")
+    sub_f, sub_b = entry_states(packed(agg_f, span), packed(agg_b, span), axes[1:])
+    full_f = local_f + lead_f[:, :, None, None] * sub_f[None]
+    full_b = local_b + lead_b[:, :, None, None] * sub_b[None]
+    back = exchange(jnp.stack([full_f, full_b], axis=1), axis)
     back = jnp.transpose(back, (1, 0, 2, 3, 4)).reshape(2, heads, n, width)
     return back[0], back[1]
+
+
+def chain_states(passage, fwd_local, back_local):
+    prior, incoming = entry_states(
+        packed(fwd_local, passage), packed(back_local, passage), ("cx", "czl", "czh")
+    )
+    return incoming, prior
 
 
 def block_terms(pieces):
@@ -204,9 +216,11 @@
 def solution(mesh):
     nx = x_extent(mesh)
     shape = mesh.devices.shape
-    devices = mesh.devices.reshape(shape[0] // nx, nx, *shape[1:])
-    mesh = jax.sharding.Mesh(devices, ("cz", "cx", "head", "dp"))
-    ctx = ("cz", "cx")
+    nz = shape[0] // nx
+    low = math.gcd(nz, 4)
+    devices = mesh.devices.reshape(nz // low, low, nx, *shape[1:])
+    mesh = jax.sharding.Mesh(devices, ("czh", "czl", "cx", "head", "dp"))
+    ctx = ("czh", "czl", "cx")
     in_specs = (
         P("dp", ctx, "head"),
         P("dp", ctx, "head"),

time: 209 us -> 174 us (0.83)
  the two profiles are of different devices: /device:TPU:67 before, /device:TPU:56 now
where the time goes in v5:
time: 174 us; the launch traced here: 173 us
  starting transfers between devices  73.3 us (42%)
  waiting for transfers between devices  39.7 us (23%)
  other arithmetic  30.2 us (17%)
  local copies, waits for them, and re-layouts  18 us (10%)
  matrix products  7.03 us (4%)
  between operations  4.48 us (3%)
    ppermute x12, starting transfers between devices, exchange(): lax.ppermute(send, axis, [(i, (i + shift) % count) for i in range(count)])  47.6 us
    ppermute x4, starting transfers between devices, z_scan(): got = lax.ppermute(held, axis, pairs)  25.7 us
    ppermute x12, waiting for transfers between devices, exchange(): lax.ppermute(send, axis, [(i, (i + shift) % count) for i in range(count)])  21.9 us
    ppermute x4, waiting for transfers between devices, z_scan(): got = lax.ppermute(held, axis, pairs)  17.8 us
    unnamed x89, local copies, waits for them, and re-layouts  6.61 us
    gather x4, local copies, waits for them, and re-layouts, exchange(): return jnp.take(jnp.stack(got), (index - jnp.arange(count)) % count, axis=0)  4.17 us
    another operation x6, other arithmetic, exchange(): return jnp.take(jnp.stack(got), (index - jnp.arange(count)) % count, axis=0)  3.68 us
  transfers between devices with their start and end apart: 16, of which 10 were waited for; matrix products, arithmetic and copies ran while one was open for 10% of the time, Pallas kernels for 0%

profile of v5, /device:TPU:56, one launch (start us, length us, event | category | flops | bytes accessed | tf_op | source)
XLA Modules:
  0.0 172.8 jit_solution(14663628204391374360)
XLA Ops:
  0.7 1.0 reduce_window_sum.11
  2.0 1.1 copy.95
  3.1 0.8 bitcast_convert_fusion
  3.9 1.1 copy.94
  5.0 0.8 bitcast_convert_fusion.1
  7.5 3.4 %collective-permute-start = (f32[2,4,136,64]{2,3,1,0:T(8,128)S(1)}, f32[2,4,136,64]{2,3,1,0:T(8,128)}, u32[]{:S(2)}, u32[]{:S(2)}) collective-permute-start(f32[2,4,136,64]{2,3,1,0:T(8,128)S(1)} %get-tuple-element.177), channel_id=1, source_target_pairs={{0,16},{16,32},{32,48},{48,0},{1,17},{17,33},{33,49},{49,1},{2,18}... | collective-permute-start | bytes 835592 | tf_op jit(solution)/shard_map/ppermute | solution.py:47
  10.9 4.6 %collective-permute-start.1 = (f32[2,4,136,64]{2,3,1,0:T(8,128)S(1)}, f32[2,4,136,64]{2,3,1,0:T(8,128)}, u32[]{:S(2)}, u32[]{:S(2)}) collective-permute-start(f32[2,4,136,64]{2,3,1,0:T(8,128)S(1)} %get-tuple-element.176), channel_id=1, source_target_pairs={{0,32},{16,48},{32,0},{48,16},{1,33},{17,49},{33,1},{49,17},{2,34}... | collective-permute-start | bytes 835592 | tf_op jit(solution)/shard_map/ppermute | solution.py:47
  15.6 3.3 %collective-permute-start.2 = (f32[2,4,136,64]{2,3,1,0:T(8,128)S(1)}, f32[2,4,136,64]{2,3,1,0:T(8,128)}, u32[]{:S(2)}, u32[]{:S(2)}) collective-permute-start(f32[2,4,136,64]{2,3,1,0:T(8,128)S(1)} %get-tuple-element.175), channel_id=1, source_target_pairs={{0,48},{16,0},{32,16},{48,32},{1,49},{17,1},{33,17},{49,33},{2,50}... | collective-permute-start | bytes 835592 | tf_op jit(solution)/shard_map/ppermute | solution.py:47
  22.6 2.0 %collective-permute-done = f32[2,4,136,64]{2,3,1,0:T(8,128)} collective-permute-done((f32[2,4,136,64]{2,3,1,0:T(8,128)S(1)}, f32[2,4,136,64]{2,3,1,0:T(8,128)}, u32[]{:S(2)}, u32[]{:S(2)}) %collective-permute-start) | collective-permute-done | bytes 278560 | tf_op jit(solution)/shard_map/ppermute | solution.py:47
  24.5 12.1 %collective-permute-done.1 = f32[2,4,136,64]{2,3,1,0:T(8,128)} collective-permute-done((f32[2,4,136,64]{2,3,1,0:T(8,128)S(1)}, f32[2,4,136,64]{2,3,1,0:T(8,128)}, u32[]{:S(2)}, u32[]{:S(2)}) %collective-permute-start.1) | collective-permute-done | bytes 278560 | tf_op jit(solution)/shard_map/ppermute | solution.py:47
  36.6 1.6 collective-permute-done.2
  38.2 1.5 pad_maximum_fusion
  39.7 2.0 %gather_fusion = f32[4,2,4,136,64]{3,4,2,1,0:T(8,128)} fusion(f32[4,2,4,136,64]{3,4,2,1,0:T(8,128)S(1)} %pad_maximum_fusion, s32[1024]{0:T(1024)S(1)} %pad_clamp_fusion.1), kind=kCustom, calls=%fused_computation | custom fusion | bytes 2228240 | tf_op jit(solution)/shard_map/jit(_take)/gather | solution.py:48
  41.8 1.9 %broadcast_select_fusion = f32[4,2,4,136,64]{3,4,2,1,0:T(8,128)S(1)} fusion(f32[4,2,4,136,64]{3,4,2,1,0:T(8,128)} %gather_fusion, pred[4]{0:T(512)(128)(4,1)S(1)} %compare_and_fusion.1), kind=kLoop, calls=%fused_computation.63 | loop fusion | flops 278528 | bytes 2228228 | tf_op jit(solution)/shard_map/jit(_take)/select_n | solution.py:48
  43.9 0.9 slice_bitcast_fusion
  44.8 1.3 fusion.92
  49.6 4.3 %collective-permute-start.3 = (f32[2,1,136,64]{2,3,0,1:T(8,128)S(1)}, f32[2,1,136,64]{2,3,0,1:T(8,128)S(1)}, u32[]{:S(2)}, u32[]{:S(2)}) collective-permute-start(f32[2,1,136,64]{2,3,0,1:T(8,128)S(1)} %get-tuple-element.189), channel_id=1, source_target_pairs={{0,64},{64,128},{128,192},{192,0},{1,65},{65,129},{129,193},{193,1... | collective-permute-start | bytes 208904 | tf_op jit(solution)/shard_map/ppermute | solution.py:47
  53.9 6.1 %collective-permute-start.4 = (f32[2,1,136,64]{2,3,0,1:T(8,128)S(1)}, f32[2,1,136,64]{2,3,0,1:T(8,128)S(1)}, u32[]{:S(2)}, u32[]{:S(2)}) collective-permute-start(f32[2,1,136,64]{2,3,0,1:T(8,128)S(1)} %get-tuple-element.188), channel_id=1, source_target_pairs={{0,128},{64,192},{128,0},{192,64},{1,129},{65,193},{129,1},{193,65... | collective-permute-start | bytes 208904 | tf_op jit(solution)/shard_map/ppermute | solution.py:47
  60.0 2.5 %collective-permute-start.5 = (f32[2,1,136,64]{2,3,0,1:T(8,128)S(1)}, f32[2,1,136,64]{2,3,0,1:T(8,128)S(1)}, u32[]{:S(2)}, u32[]{:S(2)}) collective-permute-start(f32[2,1,136,64]{2,3,0,1:T(8,128)S(1)} %get-tuple-element.187), channel_id=1, source_target_pairs={{0,192},{64,0},{128,64},{192,128},{1,193},{65,1},{129,65},{193,129... | collective-permute-start | bytes 208904 | tf_op jit(solution)/shard_map/ppermute | solution.py:47
  64.3 1.9 %collective-permute-done.4 = f32[2,1,136,64]{2,3,0,1:T(8,128)S(1)} collective-permute-done((f32[2,1,136,64]{2,3,0,1:T(8,128)S(1)}, f32[2,1,136,64]{2,3,0,1:T(8,128)S(1)}, u32[]{:S(2)}, u32[]{:S(2)}) %collective-permute-start.4) | collective-permute-done | bytes 69664 | tf_op jit(solution)/shard_map/ppermute | solution.py:47
  66.2 1.8 %collective-permute-done.5 = f32[2,1,136,64]{2,3,0,1:T(8,128)S(1)} collective-permute-done((f32[2,1,136,64]{2,3,0,1:T(8,128)S(1)}, f32[2,1,136,64]{2,3,0,1:T(8,128)S(1)}, u32[]{:S(2)}, u32[]{:S(2)}) %collective-permute-start.5) | collective-permute-done | bytes 69664 | tf_op jit(solution)/shard_map/ppermute | solution.py:47
  68.6 0.9 maximum_bitcast_fusion.2
  71.9 0.8 fusion.88
  75.2 10.9 %collective-permute-start.6 = (f32[1,136,64]{1,2,0:T(8,128)S(1)}, f32[1,136,64]{1,2,0:T(8,128)S(1)}, u32[]{:S(2)}, u32[]{:S(2)}) collective-permute-start(f32[1,136,64]{1,2,0:T(8,128)S(1)} %concatenate.191), channel_id=1, source_target_pairs={{0,256},{256,512},{512,768},{1,257},{257,513},{513,769},{2,258},{2... | collective-permute-start | bytes 104456 | tf_op jit(solution)/shard_map/ppermute | solution.py:70
  86.8 1.3 collective-permute-start.8
  89.7 2.5 %maximum_bitcast_fusion.5 = f32[4]{0:T(128)S(1)} fusion(f32[1,1]{0,1:T(1,128)} %bitcast.96, f32[1,1]{0,1:T(1,128)} %bitcast.95, f32[1,1]{0,1:T(1,128)} %bitcast.94, f32[1,1]{0,1:T(1,128)} %bitcast.93), kind=kLoop, calls=%fused_computation.243 | loop fusion | flops 12 | bytes 32 | tf_op jit(solution)/shard_map/mul | solution.py:112
  92.3 1.9 %maximum_bitcast_fusion.4 = f32[4]{0:T(128)S(1)} fusion(f32[1,1]{0,1:T(1,128)} %bitcast.73, f32[1,1]{0,1:T(1,128)} %bitcast.72, f32[1,1]{0,1:T(1,128)} %bitcast.71, f32[1,1]{0,1:T(1,128)} %constant.263.clone.1), kind=kLoop, calls=%fused_computation.241 | loop fusion | flops 12 | bytes 32 | tf_op jit(solution)/shard_map/mul | solution.py:111
  94.2 5.9 %collective-permute-done.8 = f32[1,136,64]{1,2,0:T(8,128)S(1)} collective-permute-done((f32[1,136,64]{1,2,0:T(8,128)S(1)}, f32[1,136,64]{1,2,0:T(8,128)S(1)}, u32[]{:S(2)}, u32[]{:S(2)}) %collective-permute-start.8) | collective-permute-done | bytes 34848 | tf_op jit(solution)/shard_map/ppermute | solution.py:70
  103.9 12.2 %collective-permute-start.7 = (f32[1,136,64]{1,2,0:T(8,128)S(1)}, f32[1,136,64]{1,2,0:T(8,128)S(1)}, u32[]{:S(2)}, u32[]{:S(2)}) collective-permute-start(f32[1,136,64]{1,2,0:T(8,128)S(1)} %concatenate.192), channel_id=1, source_target_pairs={{0,512},{256,768},{1,513},{257,769},{2,514},{258,770},{3,515},{259... | collective-permute-start | bytes 104456 | tf_op jit(solution)/shard_map/ppermute | solution.py:70
  117.3 1.3 collective-permute-start.9
  118.6 1.8 %multiply_bitcast_fusion = (f32[1,8]{1,0:T(1,128)S(1)}, f32[1,8,1]{1,2,0:T(1,128)S(1)}) fusion(f32[1,136,1]{1,2,0:T(1,128)} %copy-done.41, f32[]{:T(128)} %bitcast.101, f32[]{:T(128)} %bitcast.80), kind=kLoop, calls=%fused_computation.249 | loop fusion | flops 16 | bytes 104 | tf_op jit(solution)/shard_map/mul | solution.py:77
  120.4 11.9 %collective-permute-done.9 = f32[1,136,64]{1,2,0:T(8,128)S(1)} collective-permute-done((f32[1,136,64]{1,2,0:T(8,128)S(1)}, f32[1,136,64]{1,2,0:T(8,128)S(1)}, u32[]{:S(2)}, u32[]{:S(2)}) %collective-permute-start.9) | collective-permute-done | bytes 34848 | tf_op jit(solution)/shard_map/ppermute | solution.py:70
  133.2 5.9 %collective-permute-start.10 = (f32[2,1,128,64]{2,3,0,1:T(8,128)S(1)}, f32[2,1,128,64]{2,3,0,1:T(8,128)S(1)}, u32[]{:S(2)}, u32[]{:S(2)}) collective-permute-start(f32[2,1,128,64]{2,3,0,1:T(8,128)S(1)} %get-tuple-element.195), channel_id=1, source_target_pairs={{0,64},{64,128},{128,192},{192,0},{1,65},{65,129},{129,193},{193,1... | collective-permute-start | bytes 196616 | tf_op jit(solution)/shard_map/ppermute | solution.py:47
  139.1 1.9 %collective-permute-start.11 = (f32[2,1,128,64]{2,3,0,1:T(8,128)S(1)}, f32[2,1,128,64]{2,3,0,1:T(8,128)S(1)}, u32[]{:S(2)}, u32[]{:S(2)}) collective-permute-start(f32[2,1,128,64]{2,3,0,1:T(8,128)S(1)} %get-tuple-element.196), channel_id=1, source_target_pairs={{0,128},{64,192},{128,0},{192,64},{1,129},{65,193},{129,1},{193,65... | collective-permute-start | bytes 196616 | tf_op jit(solution)/shard_map/ppermute | solution.py:47
  141.0 4.3 %collective-permute-start.12 = (f32[2,1,128,64]{2,3,0,1:T(8,128)S(1)}, f32[2,1,128,64]{2,3,0,1:T(8,128)S(1)}, u32[]{:S(2)}, u32[]{:S(2)}) collective-permute-start(f32[2,1,128,64]{2,3,0,1:T(8,128)S(1)} %get-tuple-element.197), channel_id=1, source_target_pairs={{0,192},{64,0},{128,64},{192,128},{1,193},{65,1},{129,65},{193,129... | collective-permute-start | bytes 196616 | tf_op jit(solution)/shard_map/ppermute | solution.py:47
  145.4 0.9 collective-permute-done.11
  146.3 0.9 collective-permute-done.12
  148.4 3.9 %collective-permute-start.13 = (f32[2,4,128,64]{2,3,1,0:T(8,128)S(1)}, f32[2,4,128,64]{2,3,1,0:T(8,128)S(1)}, u32[]{:S(2)}, u32[]{:S(2)}) collective-permute-start(f32[2,4,128,64]{2,3,1,0:T(8,128)S(1)} %get-tuple-element.181), channel_id=1, source_target_pairs={{0,16},{16,32},{32,48},{48,0},{1,17},{17,33},{33,49},{49,1},{2,18}... | collective-permute-start | bytes 786440 | tf_op jit(solution)/shard_map/ppermute | solution.py:47
  152.3 3.6 %collective-permute-start.14 = (f32[2,4,128,64]{2,3,1,0:T(8,128)S(1)}, f32[2,4,128,64]{2,3,1,0:T(8,128)S(1)}, u32[]{:S(2)}, u32[]{:S(2)}) collective-permute-start(f32[2,4,128,64]{2,3,1,0:T(8,128)S(1)} %get-tuple-element.182), channel_id=1, source_target_pairs={{0,32},{16,48},{32,0},{48,16},{1,33},{17,49},{33,1},{49,17},{2,34}... | collective-permute-start | bytes 786440 | tf_op jit(solution)/shard_map/ppermute | solution.py:47
  156.0 3.8 %collective-permute-start.15 = (f32[2,4,128,64]{2,3,1,0:T(8,128)S(1)}, f32[2,4,128,64]{2,3,1,0:T(8,128)S(1)}, u32[]{:S(2)}, u32[]{:S(2)}) collective-permute-start(f32[2,4,128,64]{2,3,1,0:T(8,128)S(1)} %get-tuple-element.183), channel_id=1, source_target_pairs={{0,48},{16,0},{32,16},{48,32},{1,49},{17,1},{33,17},{49,33},{2,50}... | collective-permute-start | bytes 786440 | tf_op jit(solution)/shard_map/ppermute | solution.py:47
  159.9 3.6 %while.18 = (s32[]{:T(128)}, f32[2,128,8,64]{1,3,2,0:T(8,128)}, f32[2,128,128]{2,1,0:T(8,128)S(1)}, f32[2,128,128]{2,1,0:T(8,128)S(1)}, bf16[2,128,8,64]{1,3,2,0...) while((s32[]{:T(128)}, f32[2,128,8,64]{1,3,2,0:T(8,128)}, ...), condition=%wide.region_3.4_spmd, body=%wide.region_1.3_spmd.sunk | while | flops 43515904 | bytes 1224821 | solution.py:176
  159.9 1.1 fusion.127
  161.8 1.1 fusion.127
  163.8 0.8 collective-permute-done.15
  165.3 1.1 pad_maximum_fusion.3
  168.5 1.0 fusion.30
  170.3 1.0 fusion.31
  172.0 0.8 copy.110
  (251 shorter events, 28.8 us)
Async XLA Ops:
  7.3 15.1 %copy-start.1 = (bf16[1,128,128]{2,1,0:T(8,128)(2,1)S(1)}, bf16[1,128,128]{2,1,0:T(8,128)(2,1)}, u32[]{:S(2)}) copy-start(bf16[1,128,128]{2,1,0:T(8,128)(2,1)} %param.17) | copy-start | bytes 98308
  7.3 15.1 %copy-start.3 = (bf16[1,128,128]{2,1,0:T(8,128)(2,1)S(1)}, bf16[1,128,128]{2,1,0:T(8,128)(2,1)}, u32[]{:S(2)}) copy-start(bf16[1,128,128]{2,1,0:T(8,128)(2,1)} %param.18) | copy-start | bytes 98308
  7.5 17.0 %collective-permute-start = (f32[2,4,136,64]{2,3,1,0:T(8,128)S(1)}, f32[2,4,136,64]{2,3,1,0:T(8,128)}, u32[]{:S(2)}, u32[]{:S(2)}) collective-permute-start(f32[2,4,136,64]{2,3,1,0:T(8,128)S(1)} %get-tuple-element.177), channel_id=1, source_target_pairs={{0,16},{16,32},{32,48},{48,0},{1,17},{17,33},{33,49},{49,1},{2,18}... | collective-permute-start | bytes 835592 | tf_op jit(solution)/shard_map/ppermute | solution.py:47
  10.9 25.7 %collective-permute-start.1 = (f32[2,4,136,64]{2,3,1,0:T(8,128)S(1)}, f32[2,4,136,64]{2,3,1,0:T(8,128)}, u32[]{:S(2)}, u32[]{:S(2)}) collective-permute-start(f32[2,4,136,64]{2,3,1,0:T(8,128)S(1)} %get-tuple-element.176), channel_id=1, source_target_pairs={{0,32},{16,48},{32,0},{48,16},{1,33},{17,49},{33,1},{49,17},{2,34}... | collective-permute-start | bytes 835592 | tf_op jit(solution)/shard_map/ppermute | solution.py:47
  15.6 22.6 %collective-permute-start.2 = (f32[2,4,136,64]{2,3,1,0:T(8,128)S(1)}, f32[2,4,136,64]{2,3,1,0:T(8,128)}, u32[]{:S(2)}, u32[]{:S(2)}) collective-permute-start(f32[2,4,136,64]{2,3,1,0:T(8,128)S(1)} %get-tuple-element.175), channel_id=1, source_target_pairs={{0,48},{16,0},{32,16},{48,32},{1,49},{17,1},{33,17},{49,33},{2,50}... | collective-permute-start | bytes 835592 | tf_op jit(solution)/shard_map/ppermute | solution.py:47
  19.0 22.8 %copy-start.20 = (pred[4]{0:T(512)(128)(4,1)}, pred[4]{0:T(512)(128)(4,1)S(1)}, u32[]{:S(2)}) copy-start(pred[4]{0:T(512)(128)(4,1)S(1)} %compare_and_fusion.1) | copy-start | bytes 16
  19.0 25.7 %copy-start.27 = (pred[4]{0:T(512)(128)(4,1)}, pred[4]{0:T(512)(128)(4,1)S(1)}, u32[]{:S(2)}) copy-start(pred[4]{0:T(512)(128)(4,1)S(1)} %iota_compare_fusion.7) | copy-start | bytes 16
  19.1 25.7 %copy-start.25 = (pred[4]{0:T(512)(128)(4,1)}, pred[4]{0:T(512)(128)(4,1)S(1)}, u32[]{:S(2)}) copy-start(pred[4]{0:T(512)(128)(4,1)S(1)} %iota_compare_fusion.8) | copy-start | bytes 16
  19.1 25.7 %copy-start.23 = (pred[4]{0:T(512)(128)(4,1)}, pred[4]{0:T(512)(128)(4,1)S(1)}, u32[]{:S(2)}) copy-start(pred[4]{0:T(512)(128)(4,1)S(1)} %iota_compare_fusion.9) | copy-start | bytes 16
  19.1 20.6 %copy-start.36 = (f32[136]{0:T(256)}, f32[136]{0:T(256)S(1)}, u32[]{:S(2)}) copy-start(f32[136]{0:T(256)S(1)} %compare_select_fusion.23) | copy-start | bytes 1636
  19.1 20.6 %copy-start.41 = (f32[1,136,1]{1,2,0:T(1,128)}, f32[1,136,1]{1,2,0:T(1,128)S(1)}, u32[]{:S(2)}) copy-start(f32[1,136,1]{1,2,0:T(1,128)S(1)} %compare_select_fusion) | copy-start | bytes 1636
  19.2 20.6 %copy-start.19 = (s32[1024]{0:T(1024)}, s32[1024]{0:T(1024)S(1)}, u32[]{:S(2)}) copy-start(s32[1024]{0:T(1024)S(1)} %pad_clamp_fusion.1) | copy-start | bytes 12292
  49.3 13.4 %copy-start.13 = (f32[4,4]{1,0:T(4,128)S(1)}, f32[4,4]{1,0:T(4,128)}, u32[]{:S(2)}) copy-start(f32[4,4]{1,0:T(4,128)} %get-tuple-element.215) | copy-start | bytes 196
  49.3 13.5 %copy-start.26 = (pred[4]{0:T(512)(128)(4,1)S(1)}, pred[4]{0:T(512)(128)(4,1)}, u32[]{:S(2)}) copy-start(pred[4]{0:T(512)(128)(4,1)} %copy-done.25) | copy-start | bytes 16
  49.3 13.6 %copy-start.12 = (f32[4,4]{1,0:T(4,128)S(1)}, f32[4,4]{1,0:T(4,128)}, u32[]{:S(2)}) copy-start(f32[4,4]{1,0:T(4,128)} %get-tuple-element.217) | copy-start | bytes 196
  49.3 13.6 %copy-start.24 = (pred[4]{0:T(512)(128)(4,1)S(1)}, pred[4]{0:T(512)(128)(4,1)}, u32[]{:S(2)}) copy-start(pred[4]{0:T(512)(128)(4,1)} %copy-done.23) | copy-start | bytes 16
  49.3 13.7 %copy-start.15 = (f32[1,4,4]{2,1,0:T(4,128)S(1)}, f32[1,4,4]{2,1,0:T(4,128)}, u32[]{:S(2)}) copy-start(f32[1,4,4]{2,1,0:T(4,128)} %select_bitcast_fusion.10) | copy-start | bytes 196
  49.3 13.7 %copy-start.16 = (f32[1,4,4]{2,1,0:T(4,128)S(1)}, f32[1,4,4]{2,1,0:T(4,128)}, u32[]{:S(2)}) copy-start(f32[1,4,4]{2,1,0:T(4,128)} %select_bitcast_fusion.11) | copy-start | bytes 196
  49.3 13.7 %copy-start.17 = (f32[1,4,4]{2,1,0:T(4,128)S(1)}, f32[1,4,4]{2,1,0:T(4,128)}, u32[]{:S(2)}) copy-start(f32[1,4,4]{2,1,0:T(4,128)} %select_bitcast_fusion.8) | copy-start | bytes 196
  49.3 13.7 %copy-start.18 = (f32[1,4,4]{2,1,0:T(4,128)S(1)}, f32[1,4,4]{2,1,0:T(4,128)}, u32[]{:S(2)}) copy-start(f32[1,4,4]{2,1,0:T(4,128)} %select_bitcast_fusion.9) | copy-start | bytes 196
  49.3 13.7 %copy-start = (f32[4,4,128,64]{2,3,1,0:T(8,128)S(1)}, f32[4,4,128,64]{2,3,1,0:T(8,128)}, u32[]{:S(2)}) copy-start(f32[4,4,128,64]{2,3,1,0:T(8,128)} %get-tuple-element.172) | copy-start | bytes 1572868
  49.4 13.9 %copy-start.33 = (f32[4]{0:T(128)S(1)}, f32[4]{0:T(128)}, u32[]{:S(2)}) copy-start(f32[4]{0:T(128)} %get-tuple-element.212) | copy-start | bytes 52
  49.4 13.9 %copy-start.34 = (f32[4]{0:T(128)S(1)}, f32[4]{0:T(128)}, u32[]{:S(2)}) copy-start(f32[4]{0:T(128)} %get-tuple-element.214) | copy-start | bytes 52
  49.4 13.9 %copy-start.35 = (f32[4]{0:T(128)S(1)}, f32[4]{0:T(128)}, u32[]{:S(2)}) copy-start(f32[4]{0:T(128)} %get-tuple-element.216) | copy-start | bytes 52
  49.4 13.9 %copy-start.39 = (f32[4]{0:T(128)S(1)}, f32[4]{0:T(128)}, u32[]{:S(2)}) copy-start(f32[4]{0:T(128)} %pad.86.clone) | copy-start | bytes 52
  49.5 14.5 %copy-start.40 = (f32[4]{0:T(128)S(1)}, f32[4]{0:T(128)}, u32[]{:S(2)}) copy-start(f32[4]{0:T(128)} %pad.90.clone) | copy-start | bytes 52
  49.6 14.7 %collective-permute-start.3 = (f32[2,1,136,64]{2,3,0,1:T(8,128)S(1)}, f32[2,1,136,64]{2,3,0,1:T(8,128)S(1)}, u32[]{:S(2)}, u32[]{:S(2)}) collective-permute-start(f32[2,1,136,64]{2,3,0,1:T(8,128)S(1)} %get-tuple-element.189), channel_id=1, source_target_pairs={{0,64},{64,128},{128,192},{192,0},{1,65},{65,129},{129,193},{193,1... | collective-permute-start | bytes 208904 | tf_op jit(solution)/shard_map/ppermute | solution.py:47
  53.9 12.3 %collective-permute-start.4 = (f32[2,1,136,64]{2,3,0,1:T(8,128)S(1)}, f32[2,1,136,64]{2,3,0,1:T(8,128)S(1)}, u32[]{:S(2)}, u32[]{:S(2)}) collective-permute-start(f32[2,1,136,64]{2,3,0,1:T(8,128)S(1)} %get-tuple-element.188), channel_id=1, source_target_pairs={{0,128},{64,192},{128,0},{192,64},{1,129},{65,193},{129,1},{193,65... | collective-permute-start | bytes 208904 | tf_op jit(solution)/shard_map/ppermute | solution.py:47
  60.0 8.0 %collective-permute-start.5 = (f32[2,1,136,64]{2,3,0,1:T(8,128)S(1)}, f32[2,1,136,64]{2,3,0,1:T(8,128)S(1)}, u32[]{:S(2)}, u32[]{:S(2)}) collective-permute-start(f32[2,1,136,64]{2,3,0,1:T(8,128)S(1)} %get-tuple-element.187), channel_id=1, source_target_pairs={{0,192},{64,0},{128,64},{192,128},{1,193},{65,1},{129,65},{193,129... | collective-permute-start | bytes 208904 | tf_op jit(solution)/shard_map/ppermute | solution.py:47
  69.6 30.5 %copy-start.37 = (f32[136]{0:T(256)S(1)}, f32[136]{0:T(256)}, u32[]{:S(2)}) copy-start(f32[136]{0:T(256)} %copy-done.36) | copy-start | bytes 1636
  69.6 62.7 %slice-start = ((f32[136]{0:T(256)}), f32[128]{0:T(128)S(1)}, s32[]{:S(2)}) async-start(f32[136]{0:T(256)} %copy-done.36), calls=%async_computation | async-start | bytes 1024 | tf_op jit(solution)/shard_map/slice | solution.py:72
  69.6 62.7 %copy-start.38 = (f32[128]{0:T(128)S(1)}, f32[128]{0:T(128)}, u32[]{:S(2)}) copy-start(f32[128]{0:T(128)} %slice_bitcast_fusion.6) | copy-start | bytes 1540
  71.0 74.2 %copy-start.29 = (f32[4]{0:T(128)S(1)}, f32[4]{0:T(128)}, u32[]{:S(2)}) copy-start(f32[4]{0:T(128)} %get-tuple-element.158) | copy-start | bytes 52
  71.1 74.2 %copy-start.30 = (f32[4]{0:T(128)S(1)}, f32[4]{0:T(128)}, u32[]{:S(2)}) copy-start(f32[4]{0:T(128)} %get-tuple-element.204) | copy-start | bytes 52
  71.1 74.2 %copy-start.31 = (f32[4]{0:T(128)S(1)}, f32[4]{0:T(128)}, u32[]{:S(2)}) copy-start(f32[4]{0:T(128)} %get-tuple-element.206) | copy-start | bytes 52
  71.1 74.2 %copy-start.32 = (f32[4]{0:T(128)S(1)}, f32[4]{0:T(128)}, u32[]{:S(2)}) copy-start(f32[4]{0:T(128)} %get-tuple-element.208) | copy-start | bytes 52
  75.2 19.0 %collective-permute-start.6 = (f32[1,136,64]{1,2,0:T(8,128)S(1)}, f32[1,136,64]{1,2,0:T(8,128)S(1)}, u32[]{:S(2)}, u32[]{:S(2)}) collective-permute-start(f32[1,136,64]{1,2,0:T(8,128)S(1)} %concatenate.191), channel_id=1, source_target_pairs={{0,256},{256,512},{512,768},{1,257},{257,513},{513,769},{2,258},{2... | collective-permute-start | bytes 104456 | tf_op jit(solution)/shard_map/ppermute | solution.py:70
  86.8 13.2 %collective-permute-start.8 = (f32[1,136,64]{1,2,0:T(8,128)S(1)}, f32[1,136,64]{1,2,0:T(8,128)S(1)}, u32[]{:S(2)}, u32[]{:S(2)}) collective-permute-start(f32[1,136,64]{1,2,0:T(8,128)S(1)} %concatenate.203), channel_id=1, source_target_pairs={{256,0},{512,256},{768,512},{257,1},{513,257},{769,513},{258,2},{5... | collective-permute-start | bytes 104456 | tf_op jit(solution)/shard_map/ppermute | solution.py:70
  89.5 58.4 %copy-start.22 = (pred[4]{0:T(512)(128)(4,1)S(1)}, pred[4]{0:T(512)(128)(4,1)}, u32[]{:S(2)}) copy-start(pred[4]{0:T(512)(128)(4,1)} %compare_and_fusion) | copy-start | bytes 16
  103.9 16.5 %collective-permute-start.7 = (f32[1,136,64]{1,2,0:T(8,128)S(1)}, f32[1,136,64]{1,2,0:T(8,128)S(1)}, u32[]{:S(2)}, u32[]{:S(2)}) collective-permute-start(f32[1,136,64]{1,2,0:T(8,128)S(1)} %concatenate.192), channel_id=1, source_target_pairs={{0,512},{256,768},{1,513},{257,769},{2,514},{258,770},{3,515},{259... | collective-permute-start | bytes 104456 | tf_op jit(solution)/shard_map/ppermute | solution.py:70
  117.3 15.0 %collective-permute-start.9 = (f32[1,136,64]{1,2,0:T(8,128)S(1)}, f32[1,136,64]{1,2,0:T(8,128)S(1)}, u32[]{:S(2)}, u32[]{:S(2)}) collective-permute-start(f32[1,136,64]{1,2,0:T(8,128)S(1)} %concatenate.204), channel_id=1, source_target_pairs={{512,0},{768,256},{513,1},{769,257},{514,2},{770,258},{515,3},{771... | collective-permute-start | bytes 104456 | tf_op jit(solution)/shard_map/ppermute | solution.py:70
  133.2 15.0 %copy-start.11 = (f32[4,4]{1,0:T(4,128)S(1)}, f32[4,4]{1,0:T(4,128)}, u32[]{:S(2)}) copy-start(f32[4,4]{1,0:T(4,128)} %pad_maximum_fusion.8) | copy-start | bytes 196
  133.2 12.1 %collective-permute-start.10 = (f32[2,1,128,64]{2,3,0,1:T(8,128)S(1)}, f32[2,1,128,64]{2,3,0,1:T(8,128)S(1)}, u32[]{:S(2)}, u32[]{:S(2)}) collective-permute-start(f32[2,1,128,64]{2,3,0,1:T(8,128)S(1)} %get-tuple-element.195), channel_id=1, source_target_pairs={{0,64},{64,128},{128,192},{192,0},{1,65},{65,129},{129,193},{193,1... | collective-permute-start | bytes 196616 | tf_op jit(solution)/shard_map/ppermute | solution.py:47
  139.1 7.2 %collective-permute-start.11 = (f32[2,1,128,64]{2,3,0,1:T(8,128)S(1)}, f32[2,1,128,64]{2,3,0,1:T(8,128)S(1)}, u32[]{:S(2)}, u32[]{:S(2)}) collective-permute-start(f32[2,1,128,64]{2,3,0,1:T(8,128)S(1)} %get-tuple-element.196), channel_id=1, source_target_pairs={{0,128},{64,192},{128,0},{192,64},{1,129},{65,193},{129,1},{193,65... | collective-permute-start | bytes 196616 | tf_op jit(solution)/shard_map/ppermute | solution.py:47
  141.0 6.2 %collective-permute-start.12 = (f32[2,1,128,64]{2,3,0,1:T(8,128)S(1)}, f32[2,1,128,64]{2,3,0,1:T(8,128)S(1)}, u32[]{:S(2)}, u32[]{:S(2)}) collective-permute-start(f32[2,1,128,64]{2,3,0,1:T(8,128)S(1)} %get-tuple-element.197), channel_id=1, source_target_pairs={{0,192},{64,0},{128,64},{192,128},{1,193},{65,1},{129,65},{193,129... | collective-permute-start | bytes 196616 | tf_op jit(solution)/shard_map/ppermute | solution.py:47
  148.4 15.4 %collective-permute-start.13 = (f32[2,4,128,64]{2,3,1,0:T(8,128)S(1)}, f32[2,4,128,64]{2,3,1,0:T(8,128)S(1)}, u32[]{:S(2)}, u32[]{:S(2)}) collective-permute-start(f32[2,4,128,64]{2,3,1,0:T(8,128)S(1)} %get-tuple-element.181), channel_id=1, source_target_pairs={{0,16},{16,32},{32,48},{48,0},{1,17},{17,33},{33,49},{49,1},{2,18}... | collective-permute-start | bytes 786440 | tf_op jit(solution)/shard_map/ppermute | solution.py:47
  152.3 11.4 %collective-permute-start.14 = (f32[2,4,128,64]{2,3,1,0:T(8,128)S(1)}, f32[2,4,128,64]{2,3,1,0:T(8,128)S(1)}, u32[]{:S(2)}, u32[]{:S(2)}) collective-permute-start(f32[2,4,128,64]{2,3,1,0:T(8,128)S(1)} %get-tuple-element.182), channel_id=1, source_target_pairs={{0,32},{16,48},{32,0},{48,16},{1,33},{17,49},{33,1},{49,17},{2,34}... | collective-permute-start | bytes 786440 | tf_op jit(solution)/shard_map/ppermute | solution.py:47
  156.0 8.6 %collective-permute-start.15 = (f32[2,4,128,64]{2,3,1,0:T(8,128)S(1)}, f32[2,4,128,64]{2,3,1,0:T(8,128)S(1)}, u32[]{:S(2)}, u32[]{:S(2)}) collective-permute-start(f32[2,4,128,64]{2,3,1,0:T(8,128)S(1)} %get-tuple-element.183), channel_id=1, source_target_pairs={{0,48},{16,0},{32,16},{48,32},{1,49},{17,1},{33,17},{49,33},{2,50}... | collective-permute-start | bytes 786440 | tf_op jit(solution)/shard_map/ppermute | solution.py:47
  (11 other events, 60.1 us)

commit v6 on v5

--- a/solution.py
+++ b/solution.py
@@ -86,10 +86,26 @@
     return jnp.concatenate([state, rows], axis=1)
 
 
+def gathered_scan(own_f, own_b, axis):
+    count, index = lax.axis_size(axis), lax.axis_index(axis)
+    n = own_f.shape[1] - 8
+    mine = jnp.stack([own_f, own_b])
+    got = [mine]
+    for shift in range(1, count):
+        got.append(lax.ppermute(mine, axis, [(i, (i + shift) % count) for i in range(count)]))
+    members = jnp.take(jnp.stack(got), (index - jnp.arange(count)) % count, axis=0)
+    group = members[:, 0, :, n, 0]
+    entry_f = weighted(lower_weights(group, index), members[:, 0, :, :n])
+    entry_b = weighted(upper_weights(group, index), members[:, 1, :, :n])
+    return entry_f, entry_b
+
+
 def entry_states(own_f, own_b, axes):
     axis = axes[0]
     count = lax.axis_size(axis)
     heads, n, width = own_f.shape[0], own_f.shape[1] - 8, own_f.shape[2]
+    if len(axes) == 1 and count <= 8:
+        return gathered_scan(own_f, own_b, axis)
     if len(axes) == 1 or heads % count:
         whole = tuple(reversed(axes))
         return z_scan(own_f, whole, True), z_scan(own_b, whole, False)

time: 174 us -> 167 us (0.960)
  waiting for transfers between devices: 39.7 us -> 37 us
  between operations: 4.48 us -> 1.83 us
    ppermute x4 -> x3, waiting for transfers between devices: 17.8 us -> 12.8 us  [gathered_scan(): lax.ppermute(mine, axis, [(i, (i + shift) % count) for i in range(count)])]
    ppermute x12, starting transfers between devices: 47.6 us -> 45.2 us  [exchange(): lax.ppermute(send, axis, [(i, (i + shift) % count) for i in range(count)])]
    ppermute x12, waiting for transfers between devices: 21.9 us -> 24.2 us  [exchange(): lax.ppermute(send, axis, [(i, (i + shift) % count) for i in range(count)])]
    slice x6 -> x1, local copies, waits for them, and re-layouts: 2.05 us -> 0.12 us  [gathered_scan(): group = members[:, 0, :, n, 0]]
    mul x1 -> x0, other arithmetic: 1.77 us -> none  [merge(): return jnp.concatenate([state, mine[:, n:] * got_pass], axis=1)]
    ppermute x4 -> x3, starting transfers between devices: 25.7 us -> 26.4 us  [gathered_scan(): lax.ppermute(mine, axis, [(i, (i + shift) % count) for i in range(count)])]
    unnamed x89 -> x85, local copies, waits for them, and re-layouts: 6.61 us -> 6.6 us
  transfers between devices with their start and end apart: 16 -> 15, of which waited for: 10 -> 11; matrix products, arithmetic and copies ran while one was open for 10% -> 11% of each run, Pallas kernels for 0% -> 0%
where the time goes in v6:
time: 167 us; the launch traced here: 165 us
  starting transfers between devices  71.6 us (43%)
  waiting for transfers between devices  37 us (22%)
  other arithmetic  30.4 us (18%)
  local copies, waits for them, and re-layouts  16.8 us (10%)
  matrix products  7.02 us (4%)
  between operations  1.83 us (1%)
    ppermute x12, starting transfers between devices, exchange(): lax.ppermute(send, axis, [(i, (i + shift) % count) for i in range(count)])  45.2 us
    ppermute x3, starting transfers between devices, gathered_scan(): lax.ppermute(mine, axis, [(i, (i + shift) % count) for i in range(count)])  26.4 us
    ppermute x12, waiting for transfers between devices, exchange(): lax.ppermute(send, axis, [(i, (i + shift) % count) for i in range(count)])  24.2 us
    ppermute x3, waiting for transfers between devices, gathered_scan(): lax.ppermute(mine, axis, [(i, (i + shift) % count) for i in range(count)])  12.8 us
    unnamed x85, local copies, waits for them, and re-layouts  6.6 us
    gather x4, local copies, waits for them, and re-layouts, exchange(): return jnp.take(jnp.stack(got), (index - jnp.arange(count)) % count, axis=0)  4.16 us
    another operation x6, other arithmetic, exchange(): return jnp.take(jnp.stack(got), (index - jnp.arange(count)) % count, axis=0)  3.68 us
  transfers between devices with their start and end apart: 15, of which 11 were waited for; matrix products, arithmetic and copies ran while one was open for 11% of the time, Pallas kernels for 0%

profile of v6, /device:TPU:56, one launch (start us, length us, event | category | flops | bytes accessed | tf_op | source)
XLA Modules:
  0.0 164.7 jit_solution(10928724275689797343)
XLA Ops:
  0.7 1.0 reduce_window_sum.11
  2.0 1.1 copy.106
  3.1 0.8 bitcast_convert_fusion
  3.9 1.1 copy.105
  5.0 0.8 bitcast_convert_fusion.1
  7.5 3.4 %collective-permute-start = (f32[2,4,136,64]{2,3,1,0:T(8,128)S(1)}, f32[2,4,136,64]{2,3,1,0:T(8,128)}, u32[]{:S(2)}, u32[]{:S(2)}) collective-permute-start(f32[2,4,136,64]{2,3,1,0:T(8,128)S(1)} %get-tuple-element.180), channel_id=1, source_target_pairs={{0,16},{16,32},{32,48},{48,0},{1,17},{17,33},{33,49},{49,1},{2,18}... | collective-permute-start | bytes 835592 | tf_op jit(solution)/shard_map/ppermute | solution.py:47
  10.9 4.6 %collective-permute-start.1 = (f32[2,4,136,64]{2,3,1,0:T(8,128)S(1)}, f32[2,4,136,64]{2,3,1,0:T(8,128)}, u32[]{:S(2)}, u32[]{:S(2)}) collective-permute-start(f32[2,4,136,64]{2,3,1,0:T(8,128)S(1)} %get-tuple-element.179), channel_id=1, source_target_pairs={{0,32},{16,48},{32,0},{48,16},{1,33},{17,49},{33,1},{49,17},{2,34}... | collective-permute-start | bytes 835592 | tf_op jit(solution)/shard_map/ppermute | solution.py:47
  15.6 3.3 %collective-permute-start.2 = (f32[2,4,136,64]{2,3,1,0:T(8,128)S(1)}, f32[2,4,136,64]{2,3,1,0:T(8,128)}, u32[]{:S(2)}, u32[]{:S(2)}) collective-permute-start(f32[2,4,136,64]{2,3,1,0:T(8,128)S(1)} %get-tuple-element.178), channel_id=1, source_target_pairs={{0,48},{16,0},{32,16},{48,32},{1,49},{17,1},{33,17},{49,33},{2,50}... | collective-permute-start | bytes 835592 | tf_op jit(solution)/shard_map/ppermute | solution.py:47
  23.2 1.3 collective-permute-done
  24.5 12.1 %collective-permute-done.1 = f32[2,4,136,64]{2,3,1,0:T(8,128)} collective-permute-done((f32[2,4,136,64]{2,3,1,0:T(8,128)S(1)}, f32[2,4,136,64]{2,3,1,0:T(8,128)}, u32[]{:S(2)}, u32[]{:S(2)}) %collective-permute-start.1) | collective-permute-done | bytes 278560 | tf_op jit(solution)/shard_map/ppermute | solution.py:47
  36.6 1.6 collective-permute-done.2
  38.2 1.5 pad_maximum_fusion
  39.7 2.0 %gather_fusion = f32[4,2,4,136,64]{3,4,2,1,0:T(8,128)} fusion(f32[4,2,4,136,64]{3,4,2,1,0:T(8,128)S(1)} %pad_maximum_fusion, s32[1024]{0:T(1024)S(1)} %pad_clamp_fusion.3), kind=kCustom, calls=%fused_computation.2 | custom fusion | bytes 2228240 | tf_op jit(solution)/shard_map/jit(_take)/gather | solution.py:48
  41.7 1.9 %broadcast_select_fusion = f32[4,2,4,136,64]{3,4,2,1,0:T(8,128)S(1)} fusion(f32[4,2,4,136,64]{3,4,2,1,0:T(8,128)} %gather_fusion, pred[4]{0:T(512)(128)(4,1)S(1)} %compare_and_fusion.2), kind=kLoop, calls=%fused_computation.64 | loop fusion | flops 278528 | bytes 2228228 | tf_op jit(solution)/shard_map/jit(_take)/select_n | solution.py:48
  43.9 0.9 slice_bitcast_fusion
  44.8 1.3 fusion.94
  49.6 4.3 %collective-permute-start.3 = (f32[2,1,136,64]{2,3,0,1:T(8,128)S(1)}, f32[2,1,136,64]{2,3,0,1:T(8,128)S(1)}, u32[]{:S(2)}, u32[]{:S(2)}) collective-permute-start(f32[2,1,136,64]{2,3,0,1:T(8,128)S(1)} %get-tuple-element.192), channel_id=1, source_target_pairs={{0,64},{64,128},{128,192},{192,0},{1,65},{65,129},{129,193},{193,1... | collective-permute-start | bytes 208904 | tf_op jit(solution)/shard_map/ppermute | solution.py:47
  53.9 6.1 %collective-permute-start.4 = (f32[2,1,136,64]{2,3,0,1:T(8,128)S(1)}, f32[2,1,136,64]{2,3,0,1:T(8,128)S(1)}, u32[]{:S(2)}, u32[]{:S(2)}) collective-permute-start(f32[2,1,136,64]{2,3,0,1:T(8,128)S(1)} %get-tuple-element.191), channel_id=1, source_target_pairs={{0,128},{64,192},{128,0},{192,64},{1,129},{65,193},{129,1},{193,65... | collective-permute-start | bytes 208904 | tf_op jit(solution)/shard_map/ppermute | solution.py:47
  60.0 2.5 %collective-permute-start.5 = (f32[2,1,136,64]{2,3,0,1:T(8,128)S(1)}, f32[2,1,136,64]{2,3,0,1:T(8,128)S(1)}, u32[]{:S(2)}, u32[]{:S(2)}) collective-permute-start(f32[2,1,136,64]{2,3,0,1:T(8,128)S(1)} %get-tuple-element.190), channel_id=1, source_target_pairs={{0,192},{64,0},{128,64},{192,128},{1,193},{65,1},{129,65},{193,129... | collective-permute-start | bytes 208904 | tf_op jit(solution)/shard_map/ppermute | solution.py:47
  64.3 1.9 %collective-permute-done.4 = f32[2,1,136,64]{2,3,0,1:T(8,128)S(1)} collective-permute-done((f32[2,1,136,64]{2,3,0,1:T(8,128)S(1)}, f32[2,1,136,64]{2,3,0,1:T(8,128)S(1)}, u32[]{:S(2)}, u32[]{:S(2)}) %collective-permute-start.4) | collective-permute-done | bytes 69664 | tf_op jit(solution)/shard_map/ppermute | solution.py:47
  66.2 1.8 %collective-permute-done.5 = f32[2,1,136,64]{2,3,0,1:T(8,128)S(1)} collective-permute-done((f32[2,1,136,64]{2,3,0,1:T(8,128)S(1)}, f32[2,1,136,64]{2,3,0,1:T(8,128)S(1)}, u32[]{:S(2)}, u32[]{:S(2)}) %collective-permute-start.5) | collective-permute-done | bytes 69664 | tf_op jit(solution)/shard_map/ppermute | solution.py:47
  68.6 0.9 maximum_bitcast_fusion.2
  71.7 0.8 fusion.89
  74.7 10.9 %collective-permute-start.6 = (f32[2,1,136,64]{2,3,0,1:T(8,128)S(1)}, f32[2,1,136,64]{2,3,0,1:T(8,128)S(1)}, u32[]{:S(2)}, u32[]{:S(2)}) collective-permute-start(f32[2,1,136,64]{2,3,0,1:T(8,128)S(1)} %get-tuple-element.202), channel_id=1, source_target_pairs={{0,256},{256,512},{512,768},{768,0},{1,257},{257,513},{513,769},{7... | collective-permute-start | bytes 208904 | tf_op jit(solution)/shard_map/ppermute | solution.py:95
  85.6 11.8 %collective-permute-start.7 = (f32[2,1,136,64]{2,3,0,1:T(8,128)S(1)}, f32[2,1,136,64]{2,3,0,1:T(8,128)S(1)}, u32[]{:S(2)}, u32[]{:S(2)}) collective-permute-start(f32[2,1,136,64]{2,3,0,1:T(8,128)S(1)} %get-tuple-element.202), channel_id=1, source_target_pairs={{0,512},{256,768},{512,0},{768,256},{1,513},{257,769},{513,1},{769... | collective-permute-start | bytes 208904 | tf_op jit(solution)/shard_map/ppermute | solution.py:95
  97.4 3.6 %collective-permute-start.8 = (f32[2,1,136,64]{2,3,0,1:T(8,128)S(1)}, f32[2,1,136,64]{2,3,0,1:T(8,128)S(1)}, u32[]{:S(2)}, u32[]{:S(2)}) collective-permute-start(f32[2,1,136,64]{2,3,0,1:T(8,128)S(1)} %get-tuple-element.202), channel_id=1, source_target_pairs={{0,768},{256,0},{512,256},{768,512},{1,769},{257,1},{513,257},{769... | collective-permute-start | bytes 208904 | tf_op jit(solution)/shard_map/ppermute | solution.py:95
  103.7 3.1 %maximum_bitcast_fusion.6 = f32[4]{0:T(128)} fusion(f32[1,1]{0,1:T(1,128)} %bitcast.103, f32[1,1]{0,1:T(1,128)} %bitcast.102, f32[1,1]{0,1:T(1,128)} %bitcast.101, f32[1,1]{0,1:T(1,128)} %bitcast.100), kind=kLoop, calls=%fused_computation.258 | loop fusion | flops 12 | bytes 32 | tf_op jit(solution)/shard_map/mul | solution.py:128
  106.8 2.5 %maximum_bitcast_fusion.5 = f32[4]{0:T(128)} fusion(f32[1,1]{0,1:T(1,128)} %bitcast.72, f32[1,1]{0,1:T(1,128)} %bitcast.71, f32[1,1]{0,1:T(1,128)} %bitcast.70, f32[1,1]{0,1:T(1,128)} %constant.271.clone.1), kind=kLoop, calls=%fused_computation.257 | loop fusion | flops 12 | bytes 32 | tf_op jit(solution)/shard_map/mul | solution.py:127
  109.3 7.1 %collective-permute-done.7 = f32[2,1,136,64]{2,3,0,1:T(8,128)S(1)} collective-permute-done((f32[2,1,136,64]{2,3,0,1:T(8,128)S(1)}, f32[2,1,136,64]{2,3,0,1:T(8,128)S(1)}, u32[]{:S(2)}, u32[]{:S(2)}) %collective-permute-start.7) | collective-permute-done | bytes 69664 | tf_op jit(solution)/shard_map/ppermute | solution.py:95
  116.4 5.7 %collective-permute-done.8 = f32[2,1,136,64]{2,3,0,1:T(8,128)S(1)} collective-permute-done((f32[2,1,136,64]{2,3,0,1:T(8,128)S(1)}, f32[2,1,136,64]{2,3,0,1:T(8,128)S(1)}, u32[]{:S(2)}, u32[]{:S(2)}) %collective-permute-start.8) | collective-permute-done | bytes 69664 | tf_op jit(solution)/shard_map/ppermute | solution.py:95
  124.7 2.5 %collective-permute-start.9 = (f32[2,1,128,64]{2,3,0,1:T(8,128)S(1)}, f32[2,1,128,64]{2,3,0,1:T(8,128)S(1)}, u32[]{:S(2)}, u32[]{:S(2)}) collective-permute-start(f32[2,1,128,64]{2,3,0,1:T(8,128)S(1)} %get-tuple-element.198), channel_id=1, source_target_pairs={{0,64},{64,128},{128,192},{192,0},{1,65},{65,129},{129,193},{193,1... | collective-permute-start | bytes 196616 | tf_op jit(solution)/shard_map/ppermute | solution.py:47
  127.2 1.9 %collective-permute-start.10 = (f32[2,1,128,64]{2,3,0,1:T(8,128)S(1)}, f32[2,1,128,64]{2,3,0,1:T(8,128)S(1)}, u32[]{:S(2)}, u32[]{:S(2)}) collective-permute-start(f32[2,1,128,64]{2,3,0,1:T(8,128)S(1)} %get-tuple-element.199), channel_id=1, source_target_pairs={{0,128},{64,192},{128,0},{192,64},{1,129},{65,193},{129,1},{193,65... | collective-permute-start | bytes 196616 | tf_op jit(solution)/shard_map/ppermute | solution.py:47
  129.1 5.2 %collective-permute-start.11 = (f32[2,1,128,64]{2,3,0,1:T(8,128)S(1)}, f32[2,1,128,64]{2,3,0,1:T(8,128)S(1)}, u32[]{:S(2)}, u32[]{:S(2)}) collective-permute-start(f32[2,1,128,64]{2,3,0,1:T(8,128)S(1)} %get-tuple-element.200), channel_id=1, source_target_pairs={{0,192},{64,0},{128,64},{192,128},{1,193},{65,1},{129,65},{193,129... | collective-permute-start | bytes 196616 | tf_op jit(solution)/shard_map/ppermute | solution.py:47
  134.4 1.3 collective-permute-done.10
  135.6 1.4 collective-permute-done.11
  138.3 4.4 %collective-permute-start.12 = (f32[2,4,128,64]{2,3,1,0:T(8,128)S(1)}, f32[2,4,128,64]{2,3,1,0:T(8,128)S(1)}, u32[]{:S(2)}, u32[]{:S(2)}) collective-permute-start(f32[2,4,128,64]{2,3,1,0:T(8,128)S(1)} %get-tuple-element.184), channel_id=1, source_target_pairs={{0,16},{16,32},{32,48},{48,0},{1,17},{17,33},{33,49},{49,1},{2,18}... | collective-permute-start | bytes 786440 | tf_op jit(solution)/shard_map/ppermute | solution.py:47
  142.7 3.6 %collective-permute-start.13 = (f32[2,4,128,64]{2,3,1,0:T(8,128)S(1)}, f32[2,4,128,64]{2,3,1,0:T(8,128)S(1)}, u32[]{:S(2)}, u32[]{:S(2)}) collective-permute-start(f32[2,4,128,64]{2,3,1,0:T(8,128)S(1)} %get-tuple-element.185), channel_id=1, source_target_pairs={{0,32},{16,48},{32,0},{48,16},{1,33},{17,49},{33,1},{49,17},{2,34}... | collective-permute-start | bytes 786440 | tf_op jit(solution)/shard_map/ppermute | solution.py:47
  146.4 3.3 %collective-permute-start.14 = (f32[2,4,128,64]{2,3,1,0:T(8,128)S(1)}, f32[2,4,128,64]{2,3,1,0:T(8,128)S(1)}, u32[]{:S(2)}, u32[]{:S(2)}) collective-permute-start(f32[2,4,128,64]{2,3,1,0:T(8,128)S(1)} %get-tuple-element.186), channel_id=1, source_target_pairs={{0,48},{16,0},{32,16},{48,32},{1,49},{17,1},{33,17},{49,33},{2,50}... | collective-permute-start | bytes 786440 | tf_op jit(solution)/shard_map/ppermute | solution.py:47
  149.8 3.6 %while.18 = (s32[]{:T(128)}, f32[2,128,8,64]{1,3,2,0:T(8,128)}, f32[2,128,128]{2,1,0:T(8,128)S(1)}, f32[2,128,128]{2,1,0:T(8,128)S(1)}, bf16[2,128,8,64]{1,3,2,0...) while((s32[]{:T(128)}, f32[2,128,8,64]{1,3,2,0:T(8,128)}, ...), condition=%wide.region_3.4_spmd, body=%wide.region_1.3_spmd.sunk | while | flops 43515904 | bytes 1224821 | solution.py:192
  149.8 1.1 fusion.129
  151.7 1.1 fusion.129
  153.6 1.5 collective-permute-done.13
  155.2 1.3 collective-permute-done.14
  157.2 1.1 pad_maximum_fusion.3
  158.3 0.7 gather_fusion.2
  160.4 1.0 fusion.30
  162.2 1.0 fusion.31
  163.9 0.8 copy.124
  (249 shorter events, 27.8 us)
Async XLA Ops:
  1.9 5.1 %copy-start.9 = (f32[128,16]{0,1:T(8,128)}, f32[128,16]{0,1:T(8,128)S(1)}, u32[]{:S(2)}) copy-start(f32[128,16]{0,1:T(8,128)S(1)} %get-tuple-element.208) | copy-start | bytes 24580
  7.3 15.8 %copy-start.1 = (bf16[1,128,128]{2,1,0:T(8,128)(2,1)S(1)}, bf16[1,128,128]{2,1,0:T(8,128)(2,1)}, u32[]{:S(2)}) copy-start(bf16[1,128,128]{2,1,0:T(8,128)(2,1)} %param.19) | copy-start | bytes 98308
  7.3 15.8 %copy-start.3 = (bf16[1,128,128]{2,1,0:T(8,128)(2,1)S(1)}, bf16[1,128,128]{2,1,0:T(8,128)(2,1)}, u32[]{:S(2)}) copy-start(bf16[1,128,128]{2,1,0:T(8,128)(2,1)} %param.20) | copy-start | bytes 98308
  7.5 17.0 %collective-permute-start = (f32[2,4,136,64]{2,3,1,0:T(8,128)S(1)}, f32[2,4,136,64]{2,3,1,0:T(8,128)}, u32[]{:S(2)}, u32[]{:S(2)}) collective-permute-start(f32[2,4,136,64]{2,3,1,0:T(8,128)S(1)} %get-tuple-element.180), channel_id=1, source_target_pairs={{0,16},{16,32},{32,48},{48,0},{1,17},{17,33},{33,49},{49,1},{2,18}... | collective-permute-start | bytes 835592 | tf_op jit(solution)/shard_map/ppermute | solution.py:47
  10.9 25.7 %collective-permute-start.1 = (f32[2,4,136,64]{2,3,1,0:T(8,128)S(1)}, f32[2,4,136,64]{2,3,1,0:T(8,128)}, u32[]{:S(2)}, u32[]{:S(2)}) collective-permute-start(f32[2,4,136,64]{2,3,1,0:T(8,128)S(1)} %get-tuple-element.179), channel_id=1, source_target_pairs={{0,32},{16,48},{32,0},{48,16},{1,33},{17,49},{33,1},{49,17},{2,34}... | collective-permute-start | bytes 835592 | tf_op jit(solution)/shard_map/ppermute | solution.py:47
  15.6 22.6 %collective-permute-start.2 = (f32[2,4,136,64]{2,3,1,0:T(8,128)S(1)}, f32[2,4,136,64]{2,3,1,0:T(8,128)}, u32[]{:S(2)}, u32[]{:S(2)}) collective-permute-start(f32[2,4,136,64]{2,3,1,0:T(8,128)S(1)} %get-tuple-element.178), channel_id=1, source_target_pairs={{0,48},{16,0},{32,16},{48,32},{1,49},{17,1},{33,17},{49,33},{2,50}... | collective-permute-start | bytes 835592 | tf_op jit(solution)/shard_map/ppermute | solution.py:47
  19.0 22.8 %copy-start.20 = (pred[4]{0:T(512)(128)(4,1)}, pred[4]{0:T(512)(128)(4,1)S(1)}, u32[]{:S(2)}) copy-start(pred[4]{0:T(512)(128)(4,1)S(1)} %compare_and_fusion.2) | copy-start | bytes 16
  19.0 25.7 %copy-start.27 = (pred[4]{0:T(512)(128)(4,1)}, pred[4]{0:T(512)(128)(4,1)S(1)}, u32[]{:S(2)}) copy-start(pred[4]{0:T(512)(128)(4,1)S(1)} %iota_compare_fusion.7) | copy-start | bytes 16
  19.1 25.7 %copy-start.25 = (pred[4]{0:T(512)(128)(4,1)}, pred[4]{0:T(512)(128)(4,1)S(1)}, u32[]{:S(2)}) copy-start(pred[4]{0:T(512)(128)(4,1)S(1)} %iota_compare_fusion.8) | copy-start | bytes 16
  19.1 25.7 %copy-start.23 = (pred[4]{0:T(512)(128)(4,1)}, pred[4]{0:T(512)(128)(4,1)S(1)}, u32[]{:S(2)}) copy-start(pred[4]{0:T(512)(128)(4,1)S(1)} %iota_compare_fusion.9) | copy-start | bytes 16
  19.7 20.0 %copy-start.19 = (s32[1024]{0:T(1024)}, s32[1024]{0:T(1024)S(1)}, u32[]{:S(2)}) copy-start(s32[1024]{0:T(1024)S(1)} %pad_clamp_fusion.3) | copy-start | bytes 12292
  49.2 13.2 %copy-start.14 = (f32[4,4]{1,0:T(4,128)S(1)}, f32[4,4]{1,0:T(4,128)}, u32[]{:S(2)}) copy-start(f32[4,4]{1,0:T(4,128)} %get-tuple-element.218) | copy-start | bytes 196
  49.2 13.3 %copy-start.28 = (pred[4]{0:T(512)(128)(4,1)S(1)}, pred[4]{0:T(512)(128)(4,1)}, u32[]{:S(2)}) copy-start(pred[4]{0:T(512)(128)(4,1)} %copy-done.27) | copy-start | bytes 16
  49.2 13.4 %copy-start.13 = (f32[4,4]{1,0:T(4,128)S(1)}, f32[4,4]{1,0:T(4,128)}, u32[]{:S(2)}) copy-start(f32[4,4]{1,0:T(4,128)} %get-tuple-element.220) | copy-start | bytes 196
  49.2 13.5 %copy-start.26 = (pred[4]{0:T(512)(128)(4,1)S(1)}, pred[4]{0:T(512)(128)(4,1)}, u32[]{:S(2)}) copy-start(pred[4]{0:T(512)(128)(4,1)} %copy-done.25) | copy-start | bytes 16
  49.3 13.6 %copy-start.12 = (f32[4,4]{1,0:T(4,128)S(1)}, f32[4,4]{1,0:T(4,128)}, u32[]{:S(2)}) copy-start(f32[4,4]{1,0:T(4,128)} %get-tuple-element.222) | copy-start | bytes 196
  49.3 13.6 %copy-start.24 = (pred[4]{0:T(512)(128)(4,1)S(1)}, pred[4]{0:T(512)(128)(4,1)}, u32[]{:S(2)}) copy-start(pred[4]{0:T(512)(128)(4,1)} %copy-done.23) | copy-start | bytes 16
  49.3 13.7 %copy-start.15 = (f32[1,4,4]{2,1,0:T(4,128)S(1)}, f32[1,4,4]{2,1,0:T(4,128)}, u32[]{:S(2)}) copy-start(f32[1,4,4]{2,1,0:T(4,128)} %select_bitcast_fusion.10) | copy-start | bytes 196
  49.3 13.7 %copy-start.16 = (f32[1,4,4]{2,1,0:T(4,128)S(1)}, f32[1,4,4]{2,1,0:T(4,128)}, u32[]{:S(2)}) copy-start(f32[1,4,4]{2,1,0:T(4,128)} %select_bitcast_fusion.11) | copy-start | bytes 196
  49.3 13.7 %copy-start.17 = (f32[1,4,4]{2,1,0:T(4,128)S(1)}, f32[1,4,4]{2,1,0:T(4,128)}, u32[]{:S(2)}) copy-start(f32[1,4,4]{2,1,0:T(4,128)} %select_bitcast_fusion.8) | copy-start | bytes 196
  49.3 13.7 %copy-start.18 = (f32[1,4,4]{2,1,0:T(4,128)S(1)}, f32[1,4,4]{2,1,0:T(4,128)}, u32[]{:S(2)}) copy-start(f32[1,4,4]{2,1,0:T(4,128)} %select_bitcast_fusion.9) | copy-start | bytes 196
  49.3 13.7 %copy-start = (f32[4,4,128,64]{2,3,1,0:T(8,128)S(1)}, f32[4,4,128,64]{2,3,1,0:T(8,128)}, u32[]{:S(2)}) copy-start(f32[4,4,128,64]{2,3,1,0:T(8,128)} %get-tuple-element.175) | copy-start | bytes 1572868
  49.4 13.9 %copy-start.35 = (f32[4]{0:T(128)S(1)}, f32[4]{0:T(128)}, u32[]{:S(2)}) copy-start(f32[4]{0:T(128)} %get-tuple-element.217) | copy-start | bytes 52
  49.4 13.9 %copy-start.36 = (f32[4]{0:T(128)S(1)}, f32[4]{0:T(128)}, u32[]{:S(2)}) copy-start(f32[4]{0:T(128)} %get-tuple-element.219) | copy-start | bytes 52
  49.4 13.9 %copy-start.37 = (f32[4]{0:T(128)S(1)}, f32[4]{0:T(128)}, u32[]{:S(2)}) copy-start(f32[4]{0:T(128)} %get-tuple-element.221) | copy-start | bytes 52
  49.4 13.9 %copy-start.38 = (f32[4]{0:T(128)S(1)}, f32[4]{0:T(128)}, u32[]{:S(2)}) copy-start(f32[4]{0:T(128)} %pad.94.clone) | copy-start | bytes 52
  49.4 14.5 %copy-start.39 = (f32[4]{0:T(128)S(1)}, f32[4]{0:T(128)}, u32[]{:S(2)}) copy-start(f32[4]{0:T(128)} %pad.98.clone) | copy-start | bytes 52
  49.6 14.7 %collective-permute-start.3 = (f32[2,1,136,64]{2,3,0,1:T(8,128)S(1)}, f32[2,1,136,64]{2,3,0,1:T(8,128)S(1)}, u32[]{:S(2)}, u32[]{:S(2)}) collective-permute-start(f32[2,1,136,64]{2,3,0,1:T(8,128)S(1)} %get-tuple-element.192), channel_id=1, source_target_pairs={{0,64},{64,128},{128,192},{192,0},{1,65},{65,129},{129,193},{193,1... | collective-permute-start | bytes 208904 | tf_op jit(solution)/shard_map/ppermute | solution.py:47
  53.9 12.3 %collective-permute-start.4 = (f32[2,1,136,64]{2,3,0,1:T(8,128)S(1)}, f32[2,1,136,64]{2,3,0,1:T(8,128)S(1)}, u32[]{:S(2)}, u32[]{:S(2)}) collective-permute-start(f32[2,1,136,64]{2,3,0,1:T(8,128)S(1)} %get-tuple-element.191), channel_id=1, source_target_pairs={{0,128},{64,192},{128,0},{192,64},{1,129},{65,193},{129,1},{193,65... | collective-permute-start | bytes 208904 | tf_op jit(solution)/shard_map/ppermute | solution.py:47
  60.0 8.0 %collective-permute-start.5 = (f32[2,1,136,64]{2,3,0,1:T(8,128)S(1)}, f32[2,1,136,64]{2,3,0,1:T(8,128)S(1)}, u32[]{:S(2)}, u32[]{:S(2)}) collective-permute-start(f32[2,1,136,64]{2,3,0,1:T(8,128)S(1)} %get-tuple-element.190), channel_id=1, source_target_pairs={{0,192},{64,0},{128,64},{192,128},{1,193},{65,1},{129,65},{193,129... | collective-permute-start | bytes 208904 | tf_op jit(solution)/shard_map/ppermute | solution.py:47
  74.7 34.6 %collective-permute-start.6 = (f32[2,1,136,64]{2,3,0,1:T(8,128)S(1)}, f32[2,1,136,64]{2,3,0,1:T(8,128)S(1)}, u32[]{:S(2)}, u32[]{:S(2)}) collective-permute-start(f32[2,1,136,64]{2,3,0,1:T(8,128)S(1)} %get-tuple-element.202), channel_id=1, source_target_pairs={{0,256},{256,512},{512,768},{768,0},{1,257},{257,513},{513,769},{7... | collective-permute-start | bytes 208904 | tf_op jit(solution)/shard_map/ppermute | solution.py:95
  85.6 30.8 %collective-permute-start.7 = (f32[2,1,136,64]{2,3,0,1:T(8,128)S(1)}, f32[2,1,136,64]{2,3,0,1:T(8,128)S(1)}, u32[]{:S(2)}, u32[]{:S(2)}) collective-permute-start(f32[2,1,136,64]{2,3,0,1:T(8,128)S(1)} %get-tuple-element.202), channel_id=1, source_target_pairs={{0,512},{256,768},{512,0},{768,256},{1,513},{257,769},{513,1},{769... | collective-permute-start | bytes 208904 | tf_op jit(solution)/shard_map/ppermute | solution.py:95
  97.4 24.6 %collective-permute-start.8 = (f32[2,1,136,64]{2,3,0,1:T(8,128)S(1)}, f32[2,1,136,64]{2,3,0,1:T(8,128)S(1)}, u32[]{:S(2)}, u32[]{:S(2)}) collective-permute-start(f32[2,1,136,64]{2,3,0,1:T(8,128)S(1)} %get-tuple-element.202), channel_id=1, source_target_pairs={{0,768},{256,0},{512,256},{768,512},{1,769},{257,1},{513,257},{769... | collective-permute-start | bytes 208904 | tf_op jit(solution)/shard_map/ppermute | solution.py:95
  122.0 2.5 %copy-start.30 = (f32[4]{0:T(128)S(1)}, f32[4]{0:T(128)}, u32[]{:S(2)}) copy-start(f32[4]{0:T(128)} %maximum_bitcast_fusion.5) | copy-start | bytes 52
  122.1 12.2 %copy-start.31 = (f32[4]{0:T(128)S(1)}, f32[4]{0:T(128)}, u32[]{:S(2)}) copy-start(f32[4]{0:T(128)} %get-tuple-element.161) | copy-start | bytes 52
  122.1 12.2 %copy-start.32 = (f32[4]{0:T(128)S(1)}, f32[4]{0:T(128)}, u32[]{:S(2)}) copy-start(f32[4]{0:T(128)} %get-tuple-element.209) | copy-start | bytes 52
  122.1 12.3 %copy-start.33 = (f32[4]{0:T(128)S(1)}, f32[4]{0:T(128)}, u32[]{:S(2)}) copy-start(f32[4]{0:T(128)} %get-tuple-element.211) | copy-start | bytes 52
  122.1 12.3 %copy-start.34 = (f32[4]{0:T(128)S(1)}, f32[4]{0:T(128)}, u32[]{:S(2)}) copy-start(f32[4]{0:T(128)} %get-tuple-element.213) | copy-start | bytes 52
  122.8 15.0 %copy-start.22 = (pred[4]{0:T(512)(128)(4,1)S(1)}, pred[4]{0:T(512)(128)(4,1)}, u32[]{:S(2)}) copy-start(pred[4]{0:T(512)(128)(4,1)} %compare_and_fusion.1) | copy-start | bytes 16
  124.7 13.4 %copy-start.11 = (f32[4,4]{1,0:T(4,128)S(1)}, f32[4,4]{1,0:T(4,128)}, u32[]{:S(2)}) copy-start(f32[4,4]{1,0:T(4,128)} %pad_maximum_fusion.9) | copy-start | bytes 196
  124.7 9.6 %collective-permute-start.9 = (f32[2,1,128,64]{2,3,0,1:T(8,128)S(1)}, f32[2,1,128,64]{2,3,0,1:T(8,128)S(1)}, u32[]{:S(2)}, u32[]{:S(2)}) collective-permute-start(f32[2,1,128,64]{2,3,0,1:T(8,128)S(1)} %get-tuple-element.198), channel_id=1, source_target_pairs={{0,64},{64,128},{128,192},{192,0},{1,65},{65,129},{129,193},{193,1... | collective-permute-start | bytes 196616 | tf_op jit(solution)/shard_map/ppermute | solution.py:47
  127.2 8.5 %collective-permute-start.10 = (f32[2,1,128,64]{2,3,0,1:T(8,128)S(1)}, f32[2,1,128,64]{2,3,0,1:T(8,128)S(1)}, u32[]{:S(2)}, u32[]{:S(2)}) collective-permute-start(f32[2,1,128,64]{2,3,0,1:T(8,128)S(1)} %get-tuple-element.199), channel_id=1, source_target_pairs={{0,128},{64,192},{128,0},{192,64},{1,129},{65,193},{129,1},{193,65... | collective-permute-start | bytes 196616 | tf_op jit(solution)/shard_map/ppermute | solution.py:47
  129.1 8.0 %collective-permute-start.11 = (f32[2,1,128,64]{2,3,0,1:T(8,128)S(1)}, f32[2,1,128,64]{2,3,0,1:T(8,128)S(1)}, u32[]{:S(2)}, u32[]{:S(2)}) collective-permute-start(f32[2,1,128,64]{2,3,0,1:T(8,128)S(1)} %get-tuple-element.200), channel_id=1, source_target_pairs={{0,192},{64,0},{128,64},{192,128},{1,193},{65,1},{129,65},{193,129... | collective-permute-start | bytes 196616 | tf_op jit(solution)/shard_map/ppermute | solution.py:47
  138.0 11.7 %copy-start.6 = (f32[2,128,128]{2,1,0:T(8,128)S(1)}, f32[2,128,128]{2,1,0:T(8,128)}, u32[]{:S(2)}) copy-start(f32[2,128,128]{2,1,0:T(8,128)} %custom-call.11) | copy-start | bytes 393220
  138.0 11.7 %copy-start.7 = (f32[2,128,128]{2,1,0:T(8,128)S(1)}, f32[2,128,128]{2,1,0:T(8,128)}, u32[]{:S(2)}) copy-start(f32[2,128,128]{2,1,0:T(8,128)} %custom-call.12) | copy-start | bytes 393220
  138.3 15.4 %collective-permute-start.12 = (f32[2,4,128,64]{2,3,1,0:T(8,128)S(1)}, f32[2,4,128,64]{2,3,1,0:T(8,128)S(1)}, u32[]{:S(2)}, u32[]{:S(2)}) collective-permute-start(f32[2,4,128,64]{2,3,1,0:T(8,128)S(1)} %get-tuple-element.184), channel_id=1, source_target_pairs={{0,16},{16,32},{32,48},{48,0},{1,17},{17,33},{33,49},{49,1},{2,18}... | collective-permute-start | bytes 786440 | tf_op jit(solution)/shard_map/ppermute | solution.py:47
  142.7 12.4 %collective-permute-start.13 = (f32[2,4,128,64]{2,3,1,0:T(8,128)S(1)}, f32[2,4,128,64]{2,3,1,0:T(8,128)S(1)}, u32[]{:S(2)}, u32[]{:S(2)}) collective-permute-start(f32[2,4,128,64]{2,3,1,0:T(8,128)S(1)} %get-tuple-element.185), channel_id=1, source_target_pairs={{0,32},{16,48},{32,0},{48,16},{1,33},{17,49},{33,1},{49,17},{2,34}... | collective-permute-start | bytes 786440 | tf_op jit(solution)/shard_map/ppermute | solution.py:47
  146.4 10.1 %collective-permute-start.14 = (f32[2,4,128,64]{2,3,1,0:T(8,128)S(1)}, f32[2,4,128,64]{2,3,1,0:T(8,128)S(1)}, u32[]{:S(2)}, u32[]{:S(2)}) collective-permute-start(f32[2,4,128,64]{2,3,1,0:T(8,128)S(1)} %get-tuple-element.186), channel_id=1, source_target_pairs={{0,48},{16,0},{32,16},{48,32},{1,49},{17,1},{33,17},{49,33},{2,50}... | collective-permute-start | bytes 786440 | tf_op jit(solution)/shard_map/ppermute | solution.py:47
  (7 other events, 7.9 us)

commit v7 on v6

--- a/solution.py
+++ b/solution.py
@@ -15,19 +15,19 @@
 
 
 def lower_weights(p, idx):
-    k = jnp.arange(p.shape[0])[:, None]
-    q = jnp.where(k < idx, p, 1.0)
-    c = jnp.cumprod(q[::-1], axis=0)[::-1]
-    after = jnp.concatenate([c[1:], jnp.ones_like(c[:1])], axis=0)
-    return jnp.where(k < idx, after, 0.0)
+    j = jnp.arange(p.shape[0])[:, None]
+    k = jnp.arange(p.shape[0])[None, :]
+    span = ((j < k) & (k < idx))[:, :, None]
+    w = jnp.prod(jnp.where(span, p[None], 1.0), axis=1)
+    return jnp.where(j < idx, w, 0.0)
 
 
 def upper_weights(p, idx):
-    k = jnp.arange(p.shape[0])[:, None]
-    q = jnp.where(k > idx, p, 1.0)
-    c = jnp.cumprod(q, axis=0)
-    before = jnp.concatenate([jnp.ones_like(c[:1]), c[:-1]], axis=0)
-    return jnp.where(k > idx, before, 0.0)
+    j = jnp.arange(p.shape[0])[:, None]
+    k = jnp.arange(p.shape[0])[None, :]
+    span = ((idx < k) & (k < j))[:, :, None]
+    w = jnp.prod(jnp.where(span, p[None], 1.0), axis=1)
+    return jnp.where(j > idx, w, 0.0)
 
 
 def weighted(w, states):
@@ -46,6 +46,15 @@
         send = jnp.take(pieces, (index + shift) % count, axis=0)
         got.append(lax.ppermute(send, axis, [(i, (i + shift) % count) for i in range(count)]))
     return jnp.take(jnp.stack(got), (index - jnp.arange(count)) % count, axis=0)
+
+
+def exchange_received(pieces, axis):
+    count, index = lax.axis_size(axis), lax.axis_index(axis)
+    got = [jnp.take(pieces, index, axis=0)]
+    for shift in range(1, count):
+        send = jnp.take(pieces, (index + shift) % count, axis=0)
+        got.append(lax.ppermute(send, axis, [(i, (i + shift) % count) for i in range(count)]))
+    return jnp.stack(got)
 
 
 def all_weights(p, lower):
@@ -111,14 +120,16 @@
         return z_scan(own_f, whole, True), z_scan(own_b, whole, False)
     part = heads // count
     pieces = jnp.stack([own_f, own_b]).reshape(2, count, part, n + 8, width)
-    members = exchange(jnp.transpose(pieces, (1, 0, 2, 3, 4)), axis)
-    group = members[:, 0, :, n, 0]
-    fwd_all, back_all = members[:, 0, :, :n], members[:, 1, :, :n]
-    w_f, w_b = all_weights(group, True), all_weights(group, False)
+    received = exchange_received(jnp.transpose(pieces, (1, 0, 2, 3, 4)), axis)
+    slot = (lax.axis_index(axis) - jnp.arange(count)) % count
+    group = jnp.take(received[:, 0, :, n, 0], slot, axis=0)
+    fwd_all, back_all = received[:, 0, :, :n], received[:, 1, :, :n]
+    w_f = jnp.take(all_weights(group, True), slot, axis=1)
+    w_b = jnp.take(all_weights(group, False), slot, axis=1)
     local_f = (w_f[:, :, :, None, None] * fwd_all[None]).sum(axis=1)
     local_b = (w_b[:, :, :, None, None] * back_all[None]).sum(axis=1)
-    agg_f = weighted(lower_weights(group, count), fwd_all)
-    agg_b = weighted(upper_weights(group, -1), back_all)
+    agg_f = weighted(jnp.take(lower_weights(group, count), slot, axis=0), fwd_all)
+    agg_b = weighted(jnp.take(upper_weights(group, -1), slot, axis=0), back_all)
     k = jnp.arange(count)[:, None]
     lead_f = jnp.stack([jnp.prod(jnp.where(k < x, group, 1.0), axis=0) for x in range(count)])
     lead_b = jnp.stack([jnp.prod(jnp.where(k > x, group, 1.0), axis=0) for x in range(count)])

time: 167 us -> 161 us (0.964)
  waiting for transfers between devices: 37 us -> 29.8 us
    ppermute x0 -> x6, starting transfers between devices: none -> 24.2 us  [exchange_received(): lax.ppermute(send, axis, [(i, (i + shift) % count) for i in range(count)])]
    ppermute x12 -> x6, starting transfers between devices: 45.2 us -> 22.8 us  [exchange(): lax.ppermute(send, axis, [(i, (i + shift) % count) for i in range(count)])]
    ppermute x12 -> x6, waiting for transfers between devices: 24.2 us -> 5.24 us  [exchange(): lax.ppermute(send, axis, [(i, (i + shift) % count) for i in range(count)])]
    ppermute x0 -> x6, waiting for transfers between devices: none -> 12.7 us  [exchange_received(): lax.ppermute(send, axis, [(i, (i + shift) % count) for i in range(count)])]
    gather x0 -> x12, local copies, waits for them, and re-layouts: none -> 6.04 us  [the longest x3 1.22 us: entry_states(): w_b = jnp.take(all_weights(group, False), slot, axis=1)]
    and x0 -> x9, other arithmetic: none -> 5.05 us  [the longest x5 2.72 us: upper_weights(): span = ((idx < k) & (k < j))[:, :, None]]
    another operation x11 -> x4, other arithmetic: 2.93 us -> 0.06 us  [all_weights(): return jnp.stack(rows)]
    gather x4 -> x2, local copies, waits for them, and re-layouts: 4.16 us -> 1.3 us  [exchange(): return jnp.take(jnp.stack(got), (index - jnp.arange(count)) % count, axis=0)]
  transfers between devices with their start and end apart: 15 -> 15, of which waited for: 11 -> 10; matrix products, arithmetic and copies ran while one was open for 11% -> 15% of each run, Pallas kernels for 0% -> 0%
where the time goes in v7:
time: 161 us; the launch traced here: 159 us
  starting transfers between devices  73.2 us (45%)
  waiting for transfers between devices  29.8 us (19%)
  other arithmetic  29.4 us (18%)
  local copies, waits for them, and re-layouts  17.1 us (11%)
  matrix products  6.99 us (4%)
  between operations  1.88 us (1%)
    ppermute x3, starting transfers between devices, gathered_scan(): lax.ppermute(mine, axis, [(i, (i + shift) % count) for i in range(count)])  26.3 us
    ppermute x6, starting transfers between devices, exchange_received(): lax.ppermute(send, axis, [(i, (i + shift) % count) for i in range(count)])  24.2 us
    ppermute x6, starting transfers between devices, exchange(): lax.ppermute(send, axis, [(i, (i + shift) % count) for i in range(count)])  22.8 us
    ppermute x6, waiting for transfers between devices, exchange_received(): lax.ppermute(send, axis, [(i, (i + shift) % count) for i in range(count)])  12.7 us
    ppermute x3, waiting for transfers between devices, gathered_scan(): lax.ppermute(mine, axis, [(i, (i + shift) % count) for i in range(count)])  11.9 us
    unnamed x87, local copies, waits for them, and re-layouts  6.37 us
    ppermute x6, waiting for transfers between devices, exchange(): lax.ppermute(send, axis, [(i, (i + shift) % count) for i in range(count)])  5.24 us
  transfers between devices with their start and end apart: 15, of which 10 were waited for; matrix products, arithmetic and copies ran while one was open for 15% of the time, Pallas kernels for 0%

profile of v7, /device:TPU:56, one launch (start us, length us, event | category | flops | bytes accessed | tf_op | source)
XLA Modules:
  0.0 158.5 jit_solution(10911455035777568759)
XLA Ops:
  0.7 1.0 reduce_window_sum.11
  2.0 1.1 copy.325
  3.1 0.8 bitcast_convert_fusion
  3.9 1.1 copy.324
  5.0 0.8 bitcast_convert_fusion.1
  7.3 1.2 dynamic-slice_select_fusion
  8.5 3.4 %collective-permute-start = (f32[2,4,136,64]{2,3,1,0:T(8,128)}, f32[2,4,136,64]{2,3,1,0:T(8,128)S(1)}, u32[]{:S(2)}, u32[]{:S(2)}) collective-permute-start(f32[2,4,136,64]{2,3,1,0:T(8,128)} %get-tuple-element.212), channel_id=1, source_target_pairs={{0,16},{16,32},{32,48},{48,0},{1,17},{17,33},{33,49},{49,1},{2,18}... | collective-permute-start | bytes 835592 | tf_op jit(solution)/shard_map/ppermute | solution.py:56
  11.9 4.6 %collective-permute-start.1 = (f32[2,4,136,64]{2,3,1,0:T(8,128)}, f32[2,4,136,64]{2,3,1,0:T(8,128)S(1)}, u32[]{:S(2)}, u32[]{:S(2)}) collective-permute-start(f32[2,4,136,64]{2,3,1,0:T(8,128)} %get-tuple-element.211), channel_id=1, source_target_pairs={{0,32},{16,48},{32,0},{48,16},{1,33},{17,49},{33,1},{49,17},{2,34}... | collective-permute-start | bytes 835592 | tf_op jit(solution)/shard_map/ppermute | solution.py:56
  16.5 3.3 %collective-permute-start.2 = (f32[2,4,136,64]{2,3,1,0:T(8,128)S(1)}, f32[2,4,136,64]{2,3,1,0:T(8,128)S(1)}, u32[]{:S(2)}, u32[]{:S(2)}) collective-permute-start(f32[2,4,136,64]{2,3,1,0:T(8,128)S(1)} %get-tuple-element.210), channel_id=1, source_target_pairs={{0,48},{16,0},{32,16},{48,32},{1,49},{17,1},{33,17},{49,33},{2,50}... | collective-permute-start | bytes 835592 | tf_op jit(solution)/shard_map/ppermute | solution.py:56
  31.1 6.6 %collective-permute-done.1 = f32[2,4,136,64]{2,3,1,0:T(8,128)S(1)} collective-permute-done((f32[2,4,136,64]{2,3,1,0:T(8,128)}, f32[2,4,136,64]{2,3,1,0:T(8,128)S(1)}, u32[]{:S(2)}, u32[]{:S(2)}) %collective-permute-start.1) | collective-permute-done | bytes 278560 | tf_op jit(solution)/shard_map/ppermute | solution.py:56
  37.7 1.6 collective-permute-done.2
  45.0 4.3 %collective-permute-start.3 = (f32[2,1,136,64]{2,3,0,1:T(8,128)S(1)}, f32[2,1,136,64]{2,3,0,1:T(8,128)S(1)}, u32[]{:S(2)}, u32[]{:S(2)}) collective-permute-start(f32[2,1,136,64]{2,3,0,1:T(8,128)S(1)} %get-tuple-element.224), channel_id=1, source_target_pairs={{0,64},{64,128},{128,192},{192,0},{1,65},{65,129},{129,193},{193,1... | collective-permute-start | bytes 208904 | tf_op jit(solution)/shard_map/ppermute | solution.py:56
  49.3 6.1 %collective-permute-start.4 = (f32[2,1,136,64]{2,3,0,1:T(8,128)S(1)}, f32[2,1,136,64]{2,3,0,1:T(8,128)S(1)}, u32[]{:S(2)}, u32[]{:S(2)}) collective-permute-start(f32[2,1,136,64]{2,3,0,1:T(8,128)S(1)} %get-tuple-element.223), channel_id=1, source_target_pairs={{0,128},{64,192},{128,0},{192,64},{1,129},{65,193},{129,1},{193,65... | collective-permute-start | bytes 208904 | tf_op jit(solution)/shard_map/ppermute | solution.py:56
  55.4 2.5 %collective-permute-start.5 = (f32[2,1,136,64]{2,3,1,0:T(8,128)S(1)}, f32[2,1,136,64]{2,3,1,0:T(8,128)S(1)}, u32[]{:S(2)}, u32[]{:S(2)}) collective-permute-start(f32[2,1,136,64]{2,3,1,0:T(8,128)S(1)} %get-tuple-element.222), channel_id=1, source_target_pairs={{0,192},{64,0},{128,64},{192,128},{1,193},{65,1},{129,65},{193,129... | collective-permute-start | bytes 208904 | tf_op jit(solution)/shard_map/ppermute | solution.py:56
  59.0 2.6 %collective-permute-done.4 = f32[2,1,136,64]{2,3,0,1:T(8,128)S(1)} collective-permute-done((f32[2,1,136,64]{2,3,0,1:T(8,128)S(1)}, f32[2,1,136,64]{2,3,0,1:T(8,128)S(1)}, u32[]{:S(2)}, u32[]{:S(2)}) %collective-permute-start.4) | collective-permute-done | bytes 69664 | tf_op jit(solution)/shard_map/ppermute | solution.py:56
  61.6 1.9 %collective-permute-done.5 = f32[2,1,136,64]{2,3,1,0:T(8,128)S(1)} collective-permute-done((f32[2,1,136,64]{2,3,1,0:T(8,128)S(1)}, f32[2,1,136,64]{2,3,1,0:T(8,128)S(1)}, u32[]{:S(2)}, u32[]{:S(2)}) %collective-permute-start.5) | collective-permute-done | bytes 69664 | tf_op jit(solution)/shard_map/ppermute | solution.py:56
  64.3 0.8 fusion.102
  68.0 10.9 %collective-permute-start.6 = (f32[2,1,136,64]{2,3,0,1:T(8,128)S(1)}, f32[2,1,136,64]{2,3,0,1:T(8,128)S(1)}, u32[]{:S(2)}, u32[]{:S(2)}) collective-permute-start(f32[2,1,136,64]{2,3,0,1:T(8,128)S(1)} %get-tuple-element.234), channel_id=1, source_target_pairs={{0,256},{256,512},{512,768},{768,0},{1,257},{257,513},{513,769},{7... | collective-permute-start | bytes 208904 | tf_op jit(solution)/shard_map/ppermute | solution.py:104
  78.9 11.7 %collective-permute-start.7 = (f32[2,1,136,64]{2,3,0,1:T(8,128)S(1)}, f32[2,1,136,64]{2,3,0,1:T(8,128)S(1)}, u32[]{:S(2)}, u32[]{:S(2)}) collective-permute-start(f32[2,1,136,64]{2,3,0,1:T(8,128)S(1)} %get-tuple-element.234), channel_id=1, source_target_pairs={{0,512},{256,768},{512,0},{768,256},{1,513},{257,769},{513,1},{769... | collective-permute-start | bytes 208904 | tf_op jit(solution)/shard_map/ppermute | solution.py:104
  90.6 3.6 %collective-permute-start.8 = (f32[2,1,136,64]{2,3,0,1:T(8,128)S(1)}, f32[2,1,136,64]{2,3,0,1:T(8,128)S(1)}, u32[]{:S(2)}, u32[]{:S(2)}) collective-permute-start(f32[2,1,136,64]{2,3,0,1:T(8,128)S(1)} %get-tuple-element.234), channel_id=1, source_target_pairs={{0,768},{256,0},{512,256},{768,512},{1,769},{257,1},{513,257},{769... | collective-permute-start | bytes 208904 | tf_op jit(solution)/shard_map/ppermute | solution.py:104
  96.1 2.6 %maximum_bitcast_fusion.4 = f32[4]{0:T(128)S(1)} fusion(f32[1,1]{0,1:T(1,128)} %bitcast.113, f32[1,1]{0,1:T(1,128)} %bitcast.112, f32[1,1]{0,1:T(1,128)} %bitcast.111, f32[1,1]{0,1:T(1,128)} %bitcast.110), kind=kLoop, calls=%fused_computation.318 | loop fusion | flops 12 | bytes 32 | tf_op jit(solution)/shard_map/mul | solution.py:139
  98.7 2.5 %maximum_bitcast_fusion.3 = f32[4]{0:T(128)} fusion(f32[1,1]{0,1:T(1,128)} %bitcast.75, f32[1,1]{0,1:T(1,128)} %bitcast.74, f32[1,1]{0,1:T(1,128)} %bitcast.73, f32[1,1]{0,1:T(1,128)} %constant.265.clone.1), kind=kLoop, calls=%fused_computation.317 | loop fusion | flops 12 | bytes 32 | tf_op jit(solution)/shard_map/mul | solution.py:138
  101.2 9.3 %collective-permute-done.7 = f32[2,1,136,64]{2,3,0,1:T(8,128)S(1)} collective-permute-done((f32[2,1,136,64]{2,3,0,1:T(8,128)S(1)}, f32[2,1,136,64]{2,3,0,1:T(8,128)S(1)}, u32[]{:S(2)}, u32[]{:S(2)}) %collective-permute-start.7) | collective-permute-done | bytes 69664 | tf_op jit(solution)/shard_map/ppermute | solution.py:104
  110.5 2.6 %collective-permute-done.8 = f32[2,1,136,64]{2,3,0,1:T(8,128)S(1)} collective-permute-done((f32[2,1,136,64]{2,3,0,1:T(8,128)S(1)}, f32[2,1,136,64]{2,3,0,1:T(8,128)S(1)}, u32[]{:S(2)}, u32[]{:S(2)}) %collective-permute-start.8) | collective-permute-done | bytes 69664 | tf_op jit(solution)/shard_map/ppermute | solution.py:104
  113.2 0.7 gather_fusion
  113.9 0.8 bitcast_select_fusion
  114.8 0.8 select_reduce_fusion.13
  115.8 0.7 bitcast_add_fusion.3
  116.6 3.5 %collective-permute-start.9 = (f32[2,1,128,64]{2,3,0,1:T(8,128)S(1)}, f32[2,1,128,64]{2,3,0,1:T(8,128)S(1)}, u32[]{:S(2)}, u32[]{:S(2)}) collective-permute-start(f32[2,1,128,64]{2,3,0,1:T(8,128)S(1)} %get-tuple-element.230), channel_id=1, source_target_pairs={{0,64},{64,128},{128,192},{192,0},{1,65},{65,129},{129,193},{193,1... | collective-permute-start | bytes 196616 | tf_op jit(solution)/shard_map/ppermute | solution.py:47
  120.1 1.9 %collective-permute-start.10 = (f32[2,1,128,64]{2,3,0,1:T(8,128)S(1)}, f32[2,1,128,64]{2,3,0,1:T(8,128)S(1)}, u32[]{:S(2)}, u32[]{:S(2)}) collective-permute-start(f32[2,1,128,64]{2,3,0,1:T(8,128)S(1)} %get-tuple-element.231), channel_id=1, source_target_pairs={{0,128},{64,192},{128,0},{192,64},{1,129},{65,193},{129,1},{193,65... | collective-permute-start | bytes 196616 | tf_op jit(solution)/shard_map/ppermute | solution.py:47
  122.0 4.3 %collective-permute-start.11 = (f32[2,1,128,64]{2,3,0,1:T(8,128)S(1)}, f32[2,1,128,64]{2,3,0,1:T(8,128)S(1)}, u32[]{:S(2)}, u32[]{:S(2)}) collective-permute-start(f32[2,1,128,64]{2,3,0,1:T(8,128)S(1)} %get-tuple-element.232), channel_id=1, source_target_pairs={{0,192},{64,0},{128,64},{192,128},{1,193},{65,1},{129,65},{193,129... | collective-permute-start | bytes 196616 | tf_op jit(solution)/shard_map/ppermute | solution.py:47
  126.3 0.7 pad_maximum_fusion.20
  127.0 0.9 collective-permute-done.10
  127.9 1.1 collective-permute-done.11
  130.2 6.6 %collective-permute-start.12 = (f32[2,4,128,64]{2,3,1,0:T(8,128)S(1)}, f32[2,4,128,64]{2,3,1,0:T(8,128)S(1)}, u32[]{:S(2)}, u32[]{:S(2)}) collective-permute-start(f32[2,4,128,64]{2,3,1,0:T(8,128)S(1)} %get-tuple-element.216), channel_id=1, source_target_pairs={{0,16},{16,32},{32,48},{48,0},{1,17},{17,33},{33,49},{49,1},{2,18}... | collective-permute-start | bytes 786440 | tf_op jit(solution)/shard_map/ppermute | solution.py:47
  136.7 3.6 %collective-permute-start.13 = (f32[2,4,128,64]{2,3,1,0:T(8,128)S(1)}, f32[2,4,128,64]{2,3,1,0:T(8,128)S(1)}, u32[]{:S(2)}, u32[]{:S(2)}) collective-permute-start(f32[2,4,128,64]{2,3,1,0:T(8,128)S(1)} %get-tuple-element.217), channel_id=1, source_target_pairs={{0,32},{16,48},{32,0},{48,16},{1,33},{17,49},{33,1},{49,17},{2,34}... | collective-permute-start | bytes 786440 | tf_op jit(solution)/shard_map/ppermute | solution.py:47
  140.4 2.9 %collective-permute-start.14 = (f32[2,4,128,64]{2,3,1,0:T(8,128)S(1)}, f32[2,4,128,64]{2,3,1,0:T(8,128)S(1)}, u32[]{:S(2)}, u32[]{:S(2)}) collective-permute-start(f32[2,4,128,64]{2,3,1,0:T(8,128)S(1)} %get-tuple-element.218), channel_id=1, source_target_pairs={{0,48},{16,0},{32,16},{48,32},{1,49},{17,1},{33,17},{49,33},{2,50}... | collective-permute-start | bytes 786440 | tf_op jit(solution)/shard_map/ppermute | solution.py:47
  143.3 3.6 %while.18 = (s32[]{:T(128)}, f32[2,128,8,64]{1,3,2,0:T(8,128)}, f32[2,128,128]{2,1,0:T(8,128)S(1)}, f32[2,128,128]{2,1,0:T(8,128)S(1)}, bf16[2,128,8,64]{1,3,2,0...) while((s32[]{:T(128)}, f32[2,128,8,64]{1,3,2,0:T(8,128)}, ...), condition=%wide.region_3.4_spmd, body=%wide.region_1.3_spmd.sunk | while | flops 43515904 | bytes 1224821 | solution.py:203
  143.4 1.1 fusion.148
  145.2 1.1 fusion.148
  147.2 2.0 %collective-permute-done.13 = f32[2,4,128,64]{2,3,1,0:T(8,128)S(1)} collective-permute-done((f32[2,4,128,64]{2,3,1,0:T(8,128)S(1)}, f32[2,4,128,64]{2,3,1,0:T(8,128)S(1)}, u32[]{:S(2)}, u32[]{:S(2)}) %collective-permute-start.13) | collective-permute-done | bytes 262176 | tf_op jit(solution)/shard_map/ppermute | solution.py:47
  149.2 1.3 collective-permute-done.14
  151.2 1.0 pad_maximum_fusion.3
  154.2 1.0 fusion.30
  155.2 0.7 copy.362
  156.0 1.0 fusion.31
  157.0 0.7 copy.361
  157.7 0.8 copy.360
  (235 shorter events, 30.5 us)
Async XLA Ops:
  1.9 5.1 %copy-start.4 = (f32[128,16]{0,1:T(8,128)}, f32[128,16]{0,1:T(8,128)S(1)}, u32[]{:S(2)}) copy-start(f32[128,16]{0,1:T(8,128)S(1)} %get-tuple-element.240) | copy-start | bytes 24580
  7.3 23.6 %copy-start = (bf16[1,128,128]{2,1,0:T(8,128)(2,1)S(1)}, bf16[1,128,128]{2,1,0:T(8,128)(2,1)}, u32[]{:S(2)}) copy-start(bf16[1,128,128]{2,1,0:T(8,128)(2,1)} %param.25) | copy-start | bytes 98308
  7.3 23.6 %copy-start.2 = (bf16[1,128,128]{2,1,0:T(8,128)(2,1)S(1)}, bf16[1,128,128]{2,1,0:T(8,128)(2,1)}, u32[]{:S(2)}) copy-start(bf16[1,128,128]{2,1,0:T(8,128)(2,1)} %param.26) | copy-start | bytes 98308
  8.5 22.6 %collective-permute-start = (f32[2,4,136,64]{2,3,1,0:T(8,128)}, f32[2,4,136,64]{2,3,1,0:T(8,128)S(1)}, u32[]{:S(2)}, u32[]{:S(2)}) collective-permute-start(f32[2,4,136,64]{2,3,1,0:T(8,128)} %get-tuple-element.212), channel_id=1, source_target_pairs={{0,16},{16,32},{32,48},{48,0},{1,17},{17,33},{33,49},{49,1},{2,18}... | collective-permute-start | bytes 835592 | tf_op jit(solution)/shard_map/ppermute | solution.py:56
  11.9 25.8 %collective-permute-start.1 = (f32[2,4,136,64]{2,3,1,0:T(8,128)}, f32[2,4,136,64]{2,3,1,0:T(8,128)S(1)}, u32[]{:S(2)}, u32[]{:S(2)}) collective-permute-start(f32[2,4,136,64]{2,3,1,0:T(8,128)} %get-tuple-element.211), channel_id=1, source_target_pairs={{0,32},{16,48},{32,0},{48,16},{1,33},{17,49},{33,1},{49,17},{2,34}... | collective-permute-start | bytes 835592 | tf_op jit(solution)/shard_map/ppermute | solution.py:56
  16.5 22.7 %collective-permute-start.2 = (f32[2,4,136,64]{2,3,1,0:T(8,128)S(1)}, f32[2,4,136,64]{2,3,1,0:T(8,128)S(1)}, u32[]{:S(2)}, u32[]{:S(2)}) collective-permute-start(f32[2,4,136,64]{2,3,1,0:T(8,128)S(1)} %get-tuple-element.210), channel_id=1, source_target_pairs={{0,48},{16,0},{32,16},{48,32},{1,49},{17,1},{33,17},{49,33},{2,50}... | collective-permute-start | bytes 835592 | tf_op jit(solution)/shard_map/ppermute | solution.py:56
  20.5 9.9 %copy-start.11 = (pred[4]{0:T(512)(128)(4,1)}, pred[4]{0:T(512)(128)(4,1)S(1)}, u32[]{:S(2)}) copy-start(pred[4]{0:T(512)(128)(4,1)S(1)} %iota_compare_fusion.13) | copy-start | bytes 16
  20.5 9.9 %copy-start.13 = (pred[4]{0:T(512)(128)(4,1)}, pred[4]{0:T(512)(128)(4,1)S(1)}, u32[]{:S(2)}) copy-start(pred[4]{0:T(512)(128)(4,1)S(1)} %iota_compare_fusion.14) | copy-start | bytes 16
  20.5 9.9 %copy-start.15 = (pred[4]{0:T(512)(128)(4,1)}, pred[4]{0:T(512)(128)(4,1)S(1)}, u32[]{:S(2)}) copy-start(pred[4]{0:T(512)(128)(4,1)S(1)} %iota_compare_fusion.15) | copy-start | bytes 16
  20.5 9.8 %copy-start.17 = (pred[4]{0:T(512)(128)(4,1)}, pred[4]{0:T(512)(128)(4,1)S(1)}, u32[]{:S(2)}) copy-start(pred[4]{0:T(512)(128)(4,1)S(1)} %iota_compare_fusion.6) | copy-start | bytes 16
  20.5 9.8 %copy-start.19 = (pred[4]{0:T(512)(128)(4,1)}, pred[4]{0:T(512)(128)(4,1)S(1)}, u32[]{:S(2)}) copy-start(pred[4]{0:T(512)(128)(4,1)S(1)} %iota_compare_fusion.7) | copy-start | bytes 16
  20.6 9.8 %copy-start.21 = (pred[4]{0:T(512)(128)(4,1)}, pred[4]{0:T(512)(128)(4,1)S(1)}, u32[]{:S(2)}) copy-start(pred[4]{0:T(512)(128)(4,1)S(1)} %iota_compare_fusion.8) | copy-start | bytes 16
  20.6 9.8 %copy-start.23 = (pred[4]{0:T(512)(128)(4,1)}, pred[4]{0:T(512)(128)(4,1)S(1)}, u32[]{:S(2)}) copy-start(pred[4]{0:T(512)(128)(4,1)S(1)} %iota_compare_fusion.9) | copy-start | bytes 16
  20.6 9.8 %copy-start.27 = (pred[4]{0:T(512)(128)(4,1)}, pred[4]{0:T(512)(128)(4,1)S(1)}, u32[]{:S(2)}) copy-start(pred[4]{0:T(512)(128)(4,1)S(1)} %iota_compare_fusion.11) | copy-start | bytes 16
  20.6 9.8 %copy-start.29 = (pred[4]{0:T(512)(128)(4,1)}, pred[4]{0:T(512)(128)(4,1)S(1)}, u32[]{:S(2)}) copy-start(pred[4]{0:T(512)(128)(4,1)S(1)} %iota_compare_fusion.12) | copy-start | bytes 16
  39.2 1.3 copy-start.16
  39.3 1.3 copy-start.18
  39.3 1.3 copy-start.20
  39.3 1.3 copy-start.22
  39.3 1.3 copy-start.24
  39.3 2.0 %copy-start.31 = (pred[4,4]{1,0:T(4,128)(4,1)S(1)}, pred[4,4]{1,0:T(4,128)(4,1)}, u32[]{:S(2)}) copy-start(pred[4,4]{1,0:T(4,128)(4,1)} %fusion.83) | copy-start | bytes 52
  39.3 1.9 %copy-start.32 = (pred[4,4]{1,0:T(4,128)(4,1)S(1)}, pred[4,4]{1,0:T(4,128)(4,1)}, u32[]{:S(2)}) copy-start(pred[4,4]{1,0:T(4,128)(4,1)} %fusion.84) | copy-start | bytes 52
  39.3 1.9 %copy-start.33 = (pred[4,4]{1,0:T(4,128)(4,1)S(1)}, pred[4,4]{1,0:T(4,128)(4,1)}, u32[]{:S(2)}) copy-start(pred[4,4]{1,0:T(4,128)(4,1)} %fusion.85) | copy-start | bytes 52
  39.3 1.9 %copy-start.34 = (pred[4,4]{1,0:T(4,128)(4,1)S(1)}, pred[4,4]{1,0:T(4,128)(4,1)}, u32[]{:S(2)}) copy-start(pred[4,4]{1,0:T(4,128)(4,1)} %fusion.86) | copy-start | bytes 52
  39.3 1.9 %copy-start.35 = (pred[4,4]{1,0:T(4,128)(4,1)S(1)}, pred[4,4]{1,0:T(4,128)(4,1)}, u32[]{:S(2)}) copy-start(pred[4,4]{1,0:T(4,128)(4,1)} %fusion.94) | copy-start | bytes 52
  39.3 1.9 %copy-start.36 = (pred[4,4]{1,0:T(4,128)(4,1)S(1)}, pred[4,4]{1,0:T(4,128)(4,1)}, u32[]{:S(2)}) copy-start(pred[4,4]{1,0:T(4,128)(4,1)} %fusion.95) | copy-start | bytes 52
  39.4 1.9 %copy-start.37 = (pred[4,4]{1,0:T(4,128)(4,1)S(1)}, pred[4,4]{1,0:T(4,128)(4,1)}, u32[]{:S(2)}) copy-start(pred[4,4]{1,0:T(4,128)(4,1)} %fusion.96) | copy-start | bytes 52
  39.4 1.9 %copy-start.38 = (pred[4,4]{1,0:T(4,128)(4,1)S(1)}, pred[4,4]{1,0:T(4,128)(4,1)}, u32[]{:S(2)}) copy-start(pred[4,4]{1,0:T(4,128)(4,1)} %fusion.87) | copy-start | bytes 52
  39.4 1.9 %copy-start.39 = (pred[4,4]{1,0:T(4,128)(4,1)S(1)}, pred[4,4]{1,0:T(4,128)(4,1)}, u32[]{:S(2)}) copy-start(pred[4,4]{1,0:T(4,128)(4,1)} %fusion.93) | copy-start | bytes 52
  39.4 3.9 %copy-start.30 = (pred[4]{0:T(512)(128)(4,1)S(1)}, pred[4]{0:T(512)(128)(4,1)}, u32[]{:S(2)}) copy-start(pred[4]{0:T(512)(128)(4,1)} %copy-done.29) | copy-start | bytes 16
  39.4 4.5 %copy-start.28 = (pred[4]{0:T(512)(128)(4,1)S(1)}, pred[4]{0:T(512)(128)(4,1)}, u32[]{:S(2)}) copy-start(pred[4]{0:T(512)(128)(4,1)} %copy-done.27) | copy-start | bytes 16
  44.8 13.3 %copy-start.40 = (f32[4]{0:T(128)S(1)}, f32[4]{0:T(128)}, u32[]{:S(2)}) copy-start(f32[4]{0:T(128)} %pad.62.clone) | copy-start | bytes 52
  45.0 18.7 %copy-start.7 = (s32[1024]{0:T(1024)S(1)}, s32[1024]{0:T(1024)}, u32[]{:S(2)}) copy-start(s32[1024]{0:T(1024)} %pad_clamp_fusion.3) | copy-start | bytes 12292
  45.0 14.0 %collective-permute-start.3 = (f32[2,1,136,64]{2,3,0,1:T(8,128)S(1)}, f32[2,1,136,64]{2,3,0,1:T(8,128)S(1)}, u32[]{:S(2)}, u32[]{:S(2)}) collective-permute-start(f32[2,1,136,64]{2,3,0,1:T(8,128)S(1)} %get-tuple-element.224), channel_id=1, source_target_pairs={{0,64},{64,128},{128,192},{192,0},{1,65},{65,129},{129,193},{193,1... | collective-permute-start | bytes 208904 | tf_op jit(solution)/shard_map/ppermute | solution.py:56
  49.3 12.3 %collective-permute-start.4 = (f32[2,1,136,64]{2,3,0,1:T(8,128)S(1)}, f32[2,1,136,64]{2,3,0,1:T(8,128)S(1)}, u32[]{:S(2)}, u32[]{:S(2)}) collective-permute-start(f32[2,1,136,64]{2,3,0,1:T(8,128)S(1)} %get-tuple-element.223), channel_id=1, source_target_pairs={{0,128},{64,192},{128,0},{192,64},{1,129},{65,193},{129,1},{193,65... | collective-permute-start | bytes 208904 | tf_op jit(solution)/shard_map/ppermute | solution.py:56
  55.4 8.1 %collective-permute-start.5 = (f32[2,1,136,64]{2,3,1,0:T(8,128)S(1)}, f32[2,1,136,64]{2,3,1,0:T(8,128)S(1)}, u32[]{:S(2)}, u32[]{:S(2)}) collective-permute-start(f32[2,1,136,64]{2,3,1,0:T(8,128)S(1)} %get-tuple-element.222), channel_id=1, source_target_pairs={{0,192},{64,0},{128,64},{192,128},{1,193},{65,1},{129,65},{193,129... | collective-permute-start | bytes 208904 | tf_op jit(solution)/shard_map/ppermute | solution.py:56
  59.0 36.9 %copy-start.25 = (pred[4]{0:T(512)(128)(4,1)S(1)}, pred[4]{0:T(512)(128)(4,1)}, u32[]{:S(2)}) copy-start(pred[4]{0:T(512)(128)(4,1)} %compare_and_fusion.1) | copy-start | bytes 16
  68.0 33.2 %collective-permute-start.6 = (f32[2,1,136,64]{2,3,0,1:T(8,128)S(1)}, f32[2,1,136,64]{2,3,0,1:T(8,128)S(1)}, u32[]{:S(2)}, u32[]{:S(2)}) collective-permute-start(f32[2,1,136,64]{2,3,0,1:T(8,128)S(1)} %get-tuple-element.234), channel_id=1, source_target_pairs={{0,256},{256,512},{512,768},{768,0},{1,257},{257,513},{513,769},{7... | collective-permute-start | bytes 208904 | tf_op jit(solution)/shard_map/ppermute | solution.py:104
  78.9 31.6 %collective-permute-start.7 = (f32[2,1,136,64]{2,3,0,1:T(8,128)S(1)}, f32[2,1,136,64]{2,3,0,1:T(8,128)S(1)}, u32[]{:S(2)}, u32[]{:S(2)}) collective-permute-start(f32[2,1,136,64]{2,3,0,1:T(8,128)S(1)} %get-tuple-element.234), channel_id=1, source_target_pairs={{0,512},{256,768},{512,0},{768,256},{1,513},{257,769},{513,1},{769... | collective-permute-start | bytes 208904 | tf_op jit(solution)/shard_map/ppermute | solution.py:104
  90.6 22.5 %collective-permute-start.8 = (f32[2,1,136,64]{2,3,0,1:T(8,128)S(1)}, f32[2,1,136,64]{2,3,0,1:T(8,128)S(1)}, u32[]{:S(2)}, u32[]{:S(2)}) collective-permute-start(f32[2,1,136,64]{2,3,0,1:T(8,128)S(1)} %get-tuple-element.234), channel_id=1, source_target_pairs={{0,768},{256,0},{512,256},{768,512},{1,769},{257,1},{513,257},{769... | collective-permute-start | bytes 208904 | tf_op jit(solution)/shard_map/ppermute | solution.py:104
  113.9 15.8 %copy-start.26 = (pred[4]{0:T(512)(128)(4,1)S(1)}, pred[4]{0:T(512)(128)(4,1)}, u32[]{:S(2)}) copy-start(pred[4]{0:T(512)(128)(4,1)} %compare_and_fusion.1) | copy-start | bytes 16
  116.5 13.4 %copy-start.10 = (f32[4,4]{1,0:T(4,128)S(1)}, f32[4,4]{1,0:T(4,128)}, u32[]{:S(2)}) copy-start(f32[4,4]{1,0:T(4,128)} %pad_maximum_fusion.17) | copy-start | bytes 196
  116.6 10.4 %collective-permute-start.9 = (f32[2,1,128,64]{2,3,0,1:T(8,128)S(1)}, f32[2,1,128,64]{2,3,0,1:T(8,128)S(1)}, u32[]{:S(2)}, u32[]{:S(2)}) collective-permute-start(f32[2,1,128,64]{2,3,0,1:T(8,128)S(1)} %get-tuple-element.230), channel_id=1, source_target_pairs={{0,64},{64,128},{128,192},{192,0},{1,65},{65,129},{129,193},{193,1... | collective-permute-start | bytes 196616 | tf_op jit(solution)/shard_map/ppermute | solution.py:47
  120.1 7.8 %collective-permute-start.10 = (f32[2,1,128,64]{2,3,0,1:T(8,128)S(1)}, f32[2,1,128,64]{2,3,0,1:T(8,128)S(1)}, u32[]{:S(2)}, u32[]{:S(2)}) collective-permute-start(f32[2,1,128,64]{2,3,0,1:T(8,128)S(1)} %get-tuple-element.231), channel_id=1, source_target_pairs={{0,128},{64,192},{128,0},{192,64},{1,129},{65,193},{129,1},{193,65... | collective-permute-start | bytes 196616 | tf_op jit(solution)/shard_map/ppermute | solution.py:47
  122.0 6.9 %collective-permute-start.11 = (f32[2,1,128,64]{2,3,0,1:T(8,128)S(1)}, f32[2,1,128,64]{2,3,0,1:T(8,128)S(1)}, u32[]{:S(2)}, u32[]{:S(2)}) collective-permute-start(f32[2,1,128,64]{2,3,0,1:T(8,128)S(1)} %get-tuple-element.232), channel_id=1, source_target_pairs={{0,192},{64,0},{128,64},{192,128},{1,193},{65,1},{129,65},{193,129... | collective-permute-start | bytes 196616 | tf_op jit(solution)/shard_map/ppermute | solution.py:47
  130.2 17.0 %collective-permute-start.12 = (f32[2,4,128,64]{2,3,1,0:T(8,128)S(1)}, f32[2,4,128,64]{2,3,1,0:T(8,128)S(1)}, u32[]{:S(2)}, u32[]{:S(2)}) collective-permute-start(f32[2,4,128,64]{2,3,1,0:T(8,128)S(1)} %get-tuple-element.216), channel_id=1, source_target_pairs={{0,16},{16,32},{32,48},{48,0},{1,17},{17,33},{33,49},{49,1},{2,18}... | collective-permute-start | bytes 786440 | tf_op jit(solution)/shard_map/ppermute | solution.py:47
  136.7 12.4 %collective-permute-start.13 = (f32[2,4,128,64]{2,3,1,0:T(8,128)S(1)}, f32[2,4,128,64]{2,3,1,0:T(8,128)S(1)}, u32[]{:S(2)}, u32[]{:S(2)}) collective-permute-start(f32[2,4,128,64]{2,3,1,0:T(8,128)S(1)} %get-tuple-element.217), channel_id=1, source_target_pairs={{0,32},{16,48},{32,0},{48,16},{1,33},{17,49},{33,1},{49,17},{2,34}... | collective-permute-start | bytes 786440 | tf_op jit(solution)/shard_map/ppermute | solution.py:47
  140.4 10.1 %collective-permute-start.14 = (f32[2,4,128,64]{2,3,1,0:T(8,128)S(1)}, f32[2,4,128,64]{2,3,1,0:T(8,128)S(1)}, u32[]{:S(2)}, u32[]{:S(2)}) collective-permute-start(f32[2,4,128,64]{2,3,1,0:T(8,128)S(1)} %get-tuple-element.218), channel_id=1, source_target_pairs={{0,48},{16,0},{32,16},{48,32},{1,49},{17,1},{33,17},{49,33},{2,50}... | collective-permute-start | bytes 786440 | tf_op jit(solution)/shard_map/ppermute | solution.py:47
  (8 other events, 7.9 us)

commit v8 on v7

--- a/solution.py
+++ b/solution.py
@@ -99,10 +99,7 @@
     count, index = lax.axis_size(axis), lax.axis_index(axis)
     n = own_f.shape[1] - 8
     mine = jnp.stack([own_f, own_b])
-    got = [mine]
-    for shift in range(1, count):
-        got.append(lax.ppermute(mine, axis, [(i, (i + shift) % count) for i in range(count)]))
-    members = jnp.take(jnp.stack(got), (index - jnp.arange(count)) % count, axis=0)
+    members = lax.all_gather(mine, axis)
     group = members[:, 0, :, n, 0]
     entry_f = weighted(lower_weights(group, index), members[:, 0, :, :n])
     entry_b = weighted(upper_weights(group, index), members[:, 1, :, :n])

time: 161 us -> 151 us (0.938)
  blocking collectives: 0 us -> 33.8 us
  starting transfers between devices: 73.2 us -> 47.4 us
  waiting for transfers between devices: 29.8 us -> 19.4 us
  other arithmetic: 29.4 us -> 23.7 us
    all_gather x0 -> x1, blocking collectives: none -> 33.8 us  [gathered_scan(): members = lax.all_gather(mine, axis)]
    ppermute x3 -> x0, starting transfers between devices: 26.3 us -> none  [gathered_scan(): lax.ppermute(mine, axis, [(i, (i + shift) % count) for i in range(count)])]
    ppermute x3 -> x0, waiting for transfers between devices: 11.9 us -> none  [gathered_scan(): lax.ppermute(mine, axis, [(i, (i + shift) % count) for i in range(count)])]
    ppermute x6, waiting for transfers between devices: 12.7 us -> 14.4 us  [exchange_received(): lax.ppermute(send, axis, [(i, (i + shift) % count) for i in range(count)])]
  transfers between devices with their start and end apart: 15 -> 12, of which waited for: 10 -> 8; matrix products, arithmetic and copies ran while one was open for 15% -> 9% of each run, Pallas kernels for 0% -> 0%
where the time goes in v8:
time: 151 us; the launch traced here: 150 us
  starting transfers between devices  47.4 us (31%)
  blocking collectives  33.8 us (22%)
  other arithmetic  23.7 us (16%)
  waiting for transfers between devices  19.4 us (13%)
  local copies, waits for them, and re-layouts  16.5 us (11%)
  matrix products  6.99 us (5%)
  between operations  1.84 us (1%)
    all_gather x1, blocking collectives, gathered_scan(): members = lax.all_gather(mine, axis)  33.8 us
    ppermute x6, starting transfers between devices, exchange_received(): lax.ppermute(send, axis, [(i, (i + shift) % count) for i in range(count)])  24.2 us
    ppermute x6, starting transfers between devices, exchange(): lax.ppermute(send, axis, [(i, (i + shift) % count) for i in range(count)])  23.2 us
    ppermute x6, waiting for transfers between devices, exchange_received(): lax.ppermute(send, axis, [(i, (i + shift) % count) for i in range(count)])  14.4 us
    unnamed x87, local copies, waits for them, and re-layouts  6.41 us
    ppermute x6, waiting for transfers between devices, exchange(): lax.ppermute(send, axis, [(i, (i + shift) % count) for i in range(count)])  4.97 us
  transfers between devices with their start and end apart: 12, of which 8 were waited for; matrix products, arithmetic and copies ran while one was open for 9% of the time, Pallas kernels for 0%

profile of v8, /device:TPU:56, one launch (start us, length us, event | category | flops | bytes accessed | tf_op | source)
XLA Modules:
  0.0 149.8 jit_solution(11446435181659538244)
XLA Ops:
  0.7 1.0 reduce_window_sum.11
  2.0 1.1 copy.302
  3.1 0.8 bitcast_convert_fusion
  3.9 1.1 copy.301
  5.0 0.8 bitcast_convert_fusion.1
  7.3 1.2 dynamic-slice_select_fusion
  8.5 3.4 %collective-permute-start = (f32[2,4,136,64]{2,3,1,0:T(8,128)}, f32[2,4,136,64]{2,3,1,0:T(8,128)S(1)}, u32[]{:S(2)}, u32[]{:S(2)}) collective-permute-start(f32[2,4,136,64]{2,3,1,0:T(8,128)} %get-tuple-element.212), channel_id=1, source_target_pairs={{0,16},{16,32},{32,48},{48,0},{1,17},{17,33},{33,49},{49,1},{2,18}... | collective-permute-start | bytes 835592 | tf_op jit(solution)/shard_map/ppermute | solution.py:56
  11.9 4.6 %collective-permute-start.1 = (f32[2,4,136,64]{2,3,1,0:T(8,128)}, f32[2,4,136,64]{2,3,1,0:T(8,128)S(1)}, u32[]{:S(2)}, u32[]{:S(2)}) collective-permute-start(f32[2,4,136,64]{2,3,1,0:T(8,128)} %get-tuple-element.211), channel_id=1, source_target_pairs={{0,32},{16,48},{32,0},{48,16},{1,33},{17,49},{33,1},{49,17},{2,34}... | collective-permute-start | bytes 835592 | tf_op jit(solution)/shard_map/ppermute | solution.py:56
  16.5 3.3 %collective-permute-start.2 = (f32[2,4,136,64]{2,3,1,0:T(8,128)S(1)}, f32[2,4,136,64]{2,3,1,0:T(8,128)S(1)}, u32[]{:S(2)}, u32[]{:S(2)}) collective-permute-start(f32[2,4,136,64]{2,3,1,0:T(8,128)S(1)} %get-tuple-element.210), channel_id=1, source_target_pairs={{0,48},{16,0},{32,16},{48,32},{1,49},{17,1},{33,17},{49,33},{2,50}... | collective-permute-start | bytes 835592 | tf_op jit(solution)/shard_map/ppermute | solution.py:56
  21.3 0.6 pad_clamp_fusion.3
  26.9 0.6 pad_clamp_fusion.2
  29.9 7.7 %collective-permute-done.1 = f32[2,4,136,64]{2,3,1,0:T(8,128)S(1)} collective-permute-done((f32[2,4,136,64]{2,3,1,0:T(8,128)}, f32[2,4,136,64]{2,3,1,0:T(8,128)S(1)}, u32[]{:S(2)}, u32[]{:S(2)}) %collective-permute-start.1) | collective-permute-done | bytes 278560 | tf_op jit(solution)/shard_map/ppermute | solution.py:56
  37.7 1.6 %collective-permute-done.2 = f32[2,4,136,64]{2,3,1,0:T(8,128)S(1)} collective-permute-done((f32[2,4,136,64]{2,3,1,0:T(8,128)S(1)}, f32[2,4,136,64]{2,3,1,0:T(8,128)S(1)}, u32[]{:S(2)}, u32[]{:S(2)}) %collective-permute-start.2) | collective-permute-done | bytes 278560 | tf_op jit(solution)/shard_map/ppermute | solution.py:56
  44.5 4.3 %collective-permute-start.3 = (f32[2,1,136,64]{2,3,0,1:T(8,128)S(1)}, f32[2,1,136,64]{2,3,0,1:T(8,128)S(1)}, u32[]{:S(2)}, u32[]{:S(2)}) collective-permute-start(f32[2,1,136,64]{2,3,0,1:T(8,128)S(1)} %get-tuple-element.224), channel_id=1, source_target_pairs={{0,64},{64,128},{128,192},{192,0},{1,65},{65,129},{129,193},{193,1... | collective-permute-start | bytes 208904 | tf_op jit(solution)/shard_map/ppermute | solution.py:56
  48.8 6.1 %collective-permute-start.4 = (f32[2,1,136,64]{2,3,0,1:T(8,128)S(1)}, f32[2,1,136,64]{2,3,0,1:T(8,128)S(1)}, u32[]{:S(2)}, u32[]{:S(2)}) collective-permute-start(f32[2,1,136,64]{2,3,0,1:T(8,128)S(1)} %get-tuple-element.223), channel_id=1, source_target_pairs={{0,128},{64,192},{128,0},{192,64},{1,129},{65,193},{129,1},{193,65... | collective-permute-start | bytes 208904 | tf_op jit(solution)/shard_map/ppermute | solution.py:56
  54.8 2.5 %collective-permute-start.5 = (f32[2,1,136,64]{2,3,1,0:T(8,128)S(1)}, f32[2,1,136,64]{2,3,1,0:T(8,128)S(1)}, u32[]{:S(2)}, u32[]{:S(2)}) collective-permute-start(f32[2,1,136,64]{2,3,1,0:T(8,128)S(1)} %get-tuple-element.222), channel_id=1, source_target_pairs={{0,192},{64,0},{128,64},{192,128},{1,193},{65,1},{129,65},{193,129... | collective-permute-start | bytes 208904 | tf_op jit(solution)/shard_map/ppermute | solution.py:56
  57.9 3.2 %collective-permute-done.4 = f32[2,1,136,64]{2,3,0,1:T(8,128)S(1)} collective-permute-done((f32[2,1,136,64]{2,3,0,1:T(8,128)S(1)}, f32[2,1,136,64]{2,3,0,1:T(8,128)S(1)}, u32[]{:S(2)}, u32[]{:S(2)}) %collective-permute-start.4) | collective-permute-done | bytes 69664 | tf_op jit(solution)/shard_map/ppermute | solution.py:56
  61.1 1.9 %collective-permute-done.5 = f32[2,1,136,64]{2,3,1,0:T(8,128)S(1)} collective-permute-done((f32[2,1,136,64]{2,3,1,0:T(8,128)S(1)}, f32[2,1,136,64]{2,3,1,0:T(8,128)S(1)}, u32[]{:S(2)}, u32[]{:S(2)}) %collective-permute-start.5) | collective-permute-done | bytes 69664 | tf_op jit(solution)/shard_map/ppermute | solution.py:56
  63.1 0.6 gather_fusion.6
  63.7 0.8 fusion.102
  66.4 0.6 gather_fusion.8
  67.1 0.6 gather_fusion.9
  67.8 0.6 pad_bitcast_fusion.1
  68.5 0.6 pad_bitcast_fusion
  69.1 33.8 %all-gather = f32[8,1,136,64]{2,3,1,0:T(8,128)S(1)} all-gather(f32[2,1,136,64]{2,3,1,0:T(8,128)S(1)} %pad_maximum_fusion.14), channel_id=2, replica_groups=mesh['czh'=4,'czl'=4,'cx'=4,'head'=8,'dp'=2] {'czh'}, dimensions={0}, use_global_device_ids=true | all-gather | bytes 348160 | tf_op jit(solution)/shard_map/all_gather | solution.py:102
  103.6 2.6 %maximum_bitcast_fusion.3 = f32[4]{0:T(128)S(1)} fusion(f32[1,1]{0,1:T(1,128)} %bitcast.104, f32[1,1]{0,1:T(1,128)} %bitcast.103, f32[1,1]{0,1:T(1,128)} %bitcast.102, f32[1,1]{0,1:T(1,128)} %bitcast.101), kind=kLoop, calls=%fused_computation.302 | loop fusion | flops 12 | bytes 32 | tf_op jit(solution)/shard_map/mul | solution.py:136
  106.3 2.0 %maximum_bitcast_fusion.2 = f32[4]{0:T(128)S(1)} fusion(f32[1,1]{0,1:T(1,128)} %bitcast.75, f32[1,1]{0,1:T(1,128)} %bitcast.74, f32[1,1]{0,1:T(1,128)} %bitcast.73, f32[1,1]{0,1:T(1,128)} %constant.246.clone.1), kind=kLoop, calls=%fused_computation.301 | loop fusion | flops 12 | bytes 32 | tf_op jit(solution)/shard_map/mul | solution.py:135
  108.3 4.9 %collective-permute-start.6 = (f32[2,1,128,64]{2,3,0,1:T(8,128)S(1)}, f32[2,1,128,64]{2,3,0,1:T(8,128)S(1)}, u32[]{:S(2)}, u32[]{:S(2)}) collective-permute-start(f32[2,1,128,64]{2,3,0,1:T(8,128)S(1)} %get-tuple-element.230), channel_id=1, source_target_pairs={{0,64},{64,128},{128,192},{192,0},{1,65},{65,129},{129,193},{193,1... | collective-permute-start | bytes 196616 | tf_op jit(solution)/shard_map/ppermute | solution.py:47
  113.3 4.2 %collective-permute-start.7 = (f32[2,1,128,64]{2,3,0,1:T(8,128)S(1)}, f32[2,1,128,64]{2,3,0,1:T(8,128)S(1)}, u32[]{:S(2)}, u32[]{:S(2)}) collective-permute-start(f32[2,1,128,64]{2,3,0,1:T(8,128)S(1)} %get-tuple-element.231), channel_id=1, source_target_pairs={{0,128},{64,192},{128,0},{192,64},{1,129},{65,193},{129,1},{193,65... | collective-permute-start | bytes 196616 | tf_op jit(solution)/shard_map/ppermute | solution.py:47
  117.5 2.7 %collective-permute-start.8 = (f32[2,1,128,64]{2,3,0,1:T(8,128)S(1)}, f32[2,1,128,64]{2,3,0,1:T(8,128)S(1)}, u32[]{:S(2)}, u32[]{:S(2)}) collective-permute-start(f32[2,1,128,64]{2,3,0,1:T(8,128)S(1)} %get-tuple-element.232), channel_id=1, source_target_pairs={{0,192},{64,0},{128,64},{192,128},{1,193},{65,1},{129,65},{193,129... | collective-permute-start | bytes 196616 | tf_op jit(solution)/shard_map/ppermute | solution.py:47
  120.2 1.6 %collective-permute-done.7 = f32[2,1,128,64]{2,3,0,1:T(8,128)S(1)} collective-permute-done((f32[2,1,128,64]{2,3,0,1:T(8,128)S(1)}, f32[2,1,128,64]{2,3,0,1:T(8,128)S(1)}, u32[]{:S(2)}, u32[]{:S(2)}) %collective-permute-start.7) | collective-permute-done | bytes 65568 | tf_op jit(solution)/shard_map/ppermute | solution.py:47
  121.8 1.9 %collective-permute-done.8 = f32[2,1,128,64]{2,3,0,1:T(8,128)S(1)} collective-permute-done((f32[2,1,128,64]{2,3,0,1:T(8,128)S(1)}, f32[2,1,128,64]{2,3,0,1:T(8,128)S(1)}, u32[]{:S(2)}, u32[]{:S(2)}) %collective-permute-start.8) | collective-permute-done | bytes 65568 | tf_op jit(solution)/shard_map/ppermute | solution.py:47
  123.7 0.7 gather_fusion
  124.8 4.1 %collective-permute-start.9 = (f32[2,4,128,64]{2,3,1,0:T(8,128)S(1)}, f32[2,4,128,64]{2,3,1,0:T(8,128)S(1)}, u32[]{:S(2)}, u32[]{:S(2)}) collective-permute-start(f32[2,4,128,64]{2,3,1,0:T(8,128)S(1)} %get-tuple-element.216), channel_id=1, source_target_pairs={{0,16},{16,32},{32,48},{48,0},{1,17},{17,33},{33,49},{49,1},{2,18}... | collective-permute-start | bytes 786440 | tf_op jit(solution)/shard_map/ppermute | solution.py:47
  128.9 3.3 %collective-permute-start.10 = (f32[2,4,128,64]{2,3,1,0:T(8,128)S(1)}, f32[2,4,128,64]{2,3,1,0:T(8,128)S(1)}, u32[]{:S(2)}, u32[]{:S(2)}) collective-permute-start(f32[2,4,128,64]{2,3,1,0:T(8,128)S(1)} %get-tuple-element.217), channel_id=1, source_target_pairs={{0,32},{16,48},{32,0},{48,16},{1,33},{17,49},{33,1},{49,17},{2,34}... | collective-permute-start | bytes 786440 | tf_op jit(solution)/shard_map/ppermute | solution.py:47
  132.2 4.0 %collective-permute-start.11 = (f32[2,4,128,64]{2,3,1,0:T(8,128)S(1)}, f32[2,4,128,64]{2,3,1,0:T(8,128)S(1)}, u32[]{:S(2)}, u32[]{:S(2)}) collective-permute-start(f32[2,4,128,64]{2,3,1,0:T(8,128)S(1)} %get-tuple-element.218), channel_id=1, source_target_pairs={{0,48},{16,0},{32,16},{48,32},{1,49},{17,1},{33,17},{49,33},{2,50}... | collective-permute-start | bytes 786440 | tf_op jit(solution)/shard_map/ppermute | solution.py:47
  136.3 3.6 %while.18 = (s32[]{:T(128)}, f32[2,128,8,64]{1,3,2,0:T(8,128)}, f32[2,128,128]{2,1,0:T(8,128)S(1)}, f32[2,128,128]{2,1,0:T(8,128)S(1)}, bf16[2,128,8,64]{1,3,2,0...) while((s32[]{:T(128)}, f32[2,128,8,64]{1,3,2,0:T(8,128)}, ...), condition=%wide.region_3.4_spmd, body=%wide.region_1.3_spmd.sunk | while | flops 43515904 | bytes 1224821 | solution.py:200
  136.4 1.1 fusion.144
  138.2 1.1 fusion.144
  140.3 1.4 collective-permute-done.11
  141.7 0.7 copy-done.3
  142.4 1.0 pad_maximum_fusion.3
  143.4 0.6 gather_fusion.1
  145.5 1.0 fusion.30
  146.5 0.7 copy.336
  147.2 1.0 fusion.31
  148.2 0.7 copy.335
  148.9 0.8 copy.334
  (224 shorter events, 22.3 us)
Async XLA Ops:
  1.9 5.1 %copy-start.4 = (f32[128,16]{0,1:T(8,128)}, f32[128,16]{0,1:T(8,128)S(1)}, u32[]{:S(2)}) copy-start(f32[128,16]{0,1:T(8,128)S(1)} %get-tuple-element.238) | copy-start | bytes 24580
  7.3 22.5 %copy-start = (bf16[1,128,128]{2,1,0:T(8,128)(2,1)S(1)}, bf16[1,128,128]{2,1,0:T(8,128)(2,1)}, u32[]{:S(2)}) copy-start(bf16[1,128,128]{2,1,0:T(8,128)(2,1)} %param.25) | copy-start | bytes 98308
  7.3 22.5 %copy-start.2 = (bf16[1,128,128]{2,1,0:T(8,128)(2,1)S(1)}, bf16[1,128,128]{2,1,0:T(8,128)(2,1)}, u32[]{:S(2)}) copy-start(bf16[1,128,128]{2,1,0:T(8,128)(2,1)} %param.26) | copy-start | bytes 98308
  8.5 21.4 %collective-permute-start = (f32[2,4,136,64]{2,3,1,0:T(8,128)}, f32[2,4,136,64]{2,3,1,0:T(8,128)S(1)}, u32[]{:S(2)}, u32[]{:S(2)}) collective-permute-start(f32[2,4,136,64]{2,3,1,0:T(8,128)} %get-tuple-element.212), channel_id=1, source_target_pairs={{0,16},{16,32},{32,48},{48,0},{1,17},{17,33},{33,49},{49,1},{2,18}... | collective-permute-start | bytes 835592 | tf_op jit(solution)/shard_map/ppermute | solution.py:56
  11.9 25.8 %collective-permute-start.1 = (f32[2,4,136,64]{2,3,1,0:T(8,128)}, f32[2,4,136,64]{2,3,1,0:T(8,128)S(1)}, u32[]{:S(2)}, u32[]{:S(2)}) collective-permute-start(f32[2,4,136,64]{2,3,1,0:T(8,128)} %get-tuple-element.211), channel_id=1, source_target_pairs={{0,32},{16,48},{32,0},{48,16},{1,33},{17,49},{33,1},{49,17},{2,34}... | collective-permute-start | bytes 835592 | tf_op jit(solution)/shard_map/ppermute | solution.py:56
  16.5 22.7 %collective-permute-start.2 = (f32[2,4,136,64]{2,3,1,0:T(8,128)S(1)}, f32[2,4,136,64]{2,3,1,0:T(8,128)S(1)}, u32[]{:S(2)}, u32[]{:S(2)}) collective-permute-start(f32[2,4,136,64]{2,3,1,0:T(8,128)S(1)} %get-tuple-element.210), channel_id=1, source_target_pairs={{0,48},{16,0},{32,16},{48,32},{1,49},{17,1},{33,17},{49,33},{2,50}... | collective-permute-start | bytes 835592 | tf_op jit(solution)/shard_map/ppermute | solution.py:56
  20.5 8.7 %copy-start.10 = (pred[4]{0:T(512)(128)(4,1)}, pred[4]{0:T(512)(128)(4,1)S(1)}, u32[]{:S(2)}) copy-start(pred[4]{0:T(512)(128)(4,1)S(1)} %iota_compare_fusion.13) | copy-start | bytes 16
  20.5 8.7 %copy-start.12 = (pred[4]{0:T(512)(128)(4,1)}, pred[4]{0:T(512)(128)(4,1)S(1)}, u32[]{:S(2)}) copy-start(pred[4]{0:T(512)(128)(4,1)S(1)} %iota_compare_fusion.14) | copy-start | bytes 16
  20.5 8.7 %copy-start.14 = (pred[4]{0:T(512)(128)(4,1)}, pred[4]{0:T(512)(128)(4,1)S(1)}, u32[]{:S(2)}) copy-start(pred[4]{0:T(512)(128)(4,1)S(1)} %iota_compare_fusion.15) | copy-start | bytes 16
  20.6 8.6 %copy-start.16 = (pred[4]{0:T(512)(128)(4,1)}, pred[4]{0:T(512)(128)(4,1)S(1)}, u32[]{:S(2)}) copy-start(pred[4]{0:T(512)(128)(4,1)S(1)} %iota_compare_fusion.6) | copy-start | bytes 16
  20.6 8.6 %copy-start.18 = (pred[4]{0:T(512)(128)(4,1)}, pred[4]{0:T(512)(128)(4,1)S(1)}, u32[]{:S(2)}) copy-start(pred[4]{0:T(512)(128)(4,1)S(1)} %iota_compare_fusion.7) | copy-start | bytes 16
  20.6 8.6 %copy-start.20 = (pred[4]{0:T(512)(128)(4,1)}, pred[4]{0:T(512)(128)(4,1)S(1)}, u32[]{:S(2)}) copy-start(pred[4]{0:T(512)(128)(4,1)S(1)} %iota_compare_fusion.8) | copy-start | bytes 16
  20.6 8.6 %copy-start.22 = (pred[4]{0:T(512)(128)(4,1)}, pred[4]{0:T(512)(128)(4,1)S(1)}, u32[]{:S(2)}) copy-start(pred[4]{0:T(512)(128)(4,1)S(1)} %iota_compare_fusion.9) | copy-start | bytes 16
  20.6 8.6 %copy-start.25 = (pred[4]{0:T(512)(128)(4,1)}, pred[4]{0:T(512)(128)(4,1)S(1)}, u32[]{:S(2)}) copy-start(pred[4]{0:T(512)(128)(4,1)S(1)} %iota_compare_fusion.11) | copy-start | bytes 16
  20.7 8.6 %copy-start.27 = (pred[4]{0:T(512)(128)(4,1)}, pred[4]{0:T(512)(128)(4,1)S(1)}, u32[]{:S(2)}) copy-start(pred[4]{0:T(512)(128)(4,1)S(1)} %iota_compare_fusion.12) | copy-start | bytes 16
  39.2 1.2 copy-start.8
  39.2 1.3 copy-start.11
  39.2 1.3 copy-start.13
  39.2 1.3 copy-start.15
  39.3 1.3 copy-start.17
  39.3 1.3 copy-start.19
  39.3 1.3 copy-start.21
  39.3 1.3 copy-start.23
  39.3 1.4 copy-start.31
  39.3 1.4 copy-start.32
  39.3 1.4 copy-start.33
  39.3 1.4 copy-start.34
  39.3 1.4 copy-start.35
  39.3 1.4 copy-start.36
  39.4 1.4 copy-start.37
  39.4 1.4 copy-start.38
  39.4 1.4 copy-start.39
  39.4 3.3 %copy-start.28 = (pred[4]{0:T(512)(128)(4,1)S(1)}, pred[4]{0:T(512)(128)(4,1)}, u32[]{:S(2)}) copy-start(pred[4]{0:T(512)(128)(4,1)} %copy-done.27) | copy-start | bytes 16
  39.4 3.9 %copy-start.26 = (pred[4]{0:T(512)(128)(4,1)S(1)}, pred[4]{0:T(512)(128)(4,1)}, u32[]{:S(2)}) copy-start(pred[4]{0:T(512)(128)(4,1)} %copy-done.25) | copy-start | bytes 16
  44.2 13.3 %copy-start.40 = (f32[4]{0:T(128)S(1)}, f32[4]{0:T(128)}, u32[]{:S(2)}) copy-start(f32[4]{0:T(128)} %pad.58.clone) | copy-start | bytes 52
  44.4 18.7 %copy-start.7 = (s32[1024]{0:T(1024)S(1)}, s32[1024]{0:T(1024)}, u32[]{:S(2)}) copy-start(s32[1024]{0:T(1024)} %pad_clamp_fusion.2) | copy-start | bytes 12292
  44.5 13.4 %collective-permute-start.3 = (f32[2,1,136,64]{2,3,0,1:T(8,128)S(1)}, f32[2,1,136,64]{2,3,0,1:T(8,128)S(1)}, u32[]{:S(2)}, u32[]{:S(2)}) collective-permute-start(f32[2,1,136,64]{2,3,0,1:T(8,128)S(1)} %get-tuple-element.224), channel_id=1, source_target_pairs={{0,64},{64,128},{128,192},{192,0},{1,65},{65,129},{129,193},{193,1... | collective-permute-start | bytes 208904 | tf_op jit(solution)/shard_map/ppermute | solution.py:56
  48.8 12.3 %collective-permute-start.4 = (f32[2,1,136,64]{2,3,0,1:T(8,128)S(1)}, f32[2,1,136,64]{2,3,0,1:T(8,128)S(1)}, u32[]{:S(2)}, u32[]{:S(2)}) collective-permute-start(f32[2,1,136,64]{2,3,0,1:T(8,128)S(1)} %get-tuple-element.223), channel_id=1, source_target_pairs={{0,128},{64,192},{128,0},{192,64},{1,129},{65,193},{129,1},{193,65... | collective-permute-start | bytes 208904 | tf_op jit(solution)/shard_map/ppermute | solution.py:56
  54.8 8.1 %collective-permute-start.5 = (f32[2,1,136,64]{2,3,1,0:T(8,128)S(1)}, f32[2,1,136,64]{2,3,1,0:T(8,128)S(1)}, u32[]{:S(2)}, u32[]{:S(2)}) collective-permute-start(f32[2,1,136,64]{2,3,1,0:T(8,128)S(1)} %get-tuple-element.222), channel_id=1, source_target_pairs={{0,192},{64,0},{128,64},{192,128},{1,193},{65,1},{129,65},{193,129... | collective-permute-start | bytes 208904 | tf_op jit(solution)/shard_map/ppermute | solution.py:56
  63.0 40.1 %copy-start.29 = (pred[4]{0:T(512)(128)(4,1)S(1)}, pred[4]{0:T(512)(128)(4,1)}, u32[]{:S(2)}) copy-start(pred[4]{0:T(512)(128)(4,1)} %iota_compare_fusion.10) | copy-start | bytes 16
  63.0 40.1 %copy-start.30 = (pred[4]{0:T(512)(128)(4,1)S(1)}, pred[4]{0:T(512)(128)(4,1)}, u32[]{:S(2)}) copy-start(pred[4]{0:T(512)(128)(4,1)} %iota_compare_fusion.5) | copy-start | bytes 16
  63.0 40.2 %copy-start.24 = (pred[4]{0:T(512)(128)(4,1)S(1)}, pred[4]{0:T(512)(128)(4,1)}, u32[]{:S(2)}) copy-start(pred[4]{0:T(512)(128)(4,1)} %compare_and_fusion) | copy-start | bytes 16
  108.3 11.8 %collective-permute-start.6 = (f32[2,1,128,64]{2,3,0,1:T(8,128)S(1)}, f32[2,1,128,64]{2,3,0,1:T(8,128)S(1)}, u32[]{:S(2)}, u32[]{:S(2)}) collective-permute-start(f32[2,1,128,64]{2,3,0,1:T(8,128)S(1)} %get-tuple-element.230), channel_id=1, source_target_pairs={{0,64},{64,128},{128,192},{192,0},{1,65},{65,129},{129,193},{193,1... | collective-permute-start | bytes 196616 | tf_op jit(solution)/shard_map/ppermute | solution.py:47
  113.3 8.5 %collective-permute-start.7 = (f32[2,1,128,64]{2,3,0,1:T(8,128)S(1)}, f32[2,1,128,64]{2,3,0,1:T(8,128)S(1)}, u32[]{:S(2)}, u32[]{:S(2)}) collective-permute-start(f32[2,1,128,64]{2,3,0,1:T(8,128)S(1)} %get-tuple-element.231), channel_id=1, source_target_pairs={{0,128},{64,192},{128,0},{192,64},{1,129},{65,193},{129,1},{193,65... | collective-permute-start | bytes 196616 | tf_op jit(solution)/shard_map/ppermute | solution.py:47
  117.5 6.2 %collective-permute-start.8 = (f32[2,1,128,64]{2,3,0,1:T(8,128)S(1)}, f32[2,1,128,64]{2,3,0,1:T(8,128)S(1)}, u32[]{:S(2)}, u32[]{:S(2)}) collective-permute-start(f32[2,1,128,64]{2,3,0,1:T(8,128)S(1)} %get-tuple-element.232), channel_id=1, source_target_pairs={{0,192},{64,0},{128,64},{192,128},{1,193},{65,1},{129,65},{193,129... | collective-permute-start | bytes 196616 | tf_op jit(solution)/shard_map/ppermute | solution.py:47
  124.8 15.4 %collective-permute-start.9 = (f32[2,4,128,64]{2,3,1,0:T(8,128)S(1)}, f32[2,4,128,64]{2,3,1,0:T(8,128)S(1)}, u32[]{:S(2)}, u32[]{:S(2)}) collective-permute-start(f32[2,4,128,64]{2,3,1,0:T(8,128)S(1)} %get-tuple-element.216), channel_id=1, source_target_pairs={{0,16},{16,32},{32,48},{48,0},{1,17},{17,33},{33,49},{49,1},{2,18}... | collective-permute-start | bytes 786440 | tf_op jit(solution)/shard_map/ppermute | solution.py:47
  128.9 11.4 %collective-permute-start.10 = (f32[2,4,128,64]{2,3,1,0:T(8,128)S(1)}, f32[2,4,128,64]{2,3,1,0:T(8,128)S(1)}, u32[]{:S(2)}, u32[]{:S(2)}) collective-permute-start(f32[2,4,128,64]{2,3,1,0:T(8,128)S(1)} %get-tuple-element.217), channel_id=1, source_target_pairs={{0,32},{16,48},{32,0},{48,16},{1,33},{17,49},{33,1},{49,17},{2,34}... | collective-permute-start | bytes 786440 | tf_op jit(solution)/shard_map/ppermute | solution.py:47
  132.2 9.4 %collective-permute-start.11 = (f32[2,4,128,64]{2,3,1,0:T(8,128)S(1)}, f32[2,4,128,64]{2,3,1,0:T(8,128)S(1)}, u32[]{:S(2)}, u32[]{:S(2)}) collective-permute-start(f32[2,4,128,64]{2,3,1,0:T(8,128)S(1)} %get-tuple-element.218), channel_id=1, source_target_pairs={{0,48},{16,0},{32,16},{48,32},{1,49},{17,1},{33,17},{49,33},{2,50}... | collective-permute-start | bytes 786440 | tf_op jit(solution)/shard_map/ppermute | solution.py:47
  (5 other events, 4.1 us)

commit v9 on v8

--- a/solution.py
+++ b/solution.py
@@ -197,7 +197,8 @@
         jnp.repeat(jnp.transpose(write_groups, (1, 0, 2)), repeats, axis=0),
         jnp.repeat(jnp.transpose(read_groups, (1, 0, 2)), repeats, axis=0),
     )
-    inner, read_part, write_part = lax.map(block_terms, pieces)
+    blocks = [block_terms(tuple(piece[i] for piece in pieces)) for i in range(count)]
+    inner, read_part, write_part = (jnp.stack(parts) for parts in zip(*blocks))
     incoming, prior = chain_states(passage, fwd_local, back_local)
     inner = jnp.transpose(inner, (1, 0, 2, 3)).reshape(length, heads, HEAD_DIM)
     read_intra = jnp.transpose(

time: 151 us -> 153 us (1.013)
  other arithmetic: 23.7 us -> 28.2 us
  local copies, waits for them, and re-layouts: 16.5 us -> 13.4 us
    ppermute x6, waiting for transfers between devices: 4.97 us -> 9.05 us  [exchange(): lax.ppermute(send, axis, [(i, (i + shift) % count) for i in range(count)])]
    ppermute x6, waiting for transfers between devices: 14.4 us -> 10.7 us  [exchange_received(): lax.ppermute(send, axis, [(i, (i + shift) % count) for i in range(count)])]
    unnamed x87 -> x81, local copies, waits for them, and re-layouts: 6.41 us -> 3.27 us
    select_n x10, other arithmetic: 0.38 us -> 2.26 us  [upper_weights(): return jnp.where(j > idx, w, 0.0)]
  transfers between devices with their start and end apart: 12 -> 12, of which waited for: 8 -> 9; matrix products, arithmetic and copies ran while one was open for 9% -> 9% of each run, Pallas kernels for 0% -> 0%
where the time goes in v9:
time: 153 us; the launch traced here: 152 us
  starting transfers between devices  47.2 us (31%)
  blocking collectives  33.8 us (22%)
  other arithmetic  28.2 us (18%)
  waiting for transfers between devices  19.8 us (13%)
  local copies, waits for them, and re-layouts  13.4 us (9%)
  matrix products  7.55 us (5%)
  between operations  1.73 us (1%)
    all_gather x1, blocking collectives, gathered_scan(): members = lax.all_gather(mine, axis)  33.8 us
    ppermute x6, starting transfers between devices, exchange_received(): lax.ppermute(send, axis, [(i, (i + shift) % count) for i in range(count)])  24.2 us
    ppermute x6, starting transfers between devices, exchange(): lax.ppermute(send, axis, [(i, (i + shift) % count) for i in range(count)])  23 us
    ppermute x6, waiting for transfers between devices, exchange_received(): lax.ppermute(send, axis, [(i, (i + shift) % count) for i in range(count)])  10.7 us
    ppermute x6, waiting for transfers between devices, exchange(): lax.ppermute(send, axis, [(i, (i + shift) % count) for i in range(count)])  9.05 us
    unnamed x81, local copies, waits for them, and re-layouts  3.27 us
  transfers between devices with their start and end apart: 12, of which 9 were waited for; matrix products, arithmetic and copies ran while one was open for 9% of the time, Pallas kernels for 0%

profile of v9, /device:TPU:56, one launch (start us, length us, event | category | flops | bytes accessed | tf_op | source)
XLA Modules:
  0.0 151.7 jit_solution(6755915596368970818)
XLA Ops:
  0.7 1.0 reduce_window_sum.11
  1.9 1.1 copy.292
  3.1 0.8 bitcast_convert_fusion
  3.8 1.1 copy.291
  5.0 0.8 bitcast_convert_fusion.1
  7.3 1.2 dynamic-slice_select_fusion
  8.5 3.4 %collective-permute-start = (f32[2,4,136,64]{2,3,1,0:T(8,128)}, f32[2,4,136,64]{2,3,1,0:T(8,128)S(1)}, u32[]{:S(2)}, u32[]{:S(2)}) collective-permute-start(f32[2,4,136,64]{2,3,1,0:T(8,128)} %get-tuple-element.132), channel_id=1, source_target_pairs={{0,16},{16,32},{32,48},{48,0},{1,17},{17,33},{33,49},{49,1},{2,18}... | collective-permute-start | bytes 835592 | tf_op jit(solution)/shard_map/ppermute | solution.py:56
  11.9 4.6 %collective-permute-start.1 = (f32[2,4,136,64]{2,3,1,0:T(8,128)}, f32[2,4,136,64]{2,3,1,0:T(8,128)S(1)}, u32[]{:S(2)}, u32[]{:S(2)}) collective-permute-start(f32[2,4,136,64]{2,3,1,0:T(8,128)} %get-tuple-element.131), channel_id=1, source_target_pairs={{0,32},{16,48},{32,0},{48,16},{1,33},{17,49},{33,1},{49,17},{2,34}... | collective-permute-start | bytes 835592 | tf_op jit(solution)/shard_map/ppermute | solution.py:56
  16.5 3.3 %collective-permute-start.2 = (f32[2,4,136,64]{2,3,1,0:T(8,128)S(1)}, f32[2,4,136,64]{2,3,1,0:T(8,128)S(1)}, u32[]{:S(2)}, u32[]{:S(2)}) collective-permute-start(f32[2,4,136,64]{2,3,1,0:T(8,128)S(1)} %get-tuple-element.130), channel_id=1, source_target_pairs={{0,48},{16,0},{32,16},{48,32},{1,49},{17,1},{33,17},{49,33},{2,50}... | collective-permute-start | bytes 835592 | tf_op jit(solution)/shard_map/ppermute | solution.py:56
  22.6 0.6 pad_clamp_fusion.3
  30.4 1.1 convolution_bitcast_fusion
  33.6 4.1 %collective-permute-done.1 = f32[2,4,136,64]{2,3,1,0:T(8,128)S(1)} collective-permute-done((f32[2,4,136,64]{2,3,1,0:T(8,128)}, f32[2,4,136,64]{2,3,1,0:T(8,128)S(1)}, u32[]{:S(2)}, u32[]{:S(2)}) %collective-permute-start.1) | collective-permute-done | bytes 278560 | tf_op jit(solution)/shard_map/ppermute | solution.py:56
  37.7 1.6 %collective-permute-done.2 = f32[2,4,136,64]{2,3,1,0:T(8,128)S(1)} collective-permute-done((f32[2,4,136,64]{2,3,1,0:T(8,128)S(1)}, f32[2,4,136,64]{2,3,1,0:T(8,128)S(1)}, u32[]{:S(2)}, u32[]{:S(2)}) %collective-permute-start.2) | collective-permute-done | bytes 278560 | tf_op jit(solution)/shard_map/ppermute | solution.py:56
  40.0 1.3 select_reduce_fusion.12
  41.3 0.8 select_reduce_fusion.3
  43.0 0.7 broadcast_select_fusion.1
  43.7 0.7 broadcast_select_fusion.2
  44.4 0.7 broadcast_select_fusion.3
  45.8 0.7 broadcast_select_fusion.11
  48.2 4.3 %collective-permute-start.3 = (f32[2,1,136,64]{2,3,0,1:T(8,128)S(1)}, f32[2,1,136,64]{2,3,0,1:T(8,128)S(1)}, u32[]{:S(2)}, u32[]{:S(2)}) collective-permute-start(f32[2,1,136,64]{2,3,0,1:T(8,128)S(1)} %get-tuple-element.144), channel_id=1, source_target_pairs={{0,64},{64,128},{128,192},{192,0},{1,65},{65,129},{129,193},{193,1... | collective-permute-start | bytes 208904 | tf_op jit(solution)/shard_map/ppermute | solution.py:56
  52.5 6.1 %collective-permute-start.4 = (f32[2,1,136,64]{2,3,0,1:T(8,128)S(1)}, f32[2,1,136,64]{2,3,0,1:T(8,128)S(1)}, u32[]{:S(2)}, u32[]{:S(2)}) collective-permute-start(f32[2,1,136,64]{2,3,0,1:T(8,128)S(1)} %get-tuple-element.143), channel_id=1, source_target_pairs={{0,128},{64,192},{128,0},{192,64},{1,129},{65,193},{129,1},{193,65... | collective-permute-start | bytes 208904 | tf_op jit(solution)/shard_map/ppermute | solution.py:56
  58.6 2.5 %collective-permute-start.5 = (f32[2,1,136,64]{2,3,1,0:T(8,128)S(1)}, f32[2,1,136,64]{2,3,1,0:T(8,128)S(1)}, u32[]{:S(2)}, u32[]{:S(2)}) collective-permute-start(f32[2,1,136,64]{2,3,1,0:T(8,128)S(1)} %get-tuple-element.142), channel_id=1, source_target_pairs={{0,192},{64,0},{128,64},{192,128},{1,193},{65,1},{129,65},{193,129... | collective-permute-start | bytes 208904 | tf_op jit(solution)/shard_map/ppermute | solution.py:56
  61.6 3.2 %collective-permute-done.4 = f32[2,1,136,64]{2,3,0,1:T(8,128)S(1)} collective-permute-done((f32[2,1,136,64]{2,3,0,1:T(8,128)S(1)}, f32[2,1,136,64]{2,3,0,1:T(8,128)S(1)}, u32[]{:S(2)}, u32[]{:S(2)}) %collective-permute-start.4) | collective-permute-done | bytes 69664 | tf_op jit(solution)/shard_map/ppermute | solution.py:56
  64.8 1.9 %collective-permute-done.5 = f32[2,1,136,64]{2,3,1,0:T(8,128)S(1)} collective-permute-done((f32[2,1,136,64]{2,3,1,0:T(8,128)S(1)}, f32[2,1,136,64]{2,3,1,0:T(8,128)S(1)}, u32[]{:S(2)}, u32[]{:S(2)}) %collective-permute-start.5) | collective-permute-done | bytes 69664 | tf_op jit(solution)/shard_map/ppermute | solution.py:56
  66.8 0.6 gather_fusion.6
  67.5 0.8 fusion.103
  70.2 0.6 gather_fusion.8
  70.9 0.6 gather_fusion.9
  71.6 0.7 pad_bitcast_fusion.1
  72.3 0.7 pad_bitcast_fusion
  73.0 33.8 %all-gather = f32[8,1,136,64]{2,3,1,0:T(8,128)S(1)} all-gather(f32[2,1,136,64]{2,3,1,0:T(8,128)S(1)} %pad_maximum_fusion.15), channel_id=2, replica_groups=mesh['czh'=4,'czl'=4,'cx'=4,'head'=8,'dp'=2] {'czh'}, dimensions={0}, use_global_device_ids=true | all-gather | bytes 348160 | tf_op jit(solution)/shard_map/all_gather | solution.py:102
  107.5 2.5 %maximum_bitcast_fusion.3 = f32[4]{0:T(128)S(1)} fusion(f32[1,1]{0,1:T(1,128)} %bitcast.98, f32[1,1]{0,1:T(1,128)} %bitcast.97, f32[1,1]{0,1:T(1,128)} %bitcast.96, f32[1,1]{0,1:T(1,128)} %bitcast.95), kind=kLoop, calls=%fused_computation.312 | loop fusion | flops 12 | bytes 32 | tf_op jit(solution)/shard_map/mul | solution.py:136
  110.0 1.9 %maximum_bitcast_fusion.2 = f32[4]{0:T(128)S(1)} fusion(f32[1,1]{0,1:T(1,128)} %bitcast.69, f32[1,1]{0,1:T(1,128)} %bitcast.68, f32[1,1]{0,1:T(1,128)} %bitcast.67, f32[1,1]{0,1:T(1,128)} %constant.221.clone.1), kind=kLoop, calls=%fused_computation.311 | loop fusion | flops 12 | bytes 32 | tf_op jit(solution)/shard_map/mul | solution.py:135
  112.1 5.0 %collective-permute-start.6 = (f32[2,1,128,64]{2,3,0,1:T(8,128)S(1)}, f32[2,1,128,64]{2,3,0,1:T(8,128)S(1)}, u32[]{:S(2)}, u32[]{:S(2)}) collective-permute-start(f32[2,1,128,64]{2,3,0,1:T(8,128)S(1)} %get-tuple-element.150), channel_id=1, source_target_pairs={{0,64},{64,128},{128,192},{192,0},{1,65},{65,129},{129,193},{193,1... | collective-permute-start | bytes 196616 | tf_op jit(solution)/shard_map/ppermute | solution.py:47
  117.1 4.2 %collective-permute-start.7 = (f32[2,1,128,64]{2,3,0,1:T(8,128)S(1)}, f32[2,1,128,64]{2,3,0,1:T(8,128)S(1)}, u32[]{:S(2)}, u32[]{:S(2)}) collective-permute-start(f32[2,1,128,64]{2,3,0,1:T(8,128)S(1)} %get-tuple-element.151), channel_id=1, source_target_pairs={{0,128},{64,192},{128,0},{192,64},{1,129},{65,193},{129,1},{193,65... | collective-permute-start | bytes 196616 | tf_op jit(solution)/shard_map/ppermute | solution.py:47
  121.3 2.7 %collective-permute-start.8 = (f32[2,1,128,64]{2,3,0,1:T(8,128)S(1)}, f32[2,1,128,64]{2,3,0,1:T(8,128)S(1)}, u32[]{:S(2)}, u32[]{:S(2)}) collective-permute-start(f32[2,1,128,64]{2,3,0,1:T(8,128)S(1)} %get-tuple-element.152), channel_id=1, source_target_pairs={{0,192},{64,0},{128,64},{192,128},{1,193},{65,1},{129,65},{193,129... | collective-permute-start | bytes 196616 | tf_op jit(solution)/shard_map/ppermute | solution.py:47
  124.0 1.6 %collective-permute-done.7 = f32[2,1,128,64]{2,3,0,1:T(8,128)S(1)} collective-permute-done((f32[2,1,128,64]{2,3,0,1:T(8,128)S(1)}, f32[2,1,128,64]{2,3,0,1:T(8,128)S(1)}, u32[]{:S(2)}, u32[]{:S(2)}) %collective-permute-start.7) | collective-permute-done | bytes 65568 | tf_op jit(solution)/shard_map/ppermute | solution.py:47
  125.6 1.9 %collective-permute-done.8 = f32[2,1,128,64]{2,3,0,1:T(8,128)S(1)} collective-permute-done((f32[2,1,128,64]{2,3,0,1:T(8,128)S(1)}, f32[2,1,128,64]{2,3,0,1:T(8,128)S(1)}, u32[]{:S(2)}, u32[]{:S(2)}) %collective-permute-start.8) | collective-permute-done | bytes 65568 | tf_op jit(solution)/shard_map/ppermute | solution.py:47
  127.4 0.7 gather_fusion
  128.7 4.1 %collective-permute-start.9 = (f32[2,4,128,64]{2,3,1,0:T(8,128)S(1)}, f32[2,4,128,64]{2,3,1,0:T(8,128)S(1)}, u32[]{:S(2)}, u32[]{:S(2)}) collective-permute-start(f32[2,4,128,64]{2,3,1,0:T(8,128)S(1)} %get-tuple-element.136), channel_id=1, source_target_pairs={{0,16},{16,32},{32,48},{48,0},{1,17},{17,33},{33,49},{49,1},{2,18}... | collective-permute-start | bytes 786440 | tf_op jit(solution)/shard_map/ppermute | solution.py:47
  132.7 3.7 %collective-permute-start.10 = (f32[2,4,128,64]{2,3,1,0:T(8,128)S(1)}, f32[2,4,128,64]{2,3,1,0:T(8,128)S(1)}, u32[]{:S(2)}, u32[]{:S(2)}) collective-permute-start(f32[2,4,128,64]{2,3,1,0:T(8,128)S(1)} %get-tuple-element.137), channel_id=1, source_target_pairs={{0,32},{16,48},{32,0},{48,16},{1,33},{17,49},{33,1},{49,17},{2,34}... | collective-permute-start | bytes 786440 | tf_op jit(solution)/shard_map/ppermute | solution.py:47
  136.4 3.5 %collective-permute-start.11 = (f32[2,4,128,64]{2,3,1,0:T(8,128)S(1)}, f32[2,4,128,64]{2,3,1,0:T(8,128)S(1)}, u32[]{:S(2)}, u32[]{:S(2)}) collective-permute-start(f32[2,4,128,64]{2,3,1,0:T(8,128)S(1)} %get-tuple-element.138), channel_id=1, source_target_pairs={{0,48},{16,0},{32,16},{48,32},{1,49},{17,1},{33,17},{49,33},{2,50}... | collective-permute-start | bytes 786440 | tf_op jit(solution)/shard_map/ppermute | solution.py:47
  140.8 3.4 %collective-permute-done.10 = f32[2,4,128,64]{2,3,1,0:T(8,128)S(1)} collective-permute-done((f32[2,4,128,64]{2,3,1,0:T(8,128)S(1)}, f32[2,4,128,64]{2,3,1,0:T(8,128)S(1)}, u32[]{:S(2)}, u32[]{:S(2)}) %collective-permute-start.10) | collective-permute-done | bytes 262176 | tf_op jit(solution)/shard_map/ppermute | solution.py:47
  144.2 1.8 %collective-permute-done.11 = f32[2,4,128,64]{2,3,1,0:T(8,128)S(1)} collective-permute-done((f32[2,4,128,64]{2,3,1,0:T(8,128)S(1)}, f32[2,4,128,64]{2,3,1,0:T(8,128)S(1)}, u32[]{:S(2)}, u32[]{:S(2)}) %collective-permute-start.11) | collective-permute-done | bytes 262176 | tf_op jit(solution)/shard_map/ppermute | solution.py:47
  146.0 0.7 gather_fusion.1
  147.6 0.9 copy.324
  148.4 1.6 %fusion.13 = bf16[1,128,128]{2,1,0:T(8,128)(2,1)} fusion(f32[128,1,128]{2,0,1:T(8,128)S(1)} %fusion.9, f32[16,128,64]{1,2,0:T(8,128)S(1)} %bitcast.341, f32[128,16,64]{0,2,1:T(8,128)S(1)} %bitcast.361), kind=kOutput, calls=%fused_computation.47 | convolution fusion | flops 201359360 | bytes 1146880 | tf_op jit(solution)/shard_map/sgkp,gknp->sgn/dot_general | solution.py:222
  150.0 1.6 %fusion.12 = bf16[1,128,128]{2,1,0:T(8,128)(2,1)} fusion(f32[128,1,128]{2,0,1:T(8,128)S(1)} %fusion.7, f32[16,128,64]{1,2,0:T(8,128)S(1)} %bitcast.359, f32[128,16,64]{0,2,1:T(8,128)S(1)} %bitcast.360), kind=kOutput, calls=%fused_computation.46 | convolution fusion | flops 201359360 | bytes 1146880 | tf_op jit(solution)/shard_map/tgkp,gknp->tgn/dot_general | solution.py:218
  (204 shorter events, 23.0 us)
Async XLA Ops:
  7.3 14.5 %copy-start = (bf16[1,128,128]{2,1,0:T(8,128)(2,1)S(1)}, bf16[1,128,128]{2,1,0:T(8,128)(2,1)}, u32[]{:S(2)}) copy-start(bf16[1,128,128]{2,1,0:T(8,128)(2,1)} %param.23) | copy-start | bytes 98308
  7.3 14.5 %copy-start.1 = (bf16[1,128,128]{2,1,0:T(8,128)(2,1)S(1)}, bf16[1,128,128]{2,1,0:T(8,128)(2,1)}, u32[]{:S(2)}) copy-start(bf16[1,128,128]{2,1,0:T(8,128)(2,1)} %param.24) | copy-start | bytes 98308
  8.5 25.1 %collective-permute-start = (f32[2,4,136,64]{2,3,1,0:T(8,128)}, f32[2,4,136,64]{2,3,1,0:T(8,128)S(1)}, u32[]{:S(2)}, u32[]{:S(2)}) collective-permute-start(f32[2,4,136,64]{2,3,1,0:T(8,128)} %get-tuple-element.132), channel_id=1, source_target_pairs={{0,16},{16,32},{32,48},{48,0},{1,17},{17,33},{33,49},{49,1},{2,18}... | collective-permute-start | bytes 835592 | tf_op jit(solution)/shard_map/ppermute | solution.py:56
  11.9 25.8 %collective-permute-start.1 = (f32[2,4,136,64]{2,3,1,0:T(8,128)}, f32[2,4,136,64]{2,3,1,0:T(8,128)S(1)}, u32[]{:S(2)}, u32[]{:S(2)}) collective-permute-start(f32[2,4,136,64]{2,3,1,0:T(8,128)} %get-tuple-element.131), channel_id=1, source_target_pairs={{0,32},{16,48},{32,0},{48,16},{1,33},{17,49},{33,1},{49,17},{2,34}... | collective-permute-start | bytes 835592 | tf_op jit(solution)/shard_map/ppermute | solution.py:56
  16.5 22.7 %collective-permute-start.2 = (f32[2,4,136,64]{2,3,1,0:T(8,128)S(1)}, f32[2,4,136,64]{2,3,1,0:T(8,128)S(1)}, u32[]{:S(2)}, u32[]{:S(2)}) collective-permute-start(f32[2,4,136,64]{2,3,1,0:T(8,128)S(1)} %get-tuple-element.130), channel_id=1, source_target_pairs={{0,48},{16,0},{32,16},{48,32},{1,49},{17,1},{33,17},{49,33},{2,50}... | collective-permute-start | bytes 835592 | tf_op jit(solution)/shard_map/ppermute | solution.py:56
  20.5 9.5 %copy-start.10 = (pred[4]{0:T(512)(128)(4,1)}, pred[4]{0:T(512)(128)(4,1)S(1)}, u32[]{:S(2)}) copy-start(pred[4]{0:T(512)(128)(4,1)S(1)} %iota_compare_fusion.13) | copy-start | bytes 16
  20.5 9.5 %copy-start.12 = (pred[4]{0:T(512)(128)(4,1)}, pred[4]{0:T(512)(128)(4,1)S(1)}, u32[]{:S(2)}) copy-start(pred[4]{0:T(512)(128)(4,1)S(1)} %iota_compare_fusion.14) | copy-start | bytes 16
  20.5 9.5 %copy-start.14 = (pred[4]{0:T(512)(128)(4,1)}, pred[4]{0:T(512)(128)(4,1)S(1)}, u32[]{:S(2)}) copy-start(pred[4]{0:T(512)(128)(4,1)S(1)} %iota_compare_fusion.15) | copy-start | bytes 16
  20.5 9.5 %copy-start.16 = (pred[4]{0:T(512)(128)(4,1)}, pred[4]{0:T(512)(128)(4,1)S(1)}, u32[]{:S(2)}) copy-start(pred[4]{0:T(512)(128)(4,1)S(1)} %iota_compare_fusion.6) | copy-start | bytes 16
  20.5 9.5 %copy-start.18 = (pred[4]{0:T(512)(128)(4,1)}, pred[4]{0:T(512)(128)(4,1)S(1)}, u32[]{:S(2)}) copy-start(pred[4]{0:T(512)(128)(4,1)S(1)} %iota_compare_fusion.7) | copy-start | bytes 16
  20.5 9.5 %copy-start.20 = (pred[4]{0:T(512)(128)(4,1)}, pred[4]{0:T(512)(128)(4,1)S(1)}, u32[]{:S(2)}) copy-start(pred[4]{0:T(512)(128)(4,1)S(1)} %iota_compare_fusion.8) | copy-start | bytes 16
  20.6 9.5 %copy-start.22 = (pred[4]{0:T(512)(128)(4,1)}, pred[4]{0:T(512)(128)(4,1)S(1)}, u32[]{:S(2)}) copy-start(pred[4]{0:T(512)(128)(4,1)S(1)} %iota_compare_fusion.9) | copy-start | bytes 16
  20.6 9.8 %copy-start.28 = (pred[4]{0:T(512)(128)(4,1)}, pred[4]{0:T(512)(128)(4,1)S(1)}, u32[]{:S(2)}) copy-start(pred[4]{0:T(512)(128)(4,1)S(1)} %iota_compare_fusion.11) | copy-start | bytes 16
  21.8 8.6 %copy-start.5 = (pred[128,128]{1,0:T(8,128)(4,1)}, pred[128,128]{1,0:T(8,128)(4,1)S(1)}, u32[]{:S(2)}) copy-start(pred[128,128]{1,0:T(8,128)(4,1)S(1)} %iota_compare_fusion) | copy-start | bytes 49156
  21.9 8.5 %copy-start.3 = (f32[128,128]{1,0:T(8,128)}, f32[128,128]{1,0:T(8,128)S(1)}, u32[]{:S(2)}) copy-start(f32[128,128]{1,0:T(8,128)S(1)} %fusion.70) | copy-start | bytes 196612
  31.5 8.4 %copy-start.11 = (pred[4]{0:T(512)(128)(4,1)S(1)}, pred[4]{0:T(512)(128)(4,1)}, u32[]{:S(2)}) copy-start(pred[4]{0:T(512)(128)(4,1)} %copy-done.10) | copy-start | bytes 16
  31.5 8.4 %copy-start.13 = (pred[4]{0:T(512)(128)(4,1)S(1)}, pred[4]{0:T(512)(128)(4,1)}, u32[]{:S(2)}) copy-start(pred[4]{0:T(512)(128)(4,1)} %copy-done.12) | copy-start | bytes 16
  31.5 8.4 %copy-start.15 = (pred[4]{0:T(512)(128)(4,1)S(1)}, pred[4]{0:T(512)(128)(4,1)}, u32[]{:S(2)}) copy-start(pred[4]{0:T(512)(128)(4,1)} %copy-done.14) | copy-start | bytes 16
  31.5 8.4 %copy-start.17 = (pred[4]{0:T(512)(128)(4,1)S(1)}, pred[4]{0:T(512)(128)(4,1)}, u32[]{:S(2)}) copy-start(pred[4]{0:T(512)(128)(4,1)} %copy-done.16) | copy-start | bytes 16
  31.6 15.4 %copy-start.29 = (pred[4]{0:T(512)(128)(4,1)S(1)}, pred[4]{0:T(512)(128)(4,1)}, u32[]{:S(2)}) copy-start(pred[4]{0:T(512)(128)(4,1)} %copy-done.28) | copy-start | bytes 16
  47.9 13.4 %copy-start.38 = (f32[4]{0:T(128)S(1)}, f32[4]{0:T(128)}, u32[]{:S(2)}) copy-start(f32[4]{0:T(128)} %pad.58.clone) | copy-start | bytes 52
  48.1 18.7 %copy-start.8 = (s32[1024]{0:T(1024)S(1)}, s32[1024]{0:T(1024)}, u32[]{:S(2)}) copy-start(s32[1024]{0:T(1024)} %pad_clamp_fusion.2) | copy-start | bytes 12292
  48.1 20.2 %copy-start.19 = (pred[4]{0:T(512)(128)(4,1)S(1)}, pred[4]{0:T(512)(128)(4,1)}, u32[]{:S(2)}) copy-start(pred[4]{0:T(512)(128)(4,1)} %copy-done.18) | copy-start | bytes 16
  48.1 20.2 %copy-start.21 = (pred[4]{0:T(512)(128)(4,1)S(1)}, pred[4]{0:T(512)(128)(4,1)}, u32[]{:S(2)}) copy-start(pred[4]{0:T(512)(128)(4,1)} %copy-done.20) | copy-start | bytes 16
  48.1 20.2 %copy-start.23 = (pred[4]{0:T(512)(128)(4,1)S(1)}, pred[4]{0:T(512)(128)(4,1)}, u32[]{:S(2)}) copy-start(pred[4]{0:T(512)(128)(4,1)} %copy-done.22) | copy-start | bytes 16
  48.1 20.2 %copy-start.30 = (pred[4]{0:T(512)(128)(4,1)S(1)}, pred[4]{0:T(512)(128)(4,1)}, u32[]{:S(2)}) copy-start(pred[4]{0:T(512)(128)(4,1)} %copy-done.28) | copy-start | bytes 16
  48.1 20.2 %copy-start.31 = (pred[4]{0:T(512)(128)(4,1)S(1)}, pred[4]{0:T(512)(128)(4,1)}, u32[]{:S(2)}) copy-start(pred[4]{0:T(512)(128)(4,1)} %iota_compare_fusion.12) | copy-start | bytes 16
  48.2 13.4 %collective-permute-start.3 = (f32[2,1,136,64]{2,3,0,1:T(8,128)S(1)}, f32[2,1,136,64]{2,3,0,1:T(8,128)S(1)}, u32[]{:S(2)}, u32[]{:S(2)}) collective-permute-start(f32[2,1,136,64]{2,3,0,1:T(8,128)S(1)} %get-tuple-element.144), channel_id=1, source_target_pairs={{0,64},{64,128},{128,192},{192,0},{1,65},{65,129},{129,193},{193,1... | collective-permute-start | bytes 208904 | tf_op jit(solution)/shard_map/ppermute | solution.py:56
  52.5 12.3 %collective-permute-start.4 = (f32[2,1,136,64]{2,3,0,1:T(8,128)S(1)}, f32[2,1,136,64]{2,3,0,1:T(8,128)S(1)}, u32[]{:S(2)}, u32[]{:S(2)}) collective-permute-start(f32[2,1,136,64]{2,3,0,1:T(8,128)S(1)} %get-tuple-element.143), channel_id=1, source_target_pairs={{0,128},{64,192},{128,0},{192,64},{1,129},{65,193},{129,1},{193,65... | collective-permute-start | bytes 208904 | tf_op jit(solution)/shard_map/ppermute | solution.py:56
  58.6 8.1 %collective-permute-start.5 = (f32[2,1,136,64]{2,3,1,0:T(8,128)S(1)}, f32[2,1,136,64]{2,3,1,0:T(8,128)S(1)}, u32[]{:S(2)}, u32[]{:S(2)}) collective-permute-start(f32[2,1,136,64]{2,3,1,0:T(8,128)S(1)} %get-tuple-element.142), channel_id=1, source_target_pairs={{0,192},{64,0},{128,64},{192,128},{1,193},{65,1},{129,65},{193,129... | collective-permute-start | bytes 208904 | tf_op jit(solution)/shard_map/ppermute | solution.py:56
  66.7 40.2 %copy-start.36 = (pred[4]{0:T(512)(128)(4,1)S(1)}, pred[4]{0:T(512)(128)(4,1)}, u32[]{:S(2)}) copy-start(pred[4]{0:T(512)(128)(4,1)} %iota_compare_fusion.10) | copy-start | bytes 16
  66.7 40.2 %copy-start.37 = (pred[4]{0:T(512)(128)(4,1)S(1)}, pred[4]{0:T(512)(128)(4,1)}, u32[]{:S(2)}) copy-start(pred[4]{0:T(512)(128)(4,1)} %iota_compare_fusion.5) | copy-start | bytes 16
  66.7 40.4 %copy-start.26 = (pred[4]{0:T(512)(128)(4,1)S(1)}, pred[4]{0:T(512)(128)(4,1)}, u32[]{:S(2)}) copy-start(pred[4]{0:T(512)(128)(4,1)} %compare_and_fusion) | copy-start | bytes 16
  71.5 52.4 %copy-start.32 = (f32[4]{0:T(128)S(1)}, f32[4]{0:T(128)}, u32[]{:S(2)}) copy-start(f32[4]{0:T(128)} %get-tuple-element.81) | copy-start | bytes 52
  71.5 52.4 %copy-start.33 = (f32[4]{0:T(128)S(1)}, f32[4]{0:T(128)}, u32[]{:S(2)}) copy-start(f32[4]{0:T(128)} %get-tuple-element.82) | copy-start | bytes 52
  71.5 52.5 %copy-start.34 = (f32[4]{0:T(128)S(1)}, f32[4]{0:T(128)}, u32[]{:S(2)}) copy-start(f32[4]{0:T(128)} %get-tuple-element.83) | copy-start | bytes 52
  71.5 52.5 %copy-start.35 = (f32[4]{0:T(128)S(1)}, f32[4]{0:T(128)}, u32[]{:S(2)}) copy-start(f32[4]{0:T(128)} %get-tuple-element.84) | copy-start | bytes 52
  73.0 55.1 %copy-start.27 = (pred[4]{0:T(512)(128)(4,1)S(1)}, pred[4]{0:T(512)(128)(4,1)}, u32[]{:S(2)}) copy-start(pred[4]{0:T(512)(128)(4,1)} %compare_and_fusion) | copy-start | bytes 16
  112.1 11.9 %collective-permute-start.6 = (f32[2,1,128,64]{2,3,0,1:T(8,128)S(1)}, f32[2,1,128,64]{2,3,0,1:T(8,128)S(1)}, u32[]{:S(2)}, u32[]{:S(2)}) collective-permute-start(f32[2,1,128,64]{2,3,0,1:T(8,128)S(1)} %get-tuple-element.150), channel_id=1, source_target_pairs={{0,64},{64,128},{128,192},{192,0},{1,65},{65,129},{129,193},{193,1... | collective-permute-start | bytes 196616 | tf_op jit(solution)/shard_map/ppermute | solution.py:47
  117.1 8.5 %collective-permute-start.7 = (f32[2,1,128,64]{2,3,0,1:T(8,128)S(1)}, f32[2,1,128,64]{2,3,0,1:T(8,128)S(1)}, u32[]{:S(2)}, u32[]{:S(2)}) collective-permute-start(f32[2,1,128,64]{2,3,0,1:T(8,128)S(1)} %get-tuple-element.151), channel_id=1, source_target_pairs={{0,128},{64,192},{128,0},{192,64},{1,129},{65,193},{129,1},{193,65... | collective-permute-start | bytes 196616 | tf_op jit(solution)/shard_map/ppermute | solution.py:47
  121.3 6.2 %collective-permute-start.8 = (f32[2,1,128,64]{2,3,0,1:T(8,128)S(1)}, f32[2,1,128,64]{2,3,0,1:T(8,128)S(1)}, u32[]{:S(2)}, u32[]{:S(2)}) collective-permute-start(f32[2,1,128,64]{2,3,0,1:T(8,128)S(1)} %get-tuple-element.152), channel_id=1, source_target_pairs={{0,192},{64,0},{128,64},{192,128},{1,193},{65,1},{129,65},{193,129... | collective-permute-start | bytes 196616 | tf_op jit(solution)/shard_map/ppermute | solution.py:47
  128.3 11.6 %copy-start.4 = (f32[128,128]{1,0:T(8,128)S(1)}, f32[128,128]{1,0:T(8,128)}, u32[]{:S(2)}) copy-start(f32[128,128]{1,0:T(8,128)} %copy-done.3) | copy-start | bytes 196612
  128.3 11.6 %copy-start.6 = (pred[128,128]{1,0:T(8,128)(4,1)S(1)}, pred[128,128]{1,0:T(8,128)(4,1)}, u32[]{:S(2)}) copy-start(pred[128,128]{1,0:T(8,128)(4,1)} %copy-done.5) | copy-start | bytes 49156
  128.3 11.6 %copy-start.25 = (f32[8,128]{1,0:T(8,128)S(1)}, f32[8,128]{1,0:T(8,128)}, u32[]{:S(2)}) copy-start(f32[8,128]{1,0:T(8,128)} %copy-done.24) | copy-start | bytes 12292
  128.4 11.9 %copy-start.2 = (f32[1,128,8,64]{1,3,2,0:T(8,128)S(1)}, f32[1,128,8,64]{1,3,2,0:T(8,128)}, u32[]{:S(2)}) copy-start(f32[1,128,8,64]{1,3,2,0:T(8,128)} %convolution_bitcast_fusion) | copy-start | bytes 786436
  128.7 12.1 %collective-permute-start.9 = (f32[2,4,128,64]{2,3,1,0:T(8,128)S(1)}, f32[2,4,128,64]{2,3,1,0:T(8,128)S(1)}, u32[]{:S(2)}, u32[]{:S(2)}) collective-permute-start(f32[2,4,128,64]{2,3,1,0:T(8,128)S(1)} %get-tuple-element.136), channel_id=1, source_target_pairs={{0,16},{16,32},{32,48},{48,0},{1,17},{17,33},{33,49},{49,1},{2,18}... | collective-permute-start | bytes 786440 | tf_op jit(solution)/shard_map/ppermute | solution.py:47
  132.7 11.4 %collective-permute-start.10 = (f32[2,4,128,64]{2,3,1,0:T(8,128)S(1)}, f32[2,4,128,64]{2,3,1,0:T(8,128)S(1)}, u32[]{:S(2)}, u32[]{:S(2)}) collective-permute-start(f32[2,4,128,64]{2,3,1,0:T(8,128)S(1)} %get-tuple-element.137), channel_id=1, source_target_pairs={{0,32},{16,48},{32,0},{48,16},{1,33},{17,49},{33,1},{49,17},{2,34}... | collective-permute-start | bytes 786440 | tf_op jit(solution)/shard_map/ppermute | solution.py:47
  136.4 9.6 %collective-permute-start.11 = (f32[2,4,128,64]{2,3,1,0:T(8,128)S(1)}, f32[2,4,128,64]{2,3,1,0:T(8,128)S(1)}, u32[]{:S(2)}, u32[]{:S(2)}) collective-permute-start(f32[2,4,128,64]{2,3,1,0:T(8,128)S(1)} %get-tuple-element.138), channel_id=1, source_target_pairs={{0,48},{16,0},{32,16},{48,32},{1,49},{17,1},{33,17},{49,33},{2,50}... | collective-permute-start | bytes 786440 | tf_op jit(solution)/shard_map/ppermute | solution.py:47
  (3 other events, 24.6 us)

commit v10 on v8

--- a/solution.py
+++ b/solution.py
@@ -40,21 +40,7 @@
 
 
 def exchange(pieces, axis):
-    count, index = lax.axis_size(axis), lax.axis_index(axis)
-    got = [jnp.take(pieces, index, axis=0)]
-    for shift in range(1, count):
-        send = jnp.take(pieces, (index + shift) % count, axis=0)
-        got.append(lax.ppermute(send, axis, [(i, (i + shift) % count) for i in range(count)]))
-    return jnp.take(jnp.stack(got), (index - jnp.arange(count)) % count, axis=0)
-
-
-def exchange_received(pieces, axis):
-    count, index = lax.axis_size(axis), lax.axis_index(axis)
-    got = [jnp.take(pieces, index, axis=0)]
-    for shift in range(1, count):
-        send = jnp.take(pieces, (index + shift) % count, axis=0)
-        got.append(lax.ppermute(send, axis, [(i, (i + shift) % count) for i in range(count)]))
-    return jnp.stack(got)
+    return lax.all_to_all(pieces, axis, 0, 0)
 
 
 def all_weights(p, lower):
@@ -117,9 +103,9 @@
         return z_scan(own_f, whole, True), z_scan(own_b, whole, False)
     part = heads // count
     pieces = jnp.stack([own_f, own_b]).reshape(2, count, part, n + 8, width)
-    received = exchange_received(jnp.transpose(pieces, (1, 0, 2, 3, 4)), axis)
-    slot = (lax.axis_index(axis) - jnp.arange(count)) % count
-    group = jnp.take(received[:, 0, :, n, 0], slot, axis=0)
+    received = exchange(jnp.transpose(pieces, (1, 0, 2, 3, 4)), axis)
+    slot = jnp.arange(count)
+    group = received[:, 0, :, n, 0]
     fwd_all, back_all = received[:, 0, :, :n], received[:, 1, :, :n]
     w_f = jnp.take(all_weights(group, True), slot, axis=1)
     w_b = jnp.take(all_weights(group, False), slot, axis=1)

time: 151 us -> 145 us (0.960)
  starting transfers between devices: 47.4 us -> 18.6 us
  waiting for transfers between devices: 19.4 us -> 47.7 us
  other arithmetic: 23.7 us -> 18.3 us
    all_to_all x0 -> x4, waiting for transfers between devices: none -> 47.7 us  [exchange(): return lax.all_to_all(pieces, axis, 0, 0)]
    ppermute x12 -> x0, starting transfers between devices: 47.4 us -> none  [the longest x6 24.2 us: exchange_received(): lax.ppermute(send, axis, [(i, (i + shift) % count) for i in range(count)])]
    ppermute x12 -> x0, waiting for transfers between devices: 19.4 us -> none  [the longest x6 14.4 us: exchange_received(): lax.ppermute(send, axis, [(i, (i + shift) % count) for i in range(count)])]
    all_to_all x0 -> x4, starting transfers between devices: none -> 18.6 us  [exchange(): return lax.all_to_all(pieces, axis, 0, 0)]
    and x5, other arithmetic: 2.68 us -> 0.04 us  [upper_weights(): span = ((idx < k) & (k < j))[:, :, None]]
    gather x4 -> x0, local copies, waits for them, and re-layouts: 2.5 us -> none  [the longest x2 1.3 us: exchange(): return jnp.take(jnp.stack(got), (index - jnp.arange(count)) % count, axis=0)]
    and x4, other arithmetic: 2.29 us -> 0.03 us  [lower_weights(): span = ((j < k) & (k < idx))[:, :, None]]
    reduce_prod x5 -> x7, other arithmetic: 1.47 us -> 3.53 us  [the longest x2 1.48 us: entry_states(): jnp.prod(jnp.where(k < x, group, 1.0), axis=0)]
  transfers between devices with their start and end apart: 12 -> 4, of which waited for: 8 -> 4; matrix products, arithmetic and copies ran while one was open for 9% -> 6% of each run, Pallas kernels for 0% -> 0%
where the time goes in v10:
time: 145 us; the launch traced here: 144 us
  waiting for transfers between devices  47.7 us (33%)
  blocking collectives  34.6 us (24%)
  starting transfers between devices  18.6 us (13%)
  other arithmetic  18.3 us (13%)
  local copies, waits for them, and re-layouts  17.8 us (12%)
  matrix products  5.6 us (4%)
    all_to_all x4, waiting for transfers between devices, exchange(): return lax.all_to_all(pieces, axis, 0, 0)  47.7 us
    all_gather x1, blocking collectives, gathered_scan(): members = lax.all_gather(mine, axis)  34.6 us
    all_to_all x4, starting transfers between devices, exchange(): return lax.all_to_all(pieces, axis, 0, 0)  18.6 us
    unnamed x43, local copies, waits for them, and re-layouts  5.16 us
  transfers between devices with their start and end apart: 4, of which 4 were waited for; matrix products, arithmetic and copies ran while one was open for 6% of the time, Pallas kernels for 0%

profile of v10, /device:TPU:56, one launch (start us, length us, event | category | flops | bytes accessed | tf_op | source)
XLA Modules:
  0.0 144.0 jit_solution(14541304464014449911)
XLA Ops:
  0.6 1.0 reduce_window_sum.11
  1.9 1.1 copy.153
  3.0 0.8 bitcast_convert_fusion
  3.8 1.1 copy.152
  4.9 0.8 bitcast_convert_fusion.1
  7.0 1.6 %copy_bitcast_fusion = f32[4,2,4,136,64]{3,4,2,1,0:T(8,128)} fusion(f32[1,4,4,136,64]{3,4,2,1,0:T(8,128)S(1)} %bitcast.303, f32[1,4,4,136,64]{3,4,2,1,0:T(8,128)S(1)} %bitcast.302), kind=kLoop, calls=%fused_computation.44 | loop fusion | flops 278528 | bytes 2228224 | tf_op jit(solution)/shard_map/transpose | solution.py:106
  8.6 4.4 %all-to-all-start = ((f32[4,2,4,136,64]{3,4,2,1,0:T(8,128)}), f32[4,2,4,136,64]{3,4,2,1,0:T(8,128)S(1)}, u32[]{:S(2)}, u32[]{:S(2)}) async-start(f32[4,2,4,136,64]{3,4,2,1,0:T(8,128)} %copy_bitcast_fusion), calls=%async_computation | async-start | bytes 4194304 | tf_op jit(solution)/shard_map/all_to_all | solution.py:43
  14.3 0.6 pad.38.clone
  15.1 24.3 %all-to-all-done = f32[4,2,4,136,64]{3,4,2,1,0:T(8,128)S(1)} async-done(((f32[4,2,4,136,64]{3,4,2,1,0:T(8,128)}), f32[4,2,4,136,64]{3,4,2,1,0:T(8,128)S(1)}, u32[]{:S(2)}, u32[]{:S(2)}) %all-to-all-start) | async-done | bytes 1114144 | tf_op jit(solution)/shard_map/all_to_all | solution.py:43
  40.3 0.6 gather_fusion.2
  40.9 0.6 gather_fusion.1
  41.8 0.8 copy_bitcast_fusion.1
  42.6 7.3 %all-to-all-start.1 = ((f32[4,2,1,136,64]{3,4,2,1,0:T(8,128)}), f32[4,2,1,136,64]{3,4,2,1,0:T(8,128)S(1)}, u32[]{:S(2)}, u32[]{:S(2)}) async-start(f32[4,2,1,136,64]{3,4,2,1,0:T(8,128)} %copy_bitcast_fusion.1), calls=%async_computation.1 | async-start | bytes 1048576 | tf_op jit(solution)/shard_map/all_to_all | solution.py:43
  49.9 0.6 gather_fusion.7
  50.5 0.6 gather_fusion
  51.2 0.6 copy.160
  51.8 0.6 copy.174
  52.4 0.7 select_reduce_fusion.26
  53.1 0.6 pad_maximum_fusion.14
  53.7 9.5 %all-to-all-done.1 = f32[4,2,1,136,64]{3,4,2,1,0:T(8,128)S(1)} async-done(((f32[4,2,1,136,64]{3,4,2,1,0:T(8,128)}), f32[4,2,1,136,64]{3,4,2,1,0:T(8,128)S(1)}, u32[]{:S(2)}, u32[]{:S(2)}) %all-to-all-start.1) | async-done | bytes 278560 | tf_op jit(solution)/shard_map/all_to_all | solution.py:43
  63.2 0.7 slice_reduce_fusion.4
  63.8 0.8 fusion.72
  65.1 0.6 gather_fusion.6
  65.6 0.7 copy.168
  66.4 0.6 gather_fusion.3
  67.0 0.7 copy.163
  67.7 0.6 gather_fusion.5
  68.3 0.6 gather_fusion.4
  69.3 0.6 pad_bitcast_fusion.1
  69.8 0.6 pad_bitcast_fusion
  70.5 34.6 %all-gather = f32[8,1,136,64]{2,3,1,0:T(8,128)S(1)} all-gather(f32[2,1,136,64]{2,3,1,0:T(8,128)S(1)} %copy.166), channel_id=2, replica_groups=mesh['czh'=4,'czl'=4,'cx'=4,'head'=8,'dp'=2] {'czh'}, dimensions={0}, use_global_device_ids=true | all-gather | bytes 348160 | tf_op jit(solution)/shard_map/all_gather | solution.py:88
  105.2 0.8 select_reduce_fusion.18
  106.0 0.7 fusion.51
  107.1 1.9 %maximum_bitcast_fusion = f32[4]{0:T(128)S(1)} fusion(f32[1,1]{0,1:T(1,128)} %bitcast.55, f32[1,1]{0,1:T(1,128)} %bitcast.54, f32[1,1]{0,1:T(1,128)} %bitcast.53, f32[1,1]{0,1:T(1,128)} %constant.76.clone.1), kind=kLoop, calls=%fused_computation.216 | loop fusion | flops 12 | bytes 32 | tf_op jit(solution)/shard_map/mul | solution.py:121
  109.1 2.5 %maximum_bitcast_fusion.1 = f32[4]{0:T(128)S(1)} fusion(f32[1,1]{0,1:T(1,128)} %bitcast.84, f32[1,1]{0,1:T(1,128)} %bitcast.83, f32[1,1]{0,1:T(1,128)} %bitcast.82, f32[1,1]{0,1:T(1,128)} %bitcast.81), kind=kLoop, calls=%fused_computation.217 | loop fusion | flops 12 | bytes 32 | tf_op jit(solution)/shard_map/mul | solution.py:122
  111.7 0.7 copy.169
  112.5 3.4 %all-to-all-start.2 = ((f32[4,2,1,128,64]{3,4,2,1,0:T(8,128)}), f32[4,2,1,128,64]{3,4,2,1,0:T(8,128)S(1)}, u32[]{:S(2)}, u32[]{:S(2)}) async-start(f32[4,2,1,128,64]{3,4,2,1,0:T(8,128)} %copy.169), calls=%async_computation.2 | async-start | bytes 524288 | tf_op jit(solution)/shard_map/all_to_all | solution.py:43
  116.6 6.0 %all-to-all-done.2 = f32[4,2,1,128,64]{3,4,2,1,0:T(8,128)S(1)} async-done(((f32[4,2,1,128,64]{3,4,2,1,0:T(8,128)}), f32[4,2,1,128,64]{3,4,2,1,0:T(8,128)S(1)}, u32[]{:S(2)}, u32[]{:S(2)}) %all-to-all-start.2) | async-done | bytes 262176 | tf_op jit(solution)/shard_map/all_to_all | solution.py:43
  123.0 1.1 copy.175
  124.1 3.5 %all-to-all-start.3 = ((f32[4,2,4,128,64]{3,4,2,1,0:T(8,128)}), f32[4,2,4,128,64]{3,4,2,1,0:T(8,128)S(1)}, u32[]{:S(2)}, u32[]{:S(2)}) async-start(f32[4,2,4,128,64]{3,4,2,1,0:T(8,128)} %copy.175), calls=%async_computation.3 | async-start | bytes 2097152 | tf_op jit(solution)/shard_map/all_to_all | solution.py:43
  127.7 2.2 %while.14 = (s32[]{:T(128)}, f32[2,128,8,64]{1,3,2,0:T(8,128)S(1)}, f32[2,128,128]{2,1,0:T(8,128)S(1)}, f32[2,128,128]{2,1,0:T(8,128)S(1)}, bf16[2,128,8,64]{1,3...) while((s32[]{:T(128)}, f32[2,128,8,64]{1,3,2,0:T(8,128)S(1)}, ...), condition=%wide.region_3.4_spmd, body=%wide.region_1.3_spmd.sunk | while | flops 43515904 | bytes 1224821 | solution.py:186
  130.0 0.7 copy.178
  130.8 7.9 %all-to-all-done.3 = f32[4,2,4,128,64]{3,4,2,1,0:T(8,128)S(1)} async-done(((f32[4,2,4,128,64]{3,4,2,1,0:T(8,128)}), f32[4,2,4,128,64]{3,4,2,1,0:T(8,128)S(1)}, u32[]{:S(2)}, u32[]{:S(2)}) %all-to-all-start.3) | async-done | bytes 1048608 | tf_op jit(solution)/shard_map/all_to_all | solution.py:43
  139.7 1.0 fusion.30
  140.7 0.7 copy.182
  141.4 1.0 fusion.31
  142.4 0.7 copy.181
  143.1 0.8 copy.180
  (152 shorter events, 10.1 us)
Async XLA Ops:
  1.9 5.1 %copy-start.6 = (f32[128,16]{0,1:T(8,128)}, f32[128,16]{0,1:T(8,128)S(1)}, u32[]{:S(2)}) copy-start(f32[128,16]{0,1:T(8,128)S(1)} %get-tuple-element.160) | copy-start | bytes 24580
  1.9 5.1 %copy-start.8 = (f32[128,16]{0,1:T(8,128)}, f32[128,16]{0,1:T(8,128)S(1)}, u32[]{:S(2)}) copy-start(f32[128,16]{0,1:T(8,128)S(1)} %get-tuple-element.161) | copy-start | bytes 24580
  8.6 6.3 %copy-start = (bf16[1,128,128]{2,1,0:T(8,128)(2,1)S(1)}, bf16[1,128,128]{2,1,0:T(8,128)(2,1)}, u32[]{:S(2)}) copy-start(bf16[1,128,128]{2,1,0:T(8,128)(2,1)} %param.17) | copy-start | bytes 98308
  8.6 6.3 %copy-start.2 = (bf16[1,128,128]{2,1,0:T(8,128)(2,1)S(1)}, bf16[1,128,128]{2,1,0:T(8,128)(2,1)}, u32[]{:S(2)}) copy-start(bf16[1,128,128]{2,1,0:T(8,128)(2,1)} %param.18) | copy-start | bytes 98308
  8.6 30.8 %all-to-all-start = ((f32[4,2,4,136,64]{3,4,2,1,0:T(8,128)}), f32[4,2,4,136,64]{3,4,2,1,0:T(8,128)S(1)}, u32[]{:S(2)}, u32[]{:S(2)}) async-start(f32[4,2,4,136,64]{3,4,2,1,0:T(8,128)} %copy_bitcast_fusion), calls=%async_computation | async-start | bytes 4194304 | tf_op jit(solution)/shard_map/all_to_all | solution.py:43
  13.1 38.0 %copy-start.13 = (pred[4]{0:T(512)(128)(4,1)}, pred[4]{0:T(512)(128)(4,1)S(1)}, u32[]{:S(2)}) copy-start(pred[4]{0:T(512)(128)(4,1)S(1)} %broadcast_compare_fusion) | copy-start | bytes 16
  42.6 20.6 %all-to-all-start.1 = ((f32[4,2,1,136,64]{3,4,2,1,0:T(8,128)}), f32[4,2,1,136,64]{3,4,2,1,0:T(8,128)S(1)}, u32[]{:S(2)}, u32[]{:S(2)}) async-start(f32[4,2,1,136,64]{3,4,2,1,0:T(8,128)} %copy_bitcast_fusion.1), calls=%async_computation.1 | async-start | bytes 1048576 | tf_op jit(solution)/shard_map/all_to_all | solution.py:43
  109.0 7.0 %copy-start.11 = (f32[4,4,4]{2,1,0:T(4,128)S(1)}, f32[4,4,4]{2,1,0:T(4,128)}, u32[]{:S(2)}) copy-start(f32[4,4,4]{2,1,0:T(4,128)} %copy.160) | copy-start | bytes 772
  111.7 4.5 %copy-start.10 = (f32[4,4,4]{2,1,0:T(4,128)S(1)}, f32[4,4,4]{2,1,0:T(4,128)}, u32[]{:S(2)}) copy-start(f32[4,4,4]{2,1,0:T(4,128)} %copy.174) | copy-start | bytes 772
  112.5 10.2 %all-to-all-start.2 = ((f32[4,2,1,128,64]{3,4,2,1,0:T(8,128)}), f32[4,2,1,128,64]{3,4,2,1,0:T(8,128)S(1)}, u32[]{:S(2)}, u32[]{:S(2)}) async-start(f32[4,2,1,128,64]{3,4,2,1,0:T(8,128)} %copy.169), calls=%async_computation.2 | async-start | bytes 524288 | tf_op jit(solution)/shard_map/all_to_all | solution.py:43
  115.9 0.7 copy-start.14
  115.9 0.7 copy-start.15
  115.9 0.7 copy-start.16
  115.9 0.7 copy-start.17
  116.0 6.7 %copy-start.12 = (f32[4,4]{1,0:T(4,128)S(1)}, f32[4,4]{1,0:T(4,128)}, u32[]{:S(2)}) copy-start(f32[4,4]{1,0:T(4,128)} %pad_maximum_fusion.14) | copy-start | bytes 196
  123.0 4.7 %copy-start.1 = (f32[2,128,8,64]{1,3,2,0:T(8,128)S(1)}, f32[2,128,8,64]{1,3,2,0:T(8,128)}, u32[]{:S(2)}) copy-start(f32[2,128,8,64]{1,3,2,0:T(8,128)} %custom-call.16) | copy-start | bytes 1572868
  123.0 4.7 %copy-start.4 = (f32[2,128,128]{2,1,0:T(8,128)S(1)}, f32[2,128,128]{2,1,0:T(8,128)}, u32[]{:S(2)}) copy-start(f32[2,128,128]{2,1,0:T(8,128)} %custom-call.17) | copy-start | bytes 393220
  123.0 4.7 %copy-start.5 = (f32[2,128,128]{2,1,0:T(8,128)S(1)}, f32[2,128,128]{2,1,0:T(8,128)}, u32[]{:S(2)}) copy-start(f32[2,128,128]{2,1,0:T(8,128)} %custom-call.18) | copy-start | bytes 393220
  124.1 14.6 %all-to-all-start.3 = ((f32[4,2,4,128,64]{3,4,2,1,0:T(8,128)}), f32[4,2,4,128,64]{3,4,2,1,0:T(8,128)S(1)}, u32[]{:S(2)}, u32[]{:S(2)}) async-start(f32[4,2,4,128,64]{3,4,2,1,0:T(8,128)} %copy.175), calls=%async_computation.3 | async-start | bytes 2097152 | tf_op jit(solution)/shard_map/all_to_all | solution.py:43
  130.0 9.3 %copy-start.7 = (f32[128,16]{0,1:T(8,128)S(1)}, f32[128,16]{0,1:T(8,128)}, u32[]{:S(2)}) copy-start(f32[128,16]{0,1:T(8,128)} %copy-done.6) | copy-start | bytes 24580
  130.0 9.3 %copy-start.9 = (f32[128,16]{0,1:T(8,128)S(1)}, f32[128,16]{0,1:T(8,128)}, u32[]{:S(2)}) copy-start(f32[128,16]{0,1:T(8,128)} %copy-done.8) | copy-start | bytes 24580
  138.8 0.8 copy-start.3

commit v11 on v10

--- a/solution.py
+++ b/solution.py
@@ -85,7 +85,7 @@
     count, index = lax.axis_size(axis), lax.axis_index(axis)
     n = own_f.shape[1] - 8
     mine = jnp.stack([own_f, own_b])
-    members = lax.all_gather(mine, axis)
+    members = lax.all_to_all(jnp.broadcast_to(mine[None], (count,) + mine.shape), axis, 0, 0)
     group = members[:, 0, :, n, 0]
     entry_f = weighted(lower_weights(group, index), members[:, 0, :, :n])
     entry_b = weighted(upper_weights(group, index), members[:, 1, :, :n])

time: 145 us -> 166 us (1.14)
  blocking collectives: 34.6 us -> 0 us
  other arithmetic: 18.3 us -> 41 us
  starting transfers between devices: 18.6 us -> 38.8 us
  local copies, waits for them, and re-layouts: 17.8 us -> 25 us
  waiting for transfers between devices: 47.7 us -> 52.2 us
    all_gather x1 -> x0, blocking collectives: 34.6 us -> none  [gathered_scan(): members = lax.all_gather(mine, axis)]
    all_to_all x0 -> x1, starting transfers between devices: none -> 16 us  [gathered_scan(): lax.all_to_all(jnp.broadcast_to(mine[None], (count,) + mine.shape), axis,...]
    all_to_all x0 -> x1, waiting for transfers between devices: none -> 11.4 us  [gathered_scan(): lax.all_to_all(jnp.broadcast_to(mine[None], (count,) + mine.shape), axis,...]
    all_to_all x4, waiting for transfers between devices: 47.7 us -> 40.8 us  [exchange(): return lax.all_to_all(pieces, axis, 0, 0)]
    another operation x4, other arithmetic: 0.05 us -> 5.11 us  [all_weights(): return jnp.stack(rows)]
    select_n x10, other arithmetic: 0.39 us -> 4.88 us  [upper_weights(): return jnp.where(j > idx, w, 0.0)]
    all_to_all x4, starting transfers between devices: 18.6 us -> 22.8 us  [exchange(): return lax.all_to_all(pieces, axis, 0, 0)]
    select_n x8, other arithmetic: 0.3 us -> 3.82 us  [lower_weights(): return jnp.where(j < idx, w, 0.0)]
  transfers between devices with their start and end apart: 4 -> 5, of which waited for: 4 -> 5; matrix products, arithmetic and copies ran while one was open for 6% -> 19% of each run, Pallas kernels for 0% -> 0%
where the time goes in v11:
time: 166 us; the launch traced here: 164 us
  waiting for transfers between devices  52.2 us (31%)
  other arithmetic  41 us (25%)
  starting transfers between devices  38.8 us (23%)
  local copies, waits for them, and re-layouts  25 us (15%)
  matrix products  5.6 us (3%)
    all_to_all x4, waiting for transfers between devices, exchange(): return lax.all_to_all(pieces, axis, 0, 0)  40.8 us
    all_to_all x4, starting transfers between devices, exchange(): return lax.all_to_all(pieces, axis, 0, 0)  22.8 us
    all_to_all x1, starting transfers between devices, gathered_scan(): lax.all_to_all(jnp.broadcast_to(mine[None], (count,) + mine.shape), axis,...  16 us
    all_to_all x1, waiting for transfers between devices, gathered_scan(): lax.all_to_all(jnp.broadcast_to(mine[None], (count,) + mine.shape), axis,...  11.4 us
    another operation x4, other arithmetic, all_weights(): return jnp.stack(rows)  5.11 us
    select_n x10, other arithmetic, upper_weights(): return jnp.where(j > idx, w, 0.0)  4.88 us
    unnamed x55, local copies, waits for them, and re-layouts  4.71 us
    gather x3, local copies, waits for them, and re-layouts, entry_states(): w_b = jnp.take(all_weights(group, False), slot, axis=1)  4.28 us
  transfers between devices with their start and end apart: 5, of which 5 were waited for; matrix products, arithmetic and copies ran while one was open for 19% of the time, Pallas kernels for 0%

profile of v11, /device:TPU:56, one launch (start us, length us, event | category | flops | bytes accessed | tf_op | source)
XLA Modules:
  0.0 164.1 jit_solution(2410983004178207662)
XLA Ops:
  0.6 1.0 reduce_window_sum.11
  1.9 1.1 copy.127
  3.0 0.8 bitcast_convert_fusion
  3.8 1.1 copy.126
  4.9 0.8 bitcast_convert_fusion.1
  7.0 1.6 copy_bitcast_fusion
  8.6 4.4 %all-to-all-start = ((f32[4,2,4,136,64]{3,4,2,1,0:T(8,128)}), f32[4,2,4,136,64]{3,4,2,1,0:T(8,128)S(1)}, u32[]{:S(2)}, u32[]{:S(2)}) async-start(f32[4,2,4,136,64]{3,4,2,1,0:T(8,128)} %copy_bitcast_fusion), calls=%async_computation | async-start | bytes 4194304 | tf_op jit(solution)/shard_map/all_to_all | solution.py:43
  15.2 24.2 %all-to-all-done = f32[4,2,4,136,64]{3,4,2,1,0:T(8,128)S(1)} async-done(((f32[4,2,4,136,64]{3,4,2,1,0:T(8,128)}), f32[4,2,4,136,64]{3,4,2,1,0:T(8,128)S(1)}, u32[]{:S(2)}, u32[]{:S(2)}) %all-to-all-start) | async-done | bytes 1114144 | tf_op jit(solution)/shard_map/all_to_all | solution.py:43
  45.8 0.8 copy_bitcast_fusion.1
  46.7 7.3 %all-to-all-start.1 = ((f32[4,2,1,136,64]{3,4,2,1,0:T(8,128)}), f32[4,2,1,136,64]{3,4,2,1,0:T(8,128)S(1)}, u32[]{:S(2)}, u32[]{:S(2)}) async-start(f32[4,2,1,136,64]{3,4,2,1,0:T(8,128)} %copy_bitcast_fusion.1), calls=%async_computation.1 | async-start | bytes 1048576 | tf_op jit(solution)/shard_map/all_to_all | solution.py:43
  54.0 1.3 pad_maximum_fusion.9
  55.3 1.9 %gather_fusion.7 = f32[4,4,4]{2,1,0:T(4,128)} fusion(f32[4,4,4]{2,0,1:T(4,128)} %pad_maximum_fusion.9, s32[1024]{0:T(1024)S(1)} %pad_clamp_fusion), kind=kCustom, calls=%fused_computation.4.clone | custom fusion | bytes 528 | tf_op jit(solution)/shard_map/jit(_take)/gather | solution.py:111
  57.1 0.8 broadcast_select_fusion.6
  57.9 1.3 pad_maximum_fusion.8
  59.2 1.9 %gather_fusion = f32[4,4,4]{2,1,0:T(4,128)} fusion(f32[4,4,4]{2,0,1:T(4,128)} %pad_maximum_fusion.8, s32[1024]{0:T(1024)S(1)} %pad_clamp_fusion), kind=kCustom, calls=%fused_computation.clone | custom fusion | bytes 528 | tf_op jit(solution)/shard_map/jit(_take)/gather | solution.py:110
  61.0 0.8 select_bitcast_fusion.1
  63.0 1.4 select_reduce_fusion.26
  65.0 2.3 %all-to-all-done.1 = f32[4,2,1,136,64]{3,4,2,1,0:T(8,128)S(1)} async-done(((f32[4,2,1,136,64]{3,4,2,1,0:T(8,128)}), f32[4,2,1,136,64]{3,4,2,1,0:T(8,128)S(1)}, u32[]{:S(2)}, u32[]{:S(2)}) %all-to-all-start.1) | async-done | bytes 278560 | tf_op jit(solution)/shard_map/all_to_all | solution.py:43
  67.9 0.8 fusion.72
  68.7 1.4 select_reduce_fusion.23
  74.0 1.2 gather_fusion.5
  75.1 1.2 broadcast_select_fusion.11
  76.9 1.2 gather_fusion.4
  80.8 0.9 broadcast_in_dim.525
  81.7 16.0 %all-to-all-start.2 = ((f32[4,2,1,136,64]{3,4,2,1,0:T(8,128)}), f32[4,2,1,136,64]{3,4,2,1,0:T(8,128)}, u32[]{:S(2)}, u32[]{:S(2)}) async-start(f32[4,2,1,136,64]{3,4,2,1,0:T(8,128)} %broadcast_in_dim.525), calls=%async_computation.2 | async-start | bytes 1048576 | tf_op jit(solution)/shard_map/all_to_all | solution.py:88
  97.7 1.2 pad_maximum_fusion.12
  98.9 1.3 pad_maximum_fusion.11
  100.2 2.5 %maximum_bitcast_fusion.1 = f32[4]{0:T(128)} fusion(f32[1,1]{0,1:T(1,128)} %bitcast.55, f32[1,1]{0,1:T(1,128)} %bitcast.54, f32[1,1]{0,1:T(1,128)} %bitcast.53, f32[1,1]{0,1:T(1,128)} %constant.76.clone.1), kind=kLoop, calls=%fused_computation.216 | loop fusion | flops 12 | bytes 32 | tf_op jit(solution)/shard_map/mul | solution.py:121
  103.4 1.1 gather_fusion.6
  104.6 1.3 copy.141
  105.9 0.8 copy.136
  106.6 1.1 gather_fusion.3
  107.8 0.8 copy.137
  108.5 3.1 %maximum_bitcast_fusion.2 = f32[4]{0:T(128)} fusion(f32[1,1]{0,1:T(1,128)} %bitcast.84, f32[1,1]{0,1:T(1,128)} %bitcast.83, f32[1,1]{0,1:T(1,128)} %bitcast.82, f32[1,1]{0,1:T(1,128)} %bitcast.81), kind=kLoop, calls=%fused_computation.217 | loop fusion | flops 12 | bytes 32 | tf_op jit(solution)/shard_map/mul | solution.py:122
  112.5 11.4 %all-to-all-done.2 = f32[4,2,1,136,64]{3,4,2,1,0:T(8,128)} async-done(((f32[4,2,1,136,64]{3,4,2,1,0:T(8,128)}), f32[4,2,1,136,64]{3,4,2,1,0:T(8,128)}, u32[]{:S(2)}, u32[]{:S(2)}) %all-to-all-start.2) | async-done | bytes 278560 | tf_op jit(solution)/shard_map/all_to_all | solution.py:88
  123.9 0.8 slice_reduce_fusion.3
  124.8 0.8 select_reduce_fusion.18
  125.6 1.1 fusion.45
  126.7 0.8 bitcast_add_fusion.3
  129.0 7.6 %all-to-all-start.3 = ((f32[4,2,1,128,64]{3,4,2,1,0:T(8,128)}), f32[4,2,1,128,64]{3,4,2,1,0:T(8,128)S(1)}, u32[]{:S(2)}, u32[]{:S(2)}) async-start(f32[4,2,1,128,64]{3,4,2,1,0:T(8,128)} %copy.144), calls=%async_computation.3 | async-start | bytes 524288 | tf_op jit(solution)/shard_map/all_to_all | solution.py:43
  137.3 6.0 %all-to-all-done.3 = f32[4,2,1,128,64]{3,4,2,1,0:T(8,128)S(1)} async-done(((f32[4,2,1,128,64]{3,4,2,1,0:T(8,128)}), f32[4,2,1,128,64]{3,4,2,1,0:T(8,128)S(1)}, u32[]{:S(2)}, u32[]{:S(2)}) %all-to-all-start.3) | async-done | bytes 262176 | tf_op jit(solution)/shard_map/all_to_all | solution.py:43
  143.7 1.1 copy.150
  144.8 3.5 %all-to-all-start.4 = ((f32[4,2,4,128,64]{3,4,2,1,0:T(8,128)}), f32[4,2,4,128,64]{3,4,2,1,0:T(8,128)S(1)}, u32[]{:S(2)}, u32[]{:S(2)}) async-start(f32[4,2,4,128,64]{3,4,2,1,0:T(8,128)} %copy.150), calls=%async_computation.4 | async-start | bytes 2097152 | tf_op jit(solution)/shard_map/all_to_all | solution.py:43
  148.4 2.2 %while.14 = (s32[]{:T(128)}, f32[2,128,8,64]{1,3,2,0:T(8,128)S(1)}, f32[2,128,128]{2,1,0:T(8,128)S(1)}, f32[2,128,128]{2,1,0:T(8,128)S(1)}, bf16[2,128,8,64]{1,3...) while((s32[]{:T(128)}, f32[2,128,8,64]{1,3,2,0:T(8,128)S(1)}, ...), condition=%wide.region_3.4_spmd, body=%wide.region_1.3_spmd.sunk | while | flops 43515904 | bytes 1224821 | solution.py:186
  150.9 8.3 %all-to-all-done.4 = f32[4,2,4,128,64]{3,4,2,1,0:T(8,128)S(1)} async-done(((f32[4,2,4,128,64]{3,4,2,1,0:T(8,128)}), f32[4,2,4,128,64]{3,4,2,1,0:T(8,128)S(1)}, u32[]{:S(2)}, u32[]{:S(2)}) %all-to-all-start.4) | async-done | bytes 1048608 | tf_op jit(solution)/shard_map/all_to_all | solution.py:43
  159.8 1.0 fusion.30
  161.6 1.0 fusion.31
  163.3 0.8 copy.155
  (165 shorter events, 28.2 us)
Async XLA Ops:
  1.9 5.1 %copy-start.3 = (f32[128,16]{0,1:T(8,128)}, f32[128,16]{0,1:T(8,128)S(1)}, u32[]{:S(2)}) copy-start(f32[128,16]{0,1:T(8,128)S(1)} %get-tuple-element.157) | copy-start | bytes 24580
  1.9 5.1 %copy-start.5 = (f32[128,16]{0,1:T(8,128)}, f32[128,16]{0,1:T(8,128)S(1)}, u32[]{:S(2)}) copy-start(f32[128,16]{0,1:T(8,128)S(1)} %get-tuple-element.158) | copy-start | bytes 24580
  8.6 6.5 %copy-start = (bf16[1,128,128]{2,1,0:T(8,128)(2,1)S(1)}, bf16[1,128,128]{2,1,0:T(8,128)(2,1)}, u32[]{:S(2)}) copy-start(bf16[1,128,128]{2,1,0:T(8,128)(2,1)} %param.17) | copy-start | bytes 98308
  8.6 6.5 %copy-start.2 = (bf16[1,128,128]{2,1,0:T(8,128)(2,1)S(1)}, bf16[1,128,128]{2,1,0:T(8,128)(2,1)}, u32[]{:S(2)}) copy-start(bf16[1,128,128]{2,1,0:T(8,128)(2,1)} %param.18) | copy-start | bytes 98308
  8.6 30.8 %all-to-all-start = ((f32[4,2,4,136,64]{3,4,2,1,0:T(8,128)}), f32[4,2,4,136,64]{3,4,2,1,0:T(8,128)S(1)}, u32[]{:S(2)}, u32[]{:S(2)}) async-start(f32[4,2,4,136,64]{3,4,2,1,0:T(8,128)} %copy_bitcast_fusion), calls=%async_computation | async-start | bytes 4194304 | tf_op jit(solution)/shard_map/all_to_all | solution.py:43
  13.0 31.2 %copy-start.11 = (pred[4]{0:T(512)(128)(4,1)}, pred[4]{0:T(512)(128)(4,1)S(1)}, u32[]{:S(2)}) copy-start(pred[4]{0:T(512)(128)(4,1)S(1)} %iota_compare_fusion.6) | copy-start | bytes 16
  13.1 33.6 %copy-start.12 = (pred[4]{0:T(512)(128)(4,1)}, pred[4]{0:T(512)(128)(4,1)S(1)}, u32[]{:S(2)}) copy-start(pred[4]{0:T(512)(128)(4,1)S(1)} %iota_compare_fusion.7) | copy-start | bytes 16
  13.1 33.6 %copy-start.13 = (pred[4]{0:T(512)(128)(4,1)}, pred[4]{0:T(512)(128)(4,1)S(1)}, u32[]{:S(2)}) copy-start(pred[4]{0:T(512)(128)(4,1)S(1)} %iota_compare_fusion.8) | copy-start | bytes 16
  13.1 33.5 %copy-start.14 = (pred[4]{0:T(512)(128)(4,1)}, pred[4]{0:T(512)(128)(4,1)S(1)}, u32[]{:S(2)}) copy-start(pred[4]{0:T(512)(128)(4,1)S(1)} %iota_compare_fusion.9) | copy-start | bytes 16
  13.1 33.5 %copy-start.15 = (pred[4]{0:T(512)(128)(4,1)}, pred[4]{0:T(512)(128)(4,1)S(1)}, u32[]{:S(2)}) copy-start(pred[4]{0:T(512)(128)(4,1)S(1)} %iota_compare_fusion.13) | copy-start | bytes 16
  13.1 33.5 %copy-start.16 = (pred[4]{0:T(512)(128)(4,1)}, pred[4]{0:T(512)(128)(4,1)S(1)}, u32[]{:S(2)}) copy-start(pred[4]{0:T(512)(128)(4,1)S(1)} %iota_compare_fusion.14) | copy-start | bytes 16
  13.2 26.4 %copy-start.17 = (pred[4]{0:T(512)(128)(4,1)}, pred[4]{0:T(512)(128)(4,1)S(1)}, u32[]{:S(2)}) copy-start(pred[4]{0:T(512)(128)(4,1)S(1)} %iota_compare_fusion.15) | copy-start | bytes 16
  13.2 33.5 %copy-start.18 = (pred[4]{0:T(512)(128)(4,1)}, pred[4]{0:T(512)(128)(4,1)S(1)}, u32[]{:S(2)}) copy-start(pred[4]{0:T(512)(128)(4,1)S(1)} %iota_compare_fusion.11) | copy-start | bytes 16
  13.2 33.5 %copy-start.19 = (pred[4]{0:T(512)(128)(4,1)}, pred[4]{0:T(512)(128)(4,1)S(1)}, u32[]{:S(2)}) copy-start(pred[4]{0:T(512)(128)(4,1)S(1)} %iota_compare_fusion.12) | copy-start | bytes 16
  13.2 33.4 %copy-start.10 = (pred[4]{0:T(512)(128)(4,1)}, pred[4]{0:T(512)(128)(4,1)S(1)}, u32[]{:S(2)}) copy-start(pred[4]{0:T(512)(128)(4,1)S(1)} %broadcast_compare_fusion) | copy-start | bytes 16
  46.7 20.6 %all-to-all-start.1 = ((f32[4,2,1,136,64]{3,4,2,1,0:T(8,128)}), f32[4,2,1,136,64]{3,4,2,1,0:T(8,128)S(1)}, u32[]{:S(2)}, u32[]{:S(2)}) async-start(f32[4,2,1,136,64]{3,4,2,1,0:T(8,128)} %copy_bitcast_fusion.1), calls=%async_computation.1 | async-start | bytes 1048576 | tf_op jit(solution)/shard_map/all_to_all | solution.py:43
  79.5 18.2 %copy-start.24 = (f32[1,4,1]{1,2,0:T(1,128)S(1)}, f32[1,4,1]{1,2,0:T(1,128)}, u32[]{:S(2)}) copy-start(f32[1,4,1]{1,2,0:T(1,128)} %compare_select_fusion.5) | copy-start | bytes 52
  81.7 42.3 %all-to-all-start.2 = ((f32[4,2,1,136,64]{3,4,2,1,0:T(8,128)}), f32[4,2,1,136,64]{3,4,2,1,0:T(8,128)}, u32[]{:S(2)}, u32[]{:S(2)}) async-start(f32[4,2,1,136,64]{3,4,2,1,0:T(8,128)} %broadcast_in_dim.525), calls=%async_computation.2 | async-start | bytes 1048576 | tf_op jit(solution)/shard_map/all_to_all | solution.py:88
  126.7 10.0 %copy-start.8 = (f32[4,4,4]{2,1,0:T(4,128)S(1)}, f32[4,4,4]{2,1,0:T(4,128)}, u32[]{:S(2)}) copy-start(f32[4,4,4]{2,1,0:T(4,128)} %copy.134) | copy-start | bytes 772
  128.2 8.7 %copy-start.7 = (f32[4,4,4]{2,1,0:T(4,128)S(1)}, f32[4,4,4]{2,1,0:T(4,128)}, u32[]{:S(2)}) copy-start(f32[4,4,4]{2,1,0:T(4,128)} %copy.149) | copy-start | bytes 772
  129.0 14.4 %all-to-all-start.3 = ((f32[4,2,1,128,64]{3,4,2,1,0:T(8,128)}), f32[4,2,1,128,64]{3,4,2,1,0:T(8,128)S(1)}, u32[]{:S(2)}, u32[]{:S(2)}) async-start(f32[4,2,1,128,64]{3,4,2,1,0:T(8,128)} %copy.144), calls=%async_computation.3 | async-start | bytes 524288 | tf_op jit(solution)/shard_map/all_to_all | solution.py:43
  136.6 0.6 copy-start.20
  136.6 0.7 copy-start.21
  136.6 0.7 copy-start.22
  136.6 0.7 copy-start.23
  136.7 6.8 %copy-start.9 = (f32[4,4]{1,0:T(4,128)S(1)}, f32[4,4]{1,0:T(4,128)}, u32[]{:S(2)}) copy-start(f32[4,4]{1,0:T(4,128)} %pad_maximum_fusion.13) | copy-start | bytes 196
  143.7 4.7 %copy-start.1 = (f32[2,128,8,64]{1,3,2,0:T(8,128)S(1)}, f32[2,128,8,64]{1,3,2,0:T(8,128)}, u32[]{:S(2)}) copy-start(f32[2,128,8,64]{1,3,2,0:T(8,128)} %custom-call.16) | copy-start | bytes 1572868
  144.8 14.4 %all-to-all-start.4 = ((f32[4,2,4,128,64]{3,4,2,1,0:T(8,128)}), f32[4,2,4,128,64]{3,4,2,1,0:T(8,128)S(1)}, u32[]{:S(2)}, u32[]{:S(2)}) async-start(f32[4,2,4,128,64]{3,4,2,1,0:T(8,128)} %copy.150), calls=%async_computation.4 | async-start | bytes 2097152 | tf_op jit(solution)/shard_map/all_to_all | solution.py:43
  150.6 9.1 %copy-start.4 = (f32[128,16]{0,1:T(8,128)S(1)}, f32[128,16]{0,1:T(8,128)}, u32[]{:S(2)}) copy-start(f32[128,16]{0,1:T(8,128)} %copy-done.3) | copy-start | bytes 24580
  150.6 9.1 %copy-start.6 = (f32[128,16]{0,1:T(8,128)S(1)}, f32[128,16]{0,1:T(8,128)}, u32[]{:S(2)}) copy-start(f32[128,16]{0,1:T(8,128)} %copy-done.5) | copy-start | bytes 24580
